TPU v7x, 512 devices: a whole 4x8x8 slice. The times are simulated.
512 devices in a mesh: gx: 8 (over z), gy: 8 (over y), gz: 8 (over x, core).
Axes of the slice: x: 4, y: 8, z: 8, core: 2. Of those that a mesh axis runs over, the one named last changes fastest.
Arguments:
- state: bfloat16 [5, 32, 64, 6144], P(None, 'gx', 'gy', 'gz'), may hold values from -6 to 6
- diffusivity: bfloat16 [32, 64, 6144], P('gx', 'gy', 'gz'), may hold values from 0.25 to 1
- coupling: float32 [5, 5], replicated, may hold values from -3 to 3
- owner: int32 [24576, 1], P(('gx', 'gy', 'gz')), may hold values from 0 to 63; in each aligned block of 48 rows (0 to 47, 48 to 95, ...) at most 2 rows name the same one
- levels: int32 [24576], P(('gx', 'gy', 'gz')), may hold values from 0 to 3
- mark_count: int32 [1], replicated, may hold values from 12288 to 24575
- goal_weight: bfloat16 [65536, 5, 2, 2, 128], P(('gx', 'gy', 'gz')), may hold values from -6 to 6
- reaction: bfloat16 [65536, 5], P(('gx', 'gy', 'gz')), may hold values from 0.5 to 2
Outputs:
- adjoint_field: bfloat16 [5, 32, 64, 6144], P(None, 'gx', 'gy', 'gz')
- share: float32 [24576], P(('gx', 'gy', 'gz'))
- marked: float32 [24576], P(('gx', 'gy', 'gz'))
Inputs may be any that keep to these rules, and one draw needn't show every extreme that they name: owner names a device among the 64 that share the block's gx index (in the order gy, gz); no more than 2 blocks of one device name the same owner.
All inputs are finite; a program needn't handle non-finite values.
Results may differ from a plain program's by a relative error of at most 0.0031.
Values may be sent and summed in bfloat16 or wider, within the bound.
No kernel may reach another device: no remote copies, remote signals or barrier semaphores. Data moves between devices by JAX's collectives and lax.ppermute only.
A program may use at most 64 MiB of HBM per device.

v0:
```python
import jax
import jax.numpy as jnp
from jax import lax
from jax.sharding import PartitionSpec as P

BX = 2
BY = 2
BZ = 128
NBX = 2
NBY = 4
NBZ = 6
SECTIONS = 3


primal_step = 0.05
dual_step = 0.05


def extended_2(cells, sides, width):
    for axis, dim in sides:
        count = lax.axis_size(axis)
        ends = count - 1
        head = lax.slice_in_dim(cells, 0, width, axis=dim)
        tail = lax.slice_in_dim(cells, cells.shape[dim] - width, cells.shape[dim], axis=dim)
        cells = jnp.concatenate(
            [
                lax.ppermute(tail, axis, [(i, (i + 1) % count) for i in range(ends)]),
                cells,
                lax.ppermute(head, axis, [((i + 1) % count, i) for i in range(ends)]),
            ],
            axis=dim,
        )
    return cells


def neighbours(padded):
    center = padded[..., 1:-1, 1:-1, 1:-1]
    summed = padded[..., 2:, 1:-1, 1:-1] + padded[..., :-2, 1:-1, 1:-1]
    summed = summed + padded[..., 1:-1, 2:, 1:-1] + padded[..., 1:-1, :-2, 1:-1]
    summed = summed + padded[..., 1:-1, 1:-1, 2:] + padded[..., 1:-1, 1:-1, :-2]
    return summed - 6.0 * center


def laplace(field):
    widths = [(0, 0)] * (field.ndim - 3) + [(1, 1)] * 3
    return neighbours(jnp.pad(field, widths))


def couple(matrix, field, dim):
    leading = (slice(None),) * dim
    pieces = [field[leading + (col_index,)] for col_index in range(field.shape[dim])]
    combined = []
    for row_index in range(len(pieces)):
        summed = matrix[row_index, 0] * pieces[0]
        for col_index in range(1, len(pieces)):
            summed = summed + matrix[row_index, col_index] * pieces[col_index]
        combined.append(summed)
    return jnp.stack(combined, axis=dim)


def adjoint_sections(diffuse_eff, goal_field, react_rate, coupling):
    transposed = coupling.T
    dual_field = goal_field
    for section_index in range(SECTIONS):
        dual_field = dual_field + dual_step * (
            diffuse_eff[:, None] * laplace(dual_field)
            + couple(transposed, dual_field, 1)
            - react_rate[:, :, None, None, None] * dual_field
            + goal_field
        )
    return (dual_field + 0.125 * laplace(dual_field)).astype(jnp.bfloat16)


def to_blocks(field):
    depth = field.shape[0]
    shaped = field.reshape(depth, NBX, BX, NBY, BY, NBZ, BZ)
    return shaped.transpose(1, 3, 5, 0, 2, 4, 6).reshape(NBX * NBY * NBZ, depth, BX, BY, BZ)


def from_blocks(blocks):
    depth = blocks.shape[1]
    shaped = blocks.reshape(NBX, NBY, NBZ, depth, BX, BY, BZ)
    return shaped.transpose(3, 0, 4, 1, 5, 2, 6).reshape(depth, NBX * BX, NBY * BY, NBZ * BZ)


def shards(state, diffusivity, coupling, owner, levels, mark_count, goal_weight, reaction):
    state_now = state.astype(jnp.float32)
    diffuse = diffusivity.astype(jnp.float32)
    extended = extended_2(state, (("gx", 1), ("gy", 2), ("gz", 3)), 1).astype(jnp.float32)
    section_one = state_now + primal_step * (
        diffuse * neighbours(extended) + couple(coupling, state_now, 0)
    )
    section_cycle = extended_2(
        section_one.astype(jnp.bfloat16), (("gx", 1), ("gy", 2), ("gz", 3)), 1
    ).astype(section_one.dtype)
    curvature = neighbours(section_cycle)
    residual = (
        diffuse * curvature
        + couple(coupling, section_one, 0)
        - (section_one - state_now) / primal_step
    )
    effective = (diffuse * (1.0 + 0.5 * jnp.tanh(section_one[0]))).astype(jnp.bfloat16)
    eff_blocks = to_blocks(effective[None])[:, 0]
    res_blocks = to_blocks(residual)
    across_y = lax.axis_size("gy")
    across_z = lax.axis_size("gz")
    plane = across_y * across_z
    slot_total = goal_weight.shape[0]
    capacity = slot_total // plane
    targets = owner[:, 0]
    order = jnp.arange(targets.shape[0], dtype=jnp.int32)
    same = targets[:, None] == targets[None, :]
    before = order[None, :] < order[:, None]
    rank = jnp.sum((same & before).astype(jnp.int32), axis=1)
    slot_of = targets * capacity + rank
    outgoing = jnp.zeros((slot_total, BX, BY, BZ), jnp.bfloat16).at[slot_of].set(eff_blocks)
    arrived = lax.all_to_all(outgoing, ("gy", "gz"), split_axis=0, concat_axis=0, tiled=True)
    dual_slots = adjoint_sections(
        arrived.astype(jnp.float32),
        goal_weight.astype(jnp.float32),
        reaction.astype(jnp.float32),
        coupling,
    )
    returned = lax.all_to_all(dual_slots, ("gy", "gz"), split_axis=0, concat_axis=0, tiled=True)
    enriched = returned[slot_of]
    weights = jnp.exp2(2.0 * levels.astype(jnp.float32))
    indicator = weights * jnp.sum(
        jnp.abs(res_blocks * enriched.astype(jnp.float32)), axis=(1, 2, 3, 4)
    )
    overall = lax.psum(jnp.sum(indicator), ("gx", "gy", "gz"))
    block_count = owner.shape[0] * lax.axis_size("gx") * across_y * across_z
    share = indicator * block_count / overall
    marked = jnp.minimum(1.0, mark_count[0].astype(jnp.float32) * indicator / overall)
    return (from_blocks(enriched), share, marked)


def solution(mesh):
    placed = (
        P(None, "gx", "gy", "gz"),
        P("gx", "gy", "gz"),
        P(),
        P(("gx", "gy", "gz"), None),
        P(("gx", "gy", "gz")),
        P(),
        P(("gx", "gy", "gz"), None, None, None, None),
        P(("gx", "gy", "gz"), None),
    )
    return jax.shard_map(
        shards,
        mesh=mesh,
        in_specs=placed,
        out_specs=(P(None, "gx", "gy", "gz"), P(("gx", "gy", "gz")), P(("gx", "gy", "gz"))),
        check_vma=False,
    )
```

profile of v0, /device:TPU:1, one launch (start us, length us, event | category | flops | bytes accessed | tf_op | source)
XLA Modules:
  0.0 305.7 jit_solution(6317708288916450243)
XLA Ops:
  1.5 4.8 %collective-permute-start = (bf16[5,1,8,768]{3,2,1,0:T(8,128)(2,1)S(1)}, bf16[5,1,8,768]{3,2,1,0:T(8,128)(2,1)S(1)}, u32[]{:S(2)}, u32[]{:S(2)}) collective-permute-start(bf16[5,1,8,768]{3,2,1,0:T(8,128)(2,1)S(1)} %get-tuple-element.16), channel_id=1, source_target_pairs={{0,64},{64,128},{128,192},{192,256},{256,320},{320,384},{384,448},... | collective-permute-start | bytes 184328 | tf_op jit(solution)/shard_map/ppermute | solution.py:27
  23.1 3.5 %add_dynamic-update-slice_fusion.13 = f32[128,5,2,2,128]{4,3,2,1,0:T(2,128)S(1)} fusion(f32[128,5,2,2,128]{4,3,2,1,0:T(2,128)S(1)} %add_dynamic-update-slice_fusion.14, f32[]{:T(128)} %bitcast.41, f32[]{:T(128)} %bitcast.40, f32[]{:T(128)} %bitcast.39, f32[]{:T(128)} %bitcast.38, f32[]{:T(128)} %bitcast.37, f32[128,5,2,2,128]{4,3,2,1,0:T(2,128)S(1)} %convert_element_type.51), kind=kLoop, calls=%fused_computation.102 | loop fusion | flops 589824 | bytes 1572884
  29.9 3.6 %add_dynamic-update-slice_fusion.11 = f32[128,5,2,2,128]{4,3,2,1,0:T(2,128)S(1)} fusion(f32[128,5,2,2,128]{4,3,2,1,0:T(2,128)S(1)} %add_dynamic-update-slice_fusion.12, f32[]{:T(128)} %bitcast.51, f32[]{:T(128)} %bitcast.50, f32[]{:T(128)} %bitcast.49, f32[]{:T(128)} %bitcast.48, f32[]{:T(128)} %bitcast.47, f32[128,5,2,2,128]{4,3,2,1,0:T(2,128)S(1)} %convert_element_type.51), kind=kLoop, calls=%fused_computation.100 | loop fusion | flops 589824 | bytes 1572884
  33.5 3.6 %add_dynamic-update-slice_fusion.10 = f32[128,5,2,2,128]{4,3,2,1,0:T(2,128)S(1)} fusion(f32[128,5,2,2,128]{4,3,2,1,0:T(2,128)S(1)} %add_dynamic-update-slice_fusion.11, f32[]{:T(128)} %bitcast.56, f32[]{:T(128)} %bitcast.55, f32[]{:T(128)} %bitcast.54, f32[]{:T(128)} %bitcast.53, f32[]{:T(128)} %bitcast.52, f32[128,5,2,2,128]{4,3,2,1,0:T(2,128)S(1)} %convert_element_type.51), kind=kLoop, calls=%fused_computation.99 | loop fusion | flops 589824 | bytes 1572884 | tf_op jit(solution)/shard_map/stack | solution.py:58
  54.7 4.2 %collective-permute-start.4 = (bf16[5,6,10,1]{3,2,1,0:T(8,128)(2,1)S(1)}, bf16[5,6,10,1]{3,2,1,0:T(8,128)(2,1)S(1)}, u32[]{:S(2)}, u32[]{:S(2)}) collective-permute-start(bf16[5,6,10,1]{3,2,1,0:T(8,128)(2,1)S(1)} %get-tuple-element.7), channel_id=1, source_target_pairs={{0,1},{1,2},{2,3},{3,4},{4,5},{5,6},{6,7},{8,9},{9,10},{10,11},{11... | collective-permute-start | bytes 1808 | tf_op jit(solution)/shard_map/ppermute | solution.py:27
  67.0 3.9 %add_dynamic-update-slice_fusion.19 = f32[5,4,8,768]{3,2,1,0:T(8,128)} fusion(f32[5,4,8,768]{3,2,1,0:T(8,128)S(1)} %get-tuple-element.4, f32[]{:T(128)} %bitcast.7, f32[]{:T(128)} %bitcast.6, f32[]{:T(128)} %bitcast.5, f32[]{:T(128)} %bitcast.4, f32[]{:T(128)} %bitcast.3), kind=kLoop, calls=%fused_computation.118 | loop fusion | flops 221183 | bytes 589844
  71.8 5.9 %scatter_fusion = bf16[128,2,2,128]{3,2,1,0:T(2,128)(2,1)} fusion(bf16[128,2,2,128]{3,2,1,0:T(2,128)(2,1)} %broadcast_in_dim.2, s32[48]{0:T(128)S(1)} %fusion.43, bf16[48,2,2,128]{3,2,1,0:T(2,128)(2,1)S(1)} %bitcast.79), kind=kCustom, calls=%fused_computation.1 | custom fusion | bytes 147648 | tf_op jit(solution)/shard_map/scatter | solution.py:116
  77.7 12.2 %all-to-all-start = ((bf16[128,2,2,128]{3,2,1,0:T(2,128)(2,1)}), bf16[128,2,2,128]{3,2,1,0:T(2,128)(2,1)S(1)}, u32[]{:S(2)}, u32[]{:S(2)}) async-start(bf16[128,2,2,128]{3,2,1,0:T(2,128)(2,1)} %scatter_fusion), calls=%async_computation | async-start | bytes 262144 | tf_op jit(solution)/shard_map/all_to_all | solution.py:117
  90.0 4.6 %collective-permute-start.6 = (bf16[5,1,8,768]{3,2,1,0:T(8,128)(2,1)S(1)}, bf16[5,1,8,768]{3,2,1,0:T(8,128)(2,1)S(1)}, u32[]{:S(2)}, u32[]{:S(2)}) collective-permute-start(bf16[5,1,8,768]{3,2,1,0:T(8,128)(2,1)S(1)} %get-tuple-element.13), channel_id=1, source_target_pairs={{0,64},{64,128},{128,192},{192,256},{256,320},{320,384},{384,448},... | collective-permute-start | bytes 184328 | tf_op jit(solution)/shard_map/ppermute | solution.py:27
  96.1 3.9 %add_dynamic-update-slice_fusion.18 = f32[5,4,8,768]{3,2,1,0:T(8,128)} fusion(f32[5,4,8,768]{3,2,1,0:T(8,128)} %add_dynamic-update-slice_fusion.19, f32[5,4,8,768]{3,2,1,0:T(8,128)S(1)} %get-tuple-element.4, f32[]{:T(128)} %bitcast.12, f32[]{:T(128)} %bitcast.11, f32[]{:T(128)} %bitcast.10, f32[]{:T(128)} %bitcast.9, f32[]{:T(128)} %bitcast.8), kind=kLoop, calls=%fused_computation.117 | loop fusion | flops 221184 | bytes 592384
  101.2 5.9 %convert_add_fusion.2 = f32[128,5,2,2,128]{4,3,2,1,0:T(2,128)S(1)} fusion(bf16[128,5,2,2,128]{4,3,2,1,0:T(2,128)(2,1)S(1)} %copy-done, f32[128,5,2,2,128]{4,3,2,1,0:T(2,128)} %copy-done.2, f32[128,5,2,2,128]{4,3,2,1,0:T(2,128)S(1)} %convert_element_type.51, f32[128,5]{1,0:T(8,128)S(1)} %copy.21, f32[128,2,2,128]{3,2,1,0:T(2,128)S(1)} %convert_element_type.57), kind=kLoop, calls=%fused_computation.28 | loop fusion | flops 4915200 | bytes 4852224 | tf_op jit(solution)/shard_map/add | solution.py:65
  110.5 3.5 %add_dynamic-update-slice_fusion.8 = f32[128,5,2,2,128]{4,3,2,1,0:T(2,128)S(1)} fusion(f32[128,5,2,2,128]{4,3,2,1,0:T(2,128)S(1)} %add_dynamic-update-slice_fusion.9, f32[]{:T(128)} %bitcast.41, f32[]{:T(128)} %bitcast.40, f32[]{:T(128)} %bitcast.39, f32[]{:T(128)} %bitcast.38, f32[]{:T(128)} %bitcast.37, f32[128,5,2,2,128]{4,3,2,1,0:T(2,128)S(1)} %convert_add_fusion.2), kind=kLoop, calls=%fused_computation.97 | loop fusion | flops 589824 | bytes 1572884
  117.3 3.6 %add_dynamic-update-slice_fusion.6 = f32[128,5,2,2,128]{4,3,2,1,0:T(2,128)S(1)} fusion(f32[128,5,2,2,128]{4,3,2,1,0:T(2,128)S(1)} %add_dynamic-update-slice_fusion.7, f32[]{:T(128)} %bitcast.51, f32[]{:T(128)} %bitcast.50, f32[]{:T(128)} %bitcast.49, f32[]{:T(128)} %bitcast.48, f32[]{:T(128)} %bitcast.47, f32[128,5,2,2,128]{4,3,2,1,0:T(2,128)S(1)} %convert_add_fusion.2), kind=kLoop, calls=%fused_computation.95 | loop fusion | flops 589824 | bytes 1572884
  120.9 3.6 %add_dynamic-update-slice_fusion.5 = f32[128,5,2,2,128]{4,3,2,1,0:T(2,128)S(1)} fusion(f32[128,5,2,2,128]{4,3,2,1,0:T(2,128)S(1)} %add_dynamic-update-slice_fusion.6, f32[]{:T(128)} %bitcast.56, f32[]{:T(128)} %bitcast.55, f32[]{:T(128)} %bitcast.54, f32[]{:T(128)} %bitcast.53, f32[]{:T(128)} %bitcast.52, f32[128,5,2,2,128]{4,3,2,1,0:T(2,128)S(1)} %convert_add_fusion.2), kind=kLoop, calls=%fused_computation.94 | loop fusion | flops 589824 | bytes 1572884 | tf_op jit(solution)/shard_map/stack | solution.py:58
  124.5 5.5 %fusion.27 = f32[128,5,2,2,128]{4,3,2,1,0:T(2,128)S(1)} fusion(f32[128,5,2,2,128]{4,3,2,1,0:T(2,128)S(1)} %convert_add_fusion.2, bf16[128,5,2,2,128]{4,3,2,1,0:T(2,128)(2,1)S(1)} %copy-done, f32[128,5,2,2,128]{4,3,2,1,0:T(2,128)S(1)} %add_dynamic-update-slice_fusion.5, f32[128,5]{1,0:T(8,128)S(1)} %copy.21, f32[128,2,2,128]{3,2,1,0:T(2,128)S(1)} %convert_element_type.57), kind=kLoop, calls=%fused_computation.59 | loop fusion | flops 4915200 | bytes 4852224 | tf_op jit(solution)/shard_map/add | solution.py:65
  133.5 3.5 %add_dynamic-update-slice_fusion.3 = f32[128,5,2,2,128]{4,3,2,1,0:T(2,128)S(1)} fusion(f32[128,5,2,2,128]{4,3,2,1,0:T(2,128)S(1)} %add_dynamic-update-slice_fusion.4, f32[]{:T(128)} %bitcast.41, f32[]{:T(128)} %bitcast.40, f32[]{:T(128)} %bitcast.39, f32[]{:T(128)} %bitcast.38, f32[]{:T(128)} %bitcast.37, f32[128,5,2,2,128]{4,3,2,1,0:T(2,128)S(1)} %fusion.27), kind=kLoop, calls=%fused_computation.92 | loop fusion | flops 589824 | bytes 1572884
  140.2 3.6 %add_dynamic-update-slice_fusion.1 = f32[128,5,2,2,128]{4,3,2,1,0:T(2,128)S(1)} fusion(f32[128,5,2,2,128]{4,3,2,1,0:T(2,128)S(1)} %add_dynamic-update-slice_fusion.2, f32[]{:T(128)} %bitcast.51, f32[]{:T(128)} %bitcast.50, f32[]{:T(128)} %bitcast.49, f32[]{:T(128)} %bitcast.48, f32[]{:T(128)} %bitcast.47, f32[128,5,2,2,128]{4,3,2,1,0:T(2,128)S(1)} %fusion.27), kind=kLoop, calls=%fused_computation.90 | loop fusion | flops 589824 | bytes 1572884
  143.8 3.6 %add_dynamic-update-slice_fusion = f32[128,5,2,2,128]{4,3,2,1,0:T(2,128)S(1)} fusion(f32[128,5,2,2,128]{4,3,2,1,0:T(2,128)S(1)} %add_dynamic-update-slice_fusion.1, f32[]{:T(128)} %bitcast.56, f32[]{:T(128)} %bitcast.55, f32[]{:T(128)} %bitcast.54, f32[]{:T(128)} %bitcast.53, f32[]{:T(128)} %bitcast.52, f32[128,5,2,2,128]{4,3,2,1,0:T(2,128)S(1)} %fusion.27), kind=kLoop, calls=%fused_computation.89 | loop fusion | flops 589824 | bytes 1572884 | tf_op jit(solution)/shard_map/stack | solution.py:58
  147.4 5.4 %fusion.29 = f32[128,5,2,2,128]{4,3,2,1,0:T(2,128)S(1)} fusion(f32[128,5,2,2,128]{4,3,2,1,0:T(2,128)S(1)} %fusion.27, bf16[128,5,2,2,128]{4,3,2,1,0:T(2,128)(2,1)S(1)} %copy-done, f32[128,5,2,2,128]{4,3,2,1,0:T(2,128)S(1)} %add_dynamic-update-slice_fusion, f32[128,5]{1,0:T(8,128)S(1)} %copy.21, f32[128,2,2,128]{3,2,1,0:T(2,128)S(1)} %convert_element_type.57), kind=kLoop, calls=%fused_computation.61 | loop fusion | flops 4915200 | bytes 4852224 | tf_op jit(solution)/shard_map/add | solution.py:65
  152.8 4.3 %add_convert_fusion = bf16[128,5,2,2,128]{4,3,2,1,0:T(2,128)(2,1)} fusion(f32[128,5,2,2,128]{4,3,2,1,0:T(2,128)S(1)} %fusion.29), kind=kLoop, calls=%fused_computation.62 | loop fusion | flops 3276800 | bytes 1966080 | tf_op jit(solution)/shard_map/convert_element_type | solution.py:71
  157.2 9.6 %all-to-all-start.1 = ((bf16[128,5,2,2,128]{4,3,2,1,0:T(2,128)(2,1)}), bf16[128,5,2,2,128]{4,3,2,1,0:T(2,128)(2,1)}, u32[]{:S(2)}, u32[]{:S(2)}) async-start(bf16[128,5,2,2,128]{4,3,2,1,0:T(2,128)(2,1)} %add_convert_fusion), calls=%async_computation.1 | async-start | bytes 1310720 | tf_op jit(solution)/shard_map/all_to_all | solution.py:124
  181.0 3.7 %collective-permute-done.9 = bf16[5,6,1,768]{3,2,1,0:T(2,128)(2,1)S(1)} collective-permute-done((bf16[5,6,1,768]{3,2,1,0:T(2,128)(2,1)S(1)}, bf16[5,6,1,768]{3,2,1,0:T(2,128)(2,1)S(1)}, u32[]{:S(2)}, u32[]{:S(2)}) %collective-permute-start.9) | collective-permute-done | bytes 46112 | tf_op jit(solution)/shard_map/ppermute | solution.py:29
  184.9 3.7 %collective-permute-start.10 = (bf16[5,6,10,1]{3,2,1,0:T(8,128)(2,1)S(1)}, bf16[5,6,10,1]{3,2,1,0:T(8,128)(2,1)S(1)}, u32[]{:S(2)}, u32[]{:S(2)}) collective-permute-start(bf16[5,6,10,1]{3,2,1,0:T(8,128)(2,1)S(1)} %get-tuple-element.5), channel_id=1, source_target_pairs={{0,1},{1,2},{2,3},{3,4},{4,5},{5,6},{6,7},{8,9},{9,10},{10,11},{11... | collective-permute-start | bytes 1808 | tf_op jit(solution)/shard_map/ppermute | solution.py:27
  200.1 103.3 %psum.7 = f32[]{:T(128)} all-reduce(f32[]{:T(128)} %fusion.44), channel_id=1, replica_groups=mesh['gx'=8,'gy'=8,'gz'=8] {'gx','gy','gz'}, use_global_device_ids=true, to_apply=%region_4.5 | all-reduce | flops 1 | bytes 8 | tf_op jit(solution)/shard_map/psum | solution.py:130
  (85 shorter events, 90.6 us)
Async XLA Ops:
  0.6 18.2 %copy-start.5 = (bf16[128,5]{0,1:T(8,128)(2,1)S(1)}, bf16[128,5]{0,1:T(8,128)(2,1)}, u32[]{:S(2)}) copy-start(bf16[128,5]{0,1:T(8,128)(2,1)} %param.15) | copy-start | bytes 3844
  1.5 35.6 %collective-permute-start = (bf16[5,1,8,768]{3,2,1,0:T(8,128)(2,1)S(1)}, bf16[5,1,8,768]{3,2,1,0:T(8,128)(2,1)S(1)}, u32[]{:S(2)}, u32[]{:S(2)}) collective-permute-start(bf16[5,1,8,768]{3,2,1,0:T(8,128)(2,1)S(1)} %get-tuple-element.16), channel_id=1, source_target_pairs={{0,64},{64,128},{128,192},{192,256},{256,320},{320,384},{384,448},... | collective-permute-start | bytes 184328 | tf_op jit(solution)/shard_map/ppermute | solution.py:27
  6.4 30.9 %collective-permute-start.1 = (bf16[5,1,8,768]{3,2,1,0:T(8,128)(2,1)S(1)}, bf16[5,1,8,768]{3,2,1,0:T(8,128)(2,1)S(1)}, u32[]{:S(2)}, u32[]{:S(2)}) collective-permute-start(bf16[5,1,8,768]{3,2,1,0:T(8,128)(2,1)S(1)} %get-tuple-element.15), channel_id=1, source_target_pairs={{64,0},{128,64},{192,128},{256,192},{320,256},{384,320},{448,384},... | collective-permute-start | bytes 184328 | tf_op jit(solution)/shard_map/ppermute | solution.py:29
  29.9 7.3 %copy-start.1 = (bf16[5,4,8,768]{3,2,1,0:T(8,128)(2,1)S(1)}, bf16[5,4,8,768]{3,2,1,0:T(8,128)(2,1)}, u32[]{:S(2)}) copy-start(bf16[5,4,8,768]{3,2,1,0:T(8,128)(2,1)} %param.8) | copy-start | bytes 737284
  37.1 27.0 %copy-start.2 = (f32[128,5,2,2,128]{4,3,2,1,0:T(2,128)}, f32[128,5,2,2,128]{4,3,2,1,0:T(2,128)S(1)}, u32[]{:S(2)}) copy-start(f32[128,5,2,2,128]{4,3,2,1,0:T(2,128)S(1)} %add_dynamic-update-slice_fusion.10) | copy-start | bytes 3932164
  37.4 17.2 %collective-permute-start.2 = (bf16[5,6,1,768]{3,2,1,0:T(2,128)(2,1)S(1)}, bf16[5,6,1,768]{3,2,1,0:T(2,128)(2,1)S(1)}, u32[]{:S(2)}, u32[]{:S(2)}) collective-permute-start(bf16[5,6,1,768]{3,2,1,0:T(2,128)(2,1)S(1)} %get-tuple-element.11), channel_id=1, source_target_pairs={{0,8},{8,16},{16,24},{24,32},{32,40},{40,48},{48,56},{1,9},{9,17},... | collective-permute-start | bytes 138248 | tf_op jit(solution)/shard_map/ppermute | solution.py:27
  40.6 14.0 %collective-permute-start.3 = (bf16[5,6,1,768]{3,2,1,0:T(2,128)(2,1)S(1)}, bf16[5,6,1,768]{3,2,1,0:T(2,128)(2,1)S(1)}, u32[]{:S(2)}, u32[]{:S(2)}) collective-permute-start(bf16[5,6,1,768]{3,2,1,0:T(2,128)(2,1)S(1)} %get-tuple-element.12), channel_id=1, source_target_pairs={{8,0},{16,8},{24,16},{32,24},{40,32},{48,40},{56,48},{9,1},{17,9},... | collective-permute-start | bytes 138248 | tf_op jit(solution)/shard_map/ppermute | solution.py:29
  54.7 9.4 %collective-permute-start.4 = (bf16[5,6,10,1]{3,2,1,0:T(8,128)(2,1)S(1)}, bf16[5,6,10,1]{3,2,1,0:T(8,128)(2,1)S(1)}, u32[]{:S(2)}, u32[]{:S(2)}) collective-permute-start(bf16[5,6,10,1]{3,2,1,0:T(8,128)(2,1)S(1)} %get-tuple-element.7), channel_id=1, source_target_pairs={{0,1},{1,2},{2,3},{3,4},{4,5},{5,6},{6,7},{8,9},{9,10},{10,11},{11... | collective-permute-start | bytes 1808 | tf_op jit(solution)/shard_map/ppermute | solution.py:27
  59.0 6.2 %collective-permute-start.5 = (bf16[5,6,10,1]{3,2,1,0:T(8,128)(2,1)S(1)}, bf16[5,6,10,1]{3,2,1,0:T(8,128)(2,1)S(1)}, u32[]{:S(2)}, u32[]{:S(2)}) collective-permute-start(bf16[5,6,10,1]{3,2,1,0:T(8,128)(2,1)S(1)} %get-tuple-element.8), channel_id=1, source_target_pairs={{1,0},{2,1},{3,2},{4,3},{5,4},{6,5},{7,6},{9,8},{10,9},{11,10},{12... | collective-permute-start | bytes 1808 | tf_op jit(solution)/shard_map/ppermute | solution.py:29
  66.1 4.8 %copy-start.4 = (bf16[4,8,768]{2,1,0:T(8,128)(2,1)S(1)}, bf16[4,8,768]{2,1,0:T(8,128)(2,1)}, u32[]{:S(2)}) copy-start(bf16[4,8,768]{2,1,0:T(8,128)(2,1)} %param.9) | copy-start | bytes 147460
  67.0 34.1 %copy-start = (bf16[128,5,2,2,128]{4,3,2,1,0:T(2,128)(2,1)S(1)}, bf16[128,5,2,2,128]{4,3,2,1,0:T(2,128)(2,1)}, u32[]{:S(2)}) copy-start(bf16[128,5,2,2,128]{4,3,2,1,0:T(2,128)(2,1)} %param.14) | copy-start | bytes 1966084
  77.7 23.3 %all-to-all-start = ((bf16[128,2,2,128]{3,2,1,0:T(2,128)(2,1)}), bf16[128,2,2,128]{3,2,1,0:T(2,128)(2,1)S(1)}, u32[]{:S(2)}, u32[]{:S(2)}) async-start(bf16[128,2,2,128]{3,2,1,0:T(2,128)(2,1)} %scatter_fusion), calls=%async_computation | async-start | bytes 262144 | tf_op jit(solution)/shard_map/all_to_all | solution.py:117
  90.0 79.9 %collective-permute-start.6 = (bf16[5,1,8,768]{3,2,1,0:T(8,128)(2,1)S(1)}, bf16[5,1,8,768]{3,2,1,0:T(8,128)(2,1)S(1)}, u32[]{:S(2)}, u32[]{:S(2)}) collective-permute-start(bf16[5,1,8,768]{3,2,1,0:T(8,128)(2,1)S(1)} %get-tuple-element.13), channel_id=1, source_target_pairs={{0,64},{64,128},{128,192},{192,256},{256,320},{320,384},{384,448},... | collective-permute-start | bytes 184328 | tf_op jit(solution)/shard_map/ppermute | solution.py:27
  94.6 75.3 %collective-permute-start.7 = (bf16[5,1,8,768]{3,2,1,0:T(8,128)(2,1)S(1)}, bf16[5,1,8,768]{3,2,1,0:T(8,128)(2,1)S(1)}, u32[]{:S(2)}, u32[]{:S(2)}) collective-permute-start(bf16[5,1,8,768]{3,2,1,0:T(8,128)(2,1)S(1)} %get-tuple-element.14), channel_id=1, source_target_pairs={{64,0},{128,64},{192,128},{256,192},{320,256},{384,320},{448,384},... | collective-permute-start | bytes 184328 | tf_op jit(solution)/shard_map/ppermute | solution.py:29
  152.8 14.0 %copy-start.3 = (f32[5,4,8,768]{3,2,1,0:T(8,128)S(1)}, f32[5,4,8,768]{3,2,1,0:T(8,128)}, u32[]{:S(2)}) copy-start(f32[5,4,8,768]{3,2,1,0:T(8,128)} %add_dynamic-update-slice_fusion.18) | copy-start | bytes 1474564
  157.2 39.6 %all-to-all-start.1 = ((bf16[128,5,2,2,128]{4,3,2,1,0:T(2,128)(2,1)}), bf16[128,5,2,2,128]{4,3,2,1,0:T(2,128)(2,1)}, u32[]{:S(2)}, u32[]{:S(2)}) async-start(bf16[128,5,2,2,128]{4,3,2,1,0:T(2,128)(2,1)} %add_convert_fusion), calls=%async_computation.1 | async-start | bytes 1310720 | tf_op jit(solution)/shard_map/all_to_all | solution.py:124
  170.0 11.0 %collective-permute-start.8 = (bf16[5,6,1,768]{3,2,1,0:T(2,128)(2,1)S(1)}, bf16[5,6,1,768]{3,2,1,0:T(2,128)(2,1)S(1)}, u32[]{:S(2)}, u32[]{:S(2)}) collective-permute-start(bf16[5,6,1,768]{3,2,1,0:T(2,128)(2,1)S(1)} %get-tuple-element.9), channel_id=1, source_target_pairs={{0,8},{8,16},{16,24},{24,32},{32,40},{40,48},{48,56},{1,9},{9,17},... | collective-permute-start | bytes 138248 | tf_op jit(solution)/shard_map/ppermute | solution.py:27
  173.3 11.4 %collective-permute-start.9 = (bf16[5,6,1,768]{3,2,1,0:T(2,128)(2,1)S(1)}, bf16[5,6,1,768]{3,2,1,0:T(2,128)(2,1)S(1)}, u32[]{:S(2)}, u32[]{:S(2)}) collective-permute-start(bf16[5,6,1,768]{3,2,1,0:T(2,128)(2,1)S(1)} %get-tuple-element.10), channel_id=1, source_target_pairs={{8,0},{16,8},{24,16},{32,24},{40,32},{48,40},{56,48},{9,1},{17,9},... | collective-permute-start | bytes 138248 | tf_op jit(solution)/shard_map/ppermute | solution.py:29
  184.9 9.1 %collective-permute-start.10 = (bf16[5,6,10,1]{3,2,1,0:T(8,128)(2,1)S(1)}, bf16[5,6,10,1]{3,2,1,0:T(8,128)(2,1)S(1)}, u32[]{:S(2)}, u32[]{:S(2)}) collective-permute-start(bf16[5,6,10,1]{3,2,1,0:T(8,128)(2,1)S(1)} %get-tuple-element.5), channel_id=1, source_target_pairs={{0,1},{1,2},{2,3},{3,4},{4,5},{5,6},{6,7},{8,9},{9,10},{10,11},{11... | collective-permute-start | bytes 1808 | tf_op jit(solution)/shard_map/ppermute | solution.py:27
  188.7 6.2 %collective-permute-start.11 = (bf16[5,6,10,1]{3,2,1,0:T(8,128)(2,1)S(1)}, bf16[5,6,10,1]{3,2,1,0:T(8,128)(2,1)S(1)}, u32[]{:S(2)}, u32[]{:S(2)}) collective-permute-start(bf16[5,6,10,1]{3,2,1,0:T(8,128)(2,1)S(1)} %get-tuple-element.6), channel_id=1, source_target_pairs={{1,0},{2,1},{3,2},{4,3},{5,4},{6,5},{7,6},{9,8},{10,9},{11,10},{12... | collective-permute-start | bytes 1808 | tf_op jit(solution)/shard_map/ppermute | solution.py:29
  196.7 2.8 copy-start.6
where the time goes:
time: 308 us; the launch traced here: 306 us
  other arithmetic  117 us (38%)
  blocking collectives  103 us (33%)
  starting transfers between devices  55.2 us (18%)
  local copies, waits for them, and re-layouts  18.6 us (6%)
  waiting for transfers between devices  9.94 us (3%)
    psum x1, blocking collectives, shards(): overall = lax.psum(jnp.sum(indicator), ('gx', 'gy', 'gz'))  103 us
    unnamed x21, other arithmetic  68.1 us
    ppermute x6, starting transfers between devices, extended_2(): lax.ppermute(tail, axis, [(i, (i + 1) % count) for i in range(ends)])  23.9 us
    another operation x5, other arithmetic, couple(): return jnp.stack(combined, axis=dim)  17.2 us
    add x3, other arithmetic, adjoint_sections(): dual_field + dual_step * (diffuse_eff[:, None] * laplace(dual_field) + co...  16.8 us
    all_to_all x1, starting transfers between devices, shards(): lax.all_to_all(outgoing, ('gy', 'gz'), split_axis=0, concat_axis=0, tiled...  12.2 us
    all_to_all x1, starting transfers between devices, shards(): lax.all_to_all(dual_slots, ('gy', 'gz'), split_axis=0, concat_axis=0, til...  9.63 us
    ppermute x6, starting transfers between devices, extended_2(): lax.ppermute(head, axis, [((i + 1) % count, i) for i in range(ends)])  9.41 us
  transfers between devices with their start and end apart: 14, of which 5 were waited for; matrix products, arithmetic and copies ran while one was open for 38% of the time, Pallas kernels for 0%

commit v1 on v0

v1 whole, which is shorter than its diff:
```python
import jax
import jax.numpy as jnp
from jax import lax
from jax.sharding import PartitionSpec as P

BX = 2
BY = 2
BZ = 128
NBX = 2
NBY = 4
NBZ = 6
SECTIONS = 3
FIELDS = 5


primal_step = 0.05
dual_step = 0.05

REDUCE = "tree"


def faces(cells, sides):
    out = []
    for axis, dim in sides:
        count = lax.axis_size(axis)
        ends = count - 1
        head = lax.slice_in_dim(cells, 0, 1, axis=dim)
        tail = lax.slice_in_dim(cells, cells.shape[dim] - 1, cells.shape[dim], axis=dim)
        below = lax.ppermute(tail, axis, [(i, i + 1) for i in range(ends)])
        above = lax.ppermute(head, axis, [(i + 1, i) for i in range(ends)])
        out.append((below, above))
    return out


def shifted(v, dim, below, above):
    n = v.shape[dim]
    minus = jnp.concatenate([below, lax.slice_in_dim(v, 0, n - 1, axis=dim)], axis=dim)
    plus = jnp.concatenate([lax.slice_in_dim(v, 1, n, axis=dim), above], axis=dim)
    return minus, plus


def laplace_halo(v, halos, dims):
    total = None
    for (below, above), dim in zip(halos, dims):
        minus, plus = shifted(v, dim, below.astype(v.dtype), above.astype(v.dtype))
        pair = minus + plus
        total = pair if total is None else total + pair
    return total - 6.0 * v


def swap_pairs(v, dim):
    shape = v.shape
    split = shape[:dim] + (shape[dim] // 2, 2) + shape[dim + 1:]
    return jnp.flip(v.reshape(split), axis=dim + 1).reshape(shape)


def block_shift(v, dim, width):
    n = v.shape[dim]
    zero = jnp.zeros_like(lax.slice_in_dim(v, 0, 1, axis=dim))
    minus = jnp.concatenate([zero, lax.slice_in_dim(v, 0, n - 1, axis=dim)], axis=dim)
    plus = jnp.concatenate([lax.slice_in_dim(v, 1, n, axis=dim), zero], axis=dim)
    pos = lax.broadcasted_iota(jnp.int32, v.shape, dim) % width
    minus = jnp.where(pos == 0, 0.0, minus)
    plus = jnp.where(pos == width - 1, 0.0, plus)
    return minus + plus


def laplace_blocks(v):
    return swap_pairs(v, 1) + swap_pairs(v, 2) + block_shift(v, 3, BZ) - 6.0 * v


def couple(matrix, v):
    return jnp.sum(matrix[:, :, None, None, None] * v[None], axis=1)


def global_sum(x):
    if REDUCE == "psum":
        return lax.psum(x, ("gx", "gy", "gz"))
    if REDUCE == "gather":
        every = lax.all_gather(x.reshape(1), ("gx", "gy", "gz"), tiled=True)
        return jnp.sum(every)
    for axis in ("gz", "gy", "gx"):
        n = lax.axis_size(axis)
        step = 1
        while step < n:
            x = x + lax.ppermute(x, axis, [(i, (i + step) % n) for i in range(n)])
            step *= 2
    return x


def to_cells(blocks):
    depth = blocks.shape[1]
    shaped = blocks.reshape(NBX, NBY, NBZ, depth, BX, BY, BZ)
    return shaped.transpose(3, 0, 4, 1, 5, 2, 6).reshape(depth, NBX * BX, NBY * BY, NBZ * BZ)


def per_block_cells(values):
    depth = values.shape[1]
    shaped = values.reshape(NBX, NBY, NBZ, depth).transpose(3, 0, 1, 2)
    shaped = jnp.broadcast_to(
        shaped[:, :, None, :, None, :, None], (depth, NBX, BX, NBY, BY, NBZ, BZ)
    )
    return shaped.reshape(depth, NBX * BX, NBY * BY, NBZ * BZ)


def block_sums(cells):
    depth = cells.shape[0]
    shaped = cells.reshape(depth, NBX, BX, NBY, BY, NBZ, BZ)
    return jnp.sum(shaped, axis=(0, 2, 4, 6)).reshape(NBX * NBY * NBZ)


def shards(state, diffusivity, coupling, owner, levels, mark_count, goal_weight, reaction):
    sides = (("gx", 1), ("gy", 2), ("gz", 3))
    dims = (1, 2, 3)

    arrived_goal = lax.all_to_all(goal_weight, ("gy", "gz"), 0, 0, tiled=True)
    arrived_react = lax.all_to_all(reaction, ("gy", "gz"), 0, 0, tiled=True)

    state_now = state.astype(jnp.float32)
    diffuse = diffusivity.astype(jnp.float32)[None]
    state_halo = faces(state, sides)
    section_one = state_now + primal_step * (
        diffuse * laplace_halo(state_now, state_halo, dims) + couple(coupling, state_now)
    )
    section_halo = faces(section_one.astype(jnp.bfloat16), sides)
    residual = (
        diffuse * laplace_halo(section_one, section_halo, dims)
        + couple(coupling, section_one)
        - (section_one - state_now) / primal_step
    )
    effective = (diffuse[0] * (1.0 + 0.5 * jnp.tanh(section_one[0]))).astype(jnp.bfloat16)

    targets = owner[:, 0]
    order = jnp.arange(targets.shape[0], dtype=jnp.int32)
    same = targets[:, None] == targets[None, :]
    before = order[None, :] < order[:, None]
    rank = jnp.sum((same & before).astype(jnp.int32), axis=1)
    capacity = goal_weight.shape[0] // (lax.axis_size("gy") * lax.axis_size("gz"))
    slot_of = targets * capacity + rank

    goal = to_cells(arrived_goal[slot_of]).astype(jnp.float32)
    react = per_block_cells(arrived_react[slot_of]).astype(jnp.float32)
    eff = effective.astype(jnp.float32)[None]
    transposed = coupling.T
    dual = goal
    for _ in range(SECTIONS):
        dual = dual + dual_step * (
            eff * laplace_blocks(dual) + couple(transposed, dual) - react * dual + goal
        )
    enriched = (dual + 0.125 * laplace_blocks(dual)).astype(jnp.bfloat16)

    weights = jnp.exp2(2.0 * levels.astype(jnp.float32))
    indicator = weights * block_sums(jnp.abs(residual * enriched.astype(jnp.float32)))
    overall = global_sum(jnp.sum(indicator))
    block_count = owner.shape[0] * lax.axis_size("gx") * lax.axis_size("gy") * lax.axis_size("gz")
    share = indicator * block_count / overall
    marked = jnp.minimum(1.0, mark_count[0].astype(jnp.float32) * indicator / overall)
    return (enriched, share, marked)


def solution(mesh):
    placed = (
        P(None, "gx", "gy", "gz"),
        P("gx", "gy", "gz"),
        P(),
        P(("gx", "gy", "gz"), None),
        P(("gx", "gy", "gz")),
        P(),
        P(("gx", "gy", "gz"), None, None, None, None),
        P(("gx", "gy", "gz"), None),
    )
    return jax.shard_map(
        shards,
        mesh=mesh,
        in_specs=placed,
        out_specs=(P(None, "gx", "gy", "gz"), P(("gx", "gy", "gz")), P(("gx", "gy", "gz"))),
        check_vma=False,
    )
```

time: 308 us -> 202 us (0.66)
  the two profiles are of different devices: /device:TPU:1 before, /device:TPU:32 now
where the time goes in v1:
time: 202 us; the launch traced here: 201 us
  starting transfers between devices  96.1 us (48%)
  local copies, waits for them, and re-layouts  43 us (21%)
  waiting for transfers between devices  33.6 us (17%)
  other arithmetic  20.5 us (10%)
  between operations  7.65 us (4%)
    ppermute x9, starting transfers between devices, global_sum(): x = x + lax.ppermute(x, axis, [(i, (i + step) % n) for i in range(n)])  40.2 us
    ppermute x9, waiting for transfers between devices, global_sum(): x = x + lax.ppermute(x, axis, [(i, (i + step) % n) for i in range(n)])  31.1 us
    ppermute x6, starting transfers between devices, faces(): below = lax.ppermute(tail, axis, [(i, i + 1) for i in range(ends)])  17.3 us
    ppermute x6, starting transfers between devices, faces(): above = lax.ppermute(head, axis, [(i + 1, i) for i in range(ends)])  14.3 us
    rev x8, local copies, waits for them, and re-layouts, swap_pairs(): return jnp.flip(v.reshape(split), axis=dim + 1).reshape(shape)  12.7 us
    all_to_all x1, starting transfers between devices, shards(): arrived_goal = lax.all_to_all(goal_weight, ('gy', 'gz'), 0, 0, tiled=True)  12.4 us
    all_to_all x1, starting transfers between devices, shards(): arrived_react = lax.all_to_all(reaction, ('gy', 'gz'), 0, 0, tiled=True)  11.9 us
    reshape x7, local copies, waits for them, and re-layouts, swap_pairs(): return jnp.flip(v.reshape(split), axis=dim + 1).reshape(shape)  7.5 us
  transfers between devices with their start and end apart: 23, of which 11 were waited for; matrix products, arithmetic and copies ran while one was open for 9% of the time, Pallas kernels for 0%

profile of v1, /device:TPU:32, one launch (start us, length us, event | category | flops | bytes accessed | tf_op | source)
XLA Modules:
  0.0 200.9 jit_solution(13359957103080827768)
XLA Ops:
  1.6 4.3 %collective-permute-start = (bf16[5,1,8,768]{3,2,1,0:T(8,128)(2,1)S(1)}, bf16[5,1,8,768]{3,2,1,0:T(8,128)(2,1)S(1)}, u32[]{:S(2)}, u32[]{:S(2)}) collective-permute-start(bf16[5,1,8,768]{3,2,1,0:T(8,128)(2,1)S(1)} %get-tuple-element.27), channel_id=1, source_target_pairs={{0,64},{64,128},{128,192},{192,256},{256,320},{320,384},{384,448},... | collective-permute-start | bytes 184328 | tf_op jit(solution)/shard_map/ppermute | solution.py:29
  11.5 4.5 %collective-permute-start.3 = (bf16[5,4,1,768]{3,2,1,0:T(2,128)(2,1)S(1)}, bf16[5,4,1,768]{3,2,1,0:T(2,128)(2,1)S(1)}, u32[]{:S(2)}, u32[]{:S(2)}) collective-permute-start(bf16[5,4,1,768]{3,2,1,0:T(2,128)(2,1)S(1)} %get-tuple-element.32), channel_id=1, source_target_pairs={{8,0},{16,8},{24,16},{32,24},{40,32},{48,40},{56,48},{9,1},{17,9},... | collective-permute-start | bytes 92168 | tf_op jit(solution)/shard_map/ppermute | solution.py:30
  18.9 11.9 %all-to-all-start.1 = ((bf16[64,2,5]{2,1,0:T(2,128)(2,1)}), bf16[64,2,5]{2,1,0:T(2,128)(2,1)S(1)}, u32[]{:S(2)}, u32[]{:S(2)}) async-start(bf16[64,2,5]{2,1,0:T(2,128)(2,1)} %bitcast.8), calls=%async_computation.1 | async-start | bytes 65536 | tf_op jit(solution)/shard_map/all_to_all | solution.py:117
  38.3 12.4 %all-to-all-start = ((bf16[128,5,2,2,128]{4,3,2,1,0:T(2,128)(2,1)}), bf16[128,5,2,2,128]{4,3,2,1,0:T(2,128)(2,1)}, u32[]{:S(2)}, u32[]{:S(2)}) async-start(bf16[128,5,2,2,128]{4,3,2,1,0:T(2,128)(2,1)} %param.14), calls=%async_computation | async-start | bytes 1310720 | tf_op jit(solution)/shard_map/all_to_all | solution.py:116
  54.6 4.9 %collective-permute-start.6 = (bf16[5,1,8,768]{3,2,1,0:T(8,128)(2,1)S(1)}, bf16[5,1,8,768]{3,2,1,0:T(8,128)(2,1)S(1)}, u32[]{:S(2)}, u32[]{:S(2)}) collective-permute-start(bf16[5,1,8,768]{3,2,1,0:T(8,128)(2,1)S(1)} %get-tuple-element.26), channel_id=1, source_target_pairs={{0,64},{64,128},{128,192},{192,256},{256,320},{320,384},{384,448},... | collective-permute-start | bytes 184328 | tf_op jit(solution)/shard_map/ppermute | solution.py:29
  68.4 4.5 %collective-permute-start.9 = (bf16[5,4,1,768]{3,2,1,0:T(2,128)(2,1)S(1)}, bf16[5,4,1,768]{3,2,1,0:T(2,128)(2,1)S(1)}, u32[]{:S(2)}, u32[]{:S(2)}) collective-permute-start(bf16[5,4,1,768]{3,2,1,0:T(2,128)(2,1)S(1)} %get-tuple-element.23), channel_id=1, source_target_pairs={{8,0},{16,8},{24,16},{32,24},{40,32},{48,40},{56,48},{9,1},{17,9},... | collective-permute-start | bytes 92168 | tf_op jit(solution)/shard_map/ppermute | solution.py:30
  86.6 2.7 %rev.27 = f32[5,4,4,2,768]{4,3,2,1,0:T(2,128)} reverse(f32[5,4,4,2,768]{4,3,2,1,0:T(2,128)S(1)} %copy-done.2), dimensions={3} | reverse | bytes 983040 | tf_op jit(solution)/shard_map/jit(_flip)/rev | solution.py:54
  97.4 3.4 %rev.29 = f32[5,4,4,2,768]{4,3,2,1,0:T(2,128)S(1)} reverse(f32[5,4,4,2,768]{4,3,2,1,0:T(2,128)} %reshape.104), dimensions={3} | reverse | bytes 983040 | tf_op jit(solution)/shard_map/jit(_flip)/rev | solution.py:54
  107.2 2.7 %rev.31 = f32[5,4,4,2,768]{4,3,2,1,0:T(2,128)} reverse(f32[5,4,4,2,768]{4,3,2,1,0:T(2,128)S(1)} %reshape.108), dimensions={3} | reverse | bytes 983040 | tf_op jit(solution)/shard_map/jit(_flip)/rev | solution.py:54
  119.0 3.4 %fusion.56 = (f32[4,8,768]{2,1,0:T(8,128)S(1)}, bf16[5,4,8,768]{3,2,1,0:T(8,128)(2,1)}) fusion(f32[5,4,8,768]{3,2,1,0:T(8,128)S(1)} %multiply_reduce_fusion, f32[5,3,8,768]{3,2,1,0:T(8,128)} %get-tuple-element.20, f32[5,1,8,768]{3,2,1,0:T(8,128)S(1)} %copy-done.5, f32[5,1,8,768]{3,2,1,0:T(8,128)} %convert_element_type.141, ...), kind=kLoop, calls=%fused_computation.70 | loop fusion | flops 4399104 | bytes 7083520 | tf_op jit(solution)/shard_map/reduce_sum | solution.py:109
  123.2 2.7 %collective-permute-start.12 = (f32[]{:T(128)}, f32[]{:T(128)}, u32[]{:S(2)}, u32[]{:S(2)}) collective-permute-start(f32[]{:T(128)} %fusion.69), channel_id=1, source_target_pairs={{0,1},{1,2},{2,3},{3,4},{4,5},{5,6},{6,7},{7,0},{8,9},{9,10},{10,1... | collective-permute-start | bytes 20 | tf_op jit(solution)/shard_map/ppermute | solution.py:86
  128.9 4.6 %collective-permute-start.13 = (f32[]{:T(128)}, f32[]{:T(128)}, u32[]{:S(2)}, u32[]{:S(2)}) collective-permute-start(f32[]{:T(128)} %add.234), channel_id=1, source_target_pairs={{0,2},{1,3},{2,4},{3,5},{4,6},{5,7},{6,0},{7,1},{8,10},{9,11},{10,... | collective-permute-start | bytes 20 | tf_op jit(solution)/shard_map/ppermute | solution.py:86
  136.2 4.9 %collective-permute-start.14 = (f32[]{:T(128)}, f32[]{:T(128)}, u32[]{:S(2)}, u32[]{:S(2)}) collective-permute-start(f32[]{:T(128)} %add.235), channel_id=1, source_target_pairs={{0,4},{1,5},{2,6},{3,7},{4,0},{5,1},{6,2},{7,3},{8,12},{9,13},{10,... | collective-permute-start | bytes 20 | tf_op jit(solution)/shard_map/ppermute | solution.py:86
  143.8 3.2 %collective-permute-start.15 = (f32[]{:T(128)}, f32[]{:T(128)}, u32[]{:S(2)}, u32[]{:S(2)}) collective-permute-start(f32[]{:T(128)} %add.236), channel_id=1, source_target_pairs={{0,8},{8,16},{16,24},{24,32},{32,40},{40,48},{48,56},{56,0},{1,9},... | collective-permute-start | bytes 20 | tf_op jit(solution)/shard_map/ppermute | solution.py:86
  147.0 3.5 %collective-permute-done.15 = f32[]{:T(128)} collective-permute-done((f32[]{:T(128)}, f32[]{:T(128)}, u32[]{:S(2)}, u32[]{:S(2)}) %collective-permute-start.15) | collective-permute-done | bytes 36 | tf_op jit(solution)/shard_map/ppermute | solution.py:86
  151.1 3.2 %collective-permute-start.16 = (f32[]{:T(128)}, f32[]{:T(128)}, u32[]{:S(2)}, u32[]{:S(2)}) collective-permute-start(f32[]{:T(128)} %add.237), channel_id=1, source_target_pairs={{0,16},{8,24},{16,32},{24,40},{32,48},{40,56},{48,0},{56,8},{1,17}... | collective-permute-start | bytes 20 | tf_op jit(solution)/shard_map/ppermute | solution.py:86
  154.3 4.4 %collective-permute-done.16 = f32[]{:T(128)} collective-permute-done((f32[]{:T(128)}, f32[]{:T(128)}, u32[]{:S(2)}, u32[]{:S(2)}) %collective-permute-start.16) | collective-permute-done | bytes 36 | tf_op jit(solution)/shard_map/ppermute | solution.py:86
  159.4 3.2 %collective-permute-start.17 = (f32[]{:T(128)}, f32[]{:T(128)}, u32[]{:S(2)}, u32[]{:S(2)}) collective-permute-start(f32[]{:T(128)} %add.238), channel_id=1, source_target_pairs={{0,32},{8,40},{16,48},{24,56},{32,0},{40,8},{48,16},{56,24},{1,33}... | collective-permute-start | bytes 20 | tf_op jit(solution)/shard_map/ppermute | solution.py:86
  162.6 6.2 %collective-permute-done.17 = f32[]{:T(128)} collective-permute-done((f32[]{:T(128)}, f32[]{:T(128)}, u32[]{:S(2)}, u32[]{:S(2)}) %collective-permute-start.17) | collective-permute-done | bytes 36 | tf_op jit(solution)/shard_map/ppermute | solution.py:86
  169.4 6.2 %collective-permute-start.18 = (f32[]{:T(128)}, f32[]{:T(128)}, u32[]{:S(2)}, u32[]{:S(2)}) collective-permute-start(f32[]{:T(128)} %add.239), channel_id=1, source_target_pairs={{0,64},{64,128},{128,192},{192,256},{256,320},{320,384},{384,448},... | collective-permute-start | bytes 20 | tf_op jit(solution)/shard_map/ppermute | solution.py:86
  175.6 6.0 %collective-permute-done.18 = f32[]{:T(128)} collective-permute-done((f32[]{:T(128)}, f32[]{:T(128)}, u32[]{:S(2)}, u32[]{:S(2)}) %collective-permute-start.18) | collective-permute-done | bytes 36 | tf_op jit(solution)/shard_map/ppermute | solution.py:86
  182.1 3.4 %collective-permute-start.19 = (f32[]{:T(128)}, f32[]{:T(128)}, u32[]{:S(2)}, u32[]{:S(2)}) collective-permute-start(f32[]{:T(128)} %add.240), channel_id=1, source_target_pairs={{0,128},{64,192},{128,256},{192,320},{256,384},{320,448},{384,0},{... | collective-permute-start | bytes 20 | tf_op jit(solution)/shard_map/ppermute | solution.py:86
  185.6 4.2 %collective-permute-done.19 = f32[]{:T(128)} collective-permute-done((f32[]{:T(128)}, f32[]{:T(128)}, u32[]{:S(2)}, u32[]{:S(2)}) %collective-permute-start.19) | collective-permute-done | bytes 36 | tf_op jit(solution)/shard_map/ppermute | solution.py:86
  190.4 8.8 %collective-permute-start.20 = (f32[]{:T(128)}, f32[]{:T(128)}, u32[]{:S(2)}, u32[]{:S(2)}) collective-permute-start(f32[]{:T(128)} %add.241), channel_id=1, source_target_pairs={{0,256},{64,320},{128,384},{192,448},{256,0},{320,64},{384,128},{4... | collective-permute-start | bytes 20 | tf_op jit(solution)/shard_map/ppermute | solution.py:86
  (138 shorter events, 74.0 us)
Async XLA Ops:
  1.6 50.4 %collective-permute-start = (bf16[5,1,8,768]{3,2,1,0:T(8,128)(2,1)S(1)}, bf16[5,1,8,768]{3,2,1,0:T(8,128)(2,1)S(1)}, u32[]{:S(2)}, u32[]{:S(2)}) collective-permute-start(bf16[5,1,8,768]{3,2,1,0:T(8,128)(2,1)S(1)} %get-tuple-element.27), channel_id=1, source_target_pairs={{0,64},{64,128},{128,192},{192,256},{256,320},{320,384},{384,448},... | collective-permute-start | bytes 184328 | tf_op jit(solution)/shard_map/ppermute | solution.py:29
  5.9 46.1 %collective-permute-start.1 = (bf16[5,1,8,768]{3,2,1,0:T(8,128)(2,1)S(1)}, bf16[5,1,8,768]{3,2,1,0:T(8,128)(2,1)S(1)}, u32[]{:S(2)}, u32[]{:S(2)}) collective-permute-start(bf16[5,1,8,768]{3,2,1,0:T(8,128)(2,1)S(1)} %get-tuple-element.28), channel_id=1, source_target_pairs={{64,0},{128,64},{192,128},{256,192},{320,256},{384,320},{448,384},... | collective-permute-start | bytes 184328 | tf_op jit(solution)/shard_map/ppermute | solution.py:30
  8.9 42.9 %collective-permute-start.2 = (bf16[5,4,1,768]{3,2,1,0:T(2,128)(2,1)}, bf16[5,4,1,768]{3,2,1,0:T(2,128)(2,1)S(1)}, u32[]{:S(2)}, u32[]{:S(2)}) collective-permute-start(bf16[5,4,1,768]{3,2,1,0:T(2,128)(2,1)} %get-tuple-element.31), channel_id=1, source_target_pairs={{0,8},{8,16},{16,24},{24,32},{32,40},{40,48},{48,56},{1,9},{9,17},... | collective-permute-start | bytes 92168 | tf_op jit(solution)/shard_map/ppermute | solution.py:29
  11.5 40.4 %collective-permute-start.3 = (bf16[5,4,1,768]{3,2,1,0:T(2,128)(2,1)S(1)}, bf16[5,4,1,768]{3,2,1,0:T(2,128)(2,1)S(1)}, u32[]{:S(2)}, u32[]{:S(2)}) collective-permute-start(bf16[5,4,1,768]{3,2,1,0:T(2,128)(2,1)S(1)} %get-tuple-element.32), channel_id=1, source_target_pairs={{8,0},{16,8},{24,16},{32,24},{40,32},{48,40},{56,48},{9,1},{17,9},... | collective-permute-start | bytes 92168 | tf_op jit(solution)/shard_map/ppermute | solution.py:30
  16.9 17.7 %collective-permute-start.4 = (bf16[5,4,8,1]{3,2,1,0:T(8,128)(2,1)S(1)}, bf16[5,4,8,1]{3,2,1,0:T(8,128)(2,1)S(1)}, u32[]{:S(2)}, u32[]{:S(2)}) collective-permute-start(bf16[5,4,8,1]{3,2,1,0:T(8,128)(2,1)S(1)} %get-tuple-element.35), channel_id=1, source_target_pairs={{0,1},{1,2},{2,3},{3,4},{4,5},{5,6},{6,7},{8,9},{9,10},{10,11},{11... | collective-permute-start | bytes 968 | tf_op jit(solution)/shard_map/ppermute | solution.py:29
  18.9 19.4 %all-to-all-start.1 = ((bf16[64,2,5]{2,1,0:T(2,128)(2,1)}), bf16[64,2,5]{2,1,0:T(2,128)(2,1)S(1)}, u32[]{:S(2)}, u32[]{:S(2)}) async-start(bf16[64,2,5]{2,1,0:T(2,128)(2,1)} %bitcast.8), calls=%async_computation.1 | async-start | bytes 65536 | tf_op jit(solution)/shard_map/all_to_all | solution.py:117
  32.9 80.0 %copy-start.9 = (s32[768]{0:T(1024)}, s32[768]{0:T(1024)S(1)}, u32[]{:S(2)}) copy-start(s32[768]{0:T(1024)S(1)} %get-tuple-element.41) | copy-start | bytes 9220
  34.5 3.1 %collective-permute-start.5 = (bf16[5,4,8,1]{3,2,1,0:T(8,128)(2,1)S(1)}, bf16[5,4,8,1]{3,2,1,0:T(8,128)(2,1)S(1)}, u32[]{:S(2)}, u32[]{:S(2)}) collective-permute-start(bf16[5,4,8,1]{3,2,1,0:T(8,128)(2,1)S(1)} %get-tuple-element.36), channel_id=1, source_target_pairs={{1,0},{2,1},{3,2},{4,3},{5,4},{6,5},{7,6},{9,8},{10,9},{11,10},{12... | collective-permute-start | bytes 968 | tf_op jit(solution)/shard_map/ppermute | solution.py:30
  38.3 41.7 %all-to-all-start = ((bf16[128,5,2,2,128]{4,3,2,1,0:T(2,128)(2,1)}), bf16[128,5,2,2,128]{4,3,2,1,0:T(2,128)(2,1)}, u32[]{:S(2)}, u32[]{:S(2)}) async-start(bf16[128,5,2,2,128]{4,3,2,1,0:T(2,128)(2,1)} %param.14), calls=%async_computation | async-start | bytes 1310720 | tf_op jit(solution)/shard_map/all_to_all | solution.py:116
  54.6 24.1 %collective-permute-start.6 = (bf16[5,1,8,768]{3,2,1,0:T(8,128)(2,1)S(1)}, bf16[5,1,8,768]{3,2,1,0:T(8,128)(2,1)S(1)}, u32[]{:S(2)}, u32[]{:S(2)}) collective-permute-start(bf16[5,1,8,768]{3,2,1,0:T(8,128)(2,1)S(1)} %get-tuple-element.26), channel_id=1, source_target_pairs={{0,64},{64,128},{128,192},{192,256},{256,320},{320,384},{384,448},... | collective-permute-start | bytes 184328 | tf_op jit(solution)/shard_map/ppermute | solution.py:29
  59.5 13.3 %collective-permute-start.10 = (bf16[5,4,8,1]{3,2,1,0:T(8,128)(2,1)S(1)}, bf16[5,4,8,1]{3,2,1,0:T(8,128)(2,1)S(1)}, u32[]{:S(2)}, u32[]{:S(2)}) collective-permute-start(bf16[5,4,8,1]{3,2,1,0:T(8,128)(2,1)S(1)} %get-tuple-element.22), channel_id=1, source_target_pairs={{0,1},{1,2},{2,3},{3,4},{4,5},{5,6},{6,7},{8,9},{9,10},{10,11},{11... | collective-permute-start | bytes 968 | tf_op jit(solution)/shard_map/ppermute | solution.py:29
  64.5 14.8 %collective-permute-start.7 = (bf16[5,1,8,768]{3,2,1,0:T(8,128)(2,1)S(1)}, bf16[5,1,8,768]{3,2,1,0:T(8,128)(2,1)S(1)}, u32[]{:S(2)}, u32[]{:S(2)}) collective-permute-start(bf16[5,1,8,768]{3,2,1,0:T(8,128)(2,1)S(1)} %get-tuple-element.25), channel_id=1, source_target_pairs={{64,0},{128,64},{192,128},{256,192},{320,256},{384,320},{448,384},... | collective-permute-start | bytes 184328 | tf_op jit(solution)/shard_map/ppermute | solution.py:30
  65.8 11.5 %collective-permute-start.8 = (bf16[5,4,1,768]{3,2,1,0:T(2,128)(2,1)S(1)}, bf16[5,4,1,768]{3,2,1,0:T(2,128)(2,1)S(1)}, u32[]{:S(2)}, u32[]{:S(2)}) collective-permute-start(bf16[5,4,1,768]{3,2,1,0:T(2,128)(2,1)S(1)} %get-tuple-element.24), channel_id=1, source_target_pairs={{0,8},{8,16},{16,24},{24,32},{32,40},{40,48},{48,56},{1,9},{9,17},... | collective-permute-start | bytes 92168 | tf_op jit(solution)/shard_map/ppermute | solution.py:29
  68.4 9.7 %collective-permute-start.9 = (bf16[5,4,1,768]{3,2,1,0:T(2,128)(2,1)S(1)}, bf16[5,4,1,768]{3,2,1,0:T(2,128)(2,1)S(1)}, u32[]{:S(2)}, u32[]{:S(2)}) collective-permute-start(bf16[5,4,1,768]{3,2,1,0:T(2,128)(2,1)S(1)} %get-tuple-element.23), channel_id=1, source_target_pairs={{8,0},{16,8},{24,16},{32,24},{40,32},{48,40},{56,48},{9,1},{17,9},... | collective-permute-start | bytes 92168 | tf_op jit(solution)/shard_map/ppermute | solution.py:30
  72.9 3.8 %collective-permute-start.11 = (bf16[5,4,8,1]{3,2,1,0:T(8,128)(2,1)S(1)}, bf16[5,4,8,1]{3,2,1,0:T(8,128)(2,1)S(1)}, u32[]{:S(2)}, u32[]{:S(2)}) collective-permute-start(bf16[5,4,8,1]{3,2,1,0:T(8,128)(2,1)S(1)} %get-tuple-element.21), channel_id=1, source_target_pairs={{1,0},{2,1},{3,2},{4,3},{5,4},{6,5},{7,6},{9,8},{10,9},{11,10},{12... | collective-permute-start | bytes 968 | tf_op jit(solution)/shard_map/ppermute | solution.py:30
  123.2 4.4 %collective-permute-start.12 = (f32[]{:T(128)}, f32[]{:T(128)}, u32[]{:S(2)}, u32[]{:S(2)}) collective-permute-start(f32[]{:T(128)} %fusion.69), channel_id=1, source_target_pairs={{0,1},{1,2},{2,3},{3,4},{4,5},{5,6},{6,7},{7,0},{8,9},{9,10},{10,1... | collective-permute-start | bytes 20 | tf_op jit(solution)/shard_map/ppermute | solution.py:86
  128.9 6.8 %collective-permute-start.13 = (f32[]{:T(128)}, f32[]{:T(128)}, u32[]{:S(2)}, u32[]{:S(2)}) collective-permute-start(f32[]{:T(128)} %add.234), channel_id=1, source_target_pairs={{0,2},{1,3},{2,4},{3,5},{4,6},{5,7},{6,0},{7,1},{8,10},{9,11},{10,... | collective-permute-start | bytes 20 | tf_op jit(solution)/shard_map/ppermute | solution.py:86
  136.2 7.0 %collective-permute-start.14 = (f32[]{:T(128)}, f32[]{:T(128)}, u32[]{:S(2)}, u32[]{:S(2)}) collective-permute-start(f32[]{:T(128)} %add.235), channel_id=1, source_target_pairs={{0,4},{1,5},{2,6},{3,7},{4,0},{5,1},{6,2},{7,3},{8,12},{9,13},{10,... | collective-permute-start | bytes 20 | tf_op jit(solution)/shard_map/ppermute | solution.py:86
  143.8 6.8 %collective-permute-start.15 = (f32[]{:T(128)}, f32[]{:T(128)}, u32[]{:S(2)}, u32[]{:S(2)}) collective-permute-start(f32[]{:T(128)} %add.236), channel_id=1, source_target_pairs={{0,8},{8,16},{16,24},{24,32},{32,40},{40,48},{48,56},{56,0},{1,9},... | collective-permute-start | bytes 20 | tf_op jit(solution)/shard_map/ppermute | solution.py:86
  151.1 7.6 %collective-permute-start.16 = (f32[]{:T(128)}, f32[]{:T(128)}, u32[]{:S(2)}, u32[]{:S(2)}) collective-permute-start(f32[]{:T(128)} %add.237), channel_id=1, source_target_pairs={{0,16},{8,24},{16,32},{24,40},{32,48},{40,56},{48,0},{56,8},{1,17}... | collective-permute-start | bytes 20 | tf_op jit(solution)/shard_map/ppermute | solution.py:86
  159.4 9.4 %collective-permute-start.17 = (f32[]{:T(128)}, f32[]{:T(128)}, u32[]{:S(2)}, u32[]{:S(2)}) collective-permute-start(f32[]{:T(128)} %add.238), channel_id=1, source_target_pairs={{0,32},{8,40},{16,48},{24,56},{32,0},{40,8},{48,16},{56,24},{1,33}... | collective-permute-start | bytes 20 | tf_op jit(solution)/shard_map/ppermute | solution.py:86
  169.4 12.2 %collective-permute-start.18 = (f32[]{:T(128)}, f32[]{:T(128)}, u32[]{:S(2)}, u32[]{:S(2)}) collective-permute-start(f32[]{:T(128)} %add.239), channel_id=1, source_target_pairs={{0,64},{64,128},{128,192},{192,256},{256,320},{320,384},{384,448},... | collective-permute-start | bytes 20 | tf_op jit(solution)/shard_map/ppermute | solution.py:86
  182.1 7.6 %collective-permute-start.19 = (f32[]{:T(128)}, f32[]{:T(128)}, u32[]{:S(2)}, u32[]{:S(2)}) collective-permute-start(f32[]{:T(128)} %add.240), channel_id=1, source_target_pairs={{0,128},{64,192},{128,256},{192,320},{256,384},{320,448},{384,0},{... | collective-permute-start | bytes 20 | tf_op jit(solution)/shard_map/ppermute | solution.py:86
  190.4 9.4 %collective-permute-start.20 = (f32[]{:T(128)}, f32[]{:T(128)}, u32[]{:S(2)}, u32[]{:S(2)}) collective-permute-start(f32[]{:T(128)} %add.241), channel_id=1, source_target_pairs={{0,256},{64,320},{128,384},{192,448},{256,0},{320,64},{384,128},{4... | collective-permute-start | bytes 20 | tf_op jit(solution)/shard_map/ppermute | solution.py:86
  (18 other events, 170.2 us)

commit v2 on v1

--- a/solution.py
+++ b/solution.py
@@ -16,7 +16,7 @@
 primal_step = 0.05
 dual_step = 0.05
 
-REDUCE = "tree"
+REDUCE = "exchange"
 
 
 def faces(cells, sides):
@@ -48,12 +48,6 @@
     return total - 6.0 * v
 
 
-def swap_pairs(v, dim):
-    shape = v.shape
-    split = shape[:dim] + (shape[dim] // 2, 2) + shape[dim + 1:]
-    return jnp.flip(v.reshape(split), axis=dim + 1).reshape(shape)
-
-
 def block_shift(v, dim, width):
     n = v.shape[dim]
     zero = jnp.zeros_like(lax.slice_in_dim(v, 0, 1, axis=dim))
@@ -66,7 +60,7 @@
 
 
 def laplace_blocks(v):
-    return swap_pairs(v, 1) + swap_pairs(v, 2) + block_shift(v, 3, BZ) - 6.0 * v
+    return block_shift(v, 1, BX) + block_shift(v, 2, BY) + block_shift(v, 3, BZ) - 6.0 * v
 
 
 def couple(matrix, v):
@@ -76,6 +70,14 @@
 def global_sum(x):
     if REDUCE == "psum":
         return lax.psum(x, ("gx", "gy", "gz"))
+    if REDUCE == "exchange":
+        for group in (("gy", "gz"), ("gx",)):
+            count = 1
+            for axis in group:
+                count *= lax.axis_size(axis)
+            spread = jnp.broadcast_to(x.reshape(1), (count,))
+            x = jnp.sum(lax.all_to_all(spread, group, 0, 0, tiled=True))
+        return x
     if REDUCE == "gather":
         every = lax.all_gather(x.reshape(1), ("gx", "gy", "gz"), tiled=True)
         return jnp.sum(every)
@@ -113,8 +115,15 @@
     sides = (("gx", 1), ("gy", 2), ("gz", 3))
     dims = (1, 2, 3)
 
-    arrived_goal = lax.all_to_all(goal_weight, ("gy", "gz"), 0, 0, tiled=True)
-    arrived_react = lax.all_to_all(reaction, ("gy", "gz"), 0, 0, tiled=True)
+    slots = goal_weight.shape[0]
+    packed = jnp.concatenate(
+        [
+            goal_weight.reshape(slots, FIELDS, BX * BY, BZ),
+            jnp.broadcast_to(reaction[:, :, None, None], (slots, FIELDS, 1, BZ)),
+        ],
+        axis=2,
+    )
+    arrived = lax.all_to_all(packed, ("gy", "gz"), 0, 0, tiled=True)
 
     state_now = state.astype(jnp.float32)
     diffuse = diffusivity.astype(jnp.float32)[None]
@@ -138,8 +147,9 @@
     capacity = goal_weight.shape[0] // (lax.axis_size("gy") * lax.axis_size("gz"))
     slot_of = targets * capacity + rank
 
-    goal = to_cells(arrived_goal[slot_of]).astype(jnp.float32)
-    react = per_block_cells(arrived_react[slot_of]).astype(jnp.float32)
+    mine = arrived[slot_of]
+    goal = to_cells(mine[:, :, : BX * BY].reshape(-1, FIELDS, BX, BY, BZ)).astype(jnp.float32)
+    react = per_block_cells(mine[:, :, BX * BY, 0]).astype(jnp.float32)
     eff = effective.astype(jnp.float32)[None]
     transposed = coupling.T
     dual = goal

time: 202 us -> 141 us (0.70)
  the two profiles are of different devices: /device:TPU:32 before, /device:TPU:1 now
where the time goes in v2:
time: 141 us; the launch traced here: 140 us
  starting transfers between devices  69.1 us (49%)
  other arithmetic  26.4 us (19%)
  local copies, waits for them, and re-layouts  23.6 us (17%)
  waiting for transfers between devices  19.3 us (14%)
  between operations  1.85 us (1%)
    all_to_all x2, starting transfers between devices, global_sum(): x = jnp.sum(lax.all_to_all(spread, group, 0, 0, tiled=True))  24.2 us
    ppermute x6, starting transfers between devices, faces(): below = lax.ppermute(tail, axis, [(i, i + 1) for i in range(ends)])  23 us
    all_to_all x2, waiting for transfers between devices, global_sum(): x = jnp.sum(lax.all_to_all(spread, group, 0, 0, tiled=True))  15.3 us
    all_to_all x1, starting transfers between devices, shards(): arrived = lax.all_to_all(packed, ('gy', 'gz'), 0, 0, tiled=True)  11.7 us
    ppermute x6, starting transfers between devices, faces(): above = lax.ppermute(head, axis, [(i + 1, i) for i in range(ends)])  10.1 us
    convert_element_type x12, other arithmetic, laplace_halo(): minus, plus = shifted(v, dim, below.astype(v.dtype), above.astype(v.dtype))  7.6 us
    slice x3, local copies, waits for them, and re-layouts, faces(): lax.slice_in_dim(cells, cells.shape[dim] - 1, cells.shape[dim], axis=dim)  4.9 us
    ppermute x6, waiting for transfers between devices, faces(): above = lax.ppermute(head, axis, [(i + 1, i) for i in range(ends)])  4.07 us
  transfers between devices with their start and end apart: 15, of which 4 were waited for; matrix products, arithmetic and copies ran while one was open for 18% of the time, Pallas kernels for 0%

profile of v2, /device:TPU:1, one launch (start us, length us, event | category | flops | bytes accessed | tf_op | source)
XLA Modules:
  0.0 140.2 jit_solution(213322028345997932)
XLA Ops:
  0.6 1.6 %fusion.119 = (bf16[5,1,8,768]{3,2,1,0:T(8,128)(2,1)}, bf16[5,1,8,768]{3,2,1,0:T(8,128)(2,1)}) fusion(bf16[5,4,8,768]{3,2,1,0:T(8,128)(2,1)} %param.8), kind=kLoop, calls=%fused_computation.154 | loop fusion | bytes 245760 | tf_op jit(solution)/shard_map/slice | solution.py:28
  2.2 5.4 %collective-permute-start = (bf16[5,1,8,768]{3,2,1,0:T(8,128)(2,1)}, bf16[5,1,8,768]{3,2,1,0:T(8,128)(2,1)}, u32[]{:S(2)}, u32[]{:S(2)}) collective-permute-start(bf16[5,1,8,768]{3,2,1,0:T(8,128)(2,1)} %get-tuple-element.43), channel_id=1, source_target_pairs={{0,64},{64,128},{128,192},{192,256},{256,320},{320,384},{384,448},... | collective-permute-start | bytes 184328 | tf_op jit(solution)/shard_map/ppermute | solution.py:29
  8.9 1.8 %fusion.121 = (bf16[5,4,1,768]{3,2,1,0:T(2,128)(2,1)}, bf16[5,4,1,768]{3,2,1,0:T(2,128)(2,1)}) fusion(bf16[5,4,8,768]{3,2,1,0:T(8,128)(2,1)} %param.8), kind=kLoop, calls=%fused_computation.156 | loop fusion | bytes 122880 | tf_op jit(solution)/shard_map/slice | solution.py:28
  10.7 3.8 %collective-permute-start.2 = (bf16[5,4,1,768]{3,2,1,0:T(2,128)(2,1)}, bf16[5,4,1,768]{3,2,1,0:T(2,128)(2,1)}, u32[]{:S(2)}, u32[]{:S(2)}) collective-permute-start(bf16[5,4,1,768]{3,2,1,0:T(2,128)(2,1)} %get-tuple-element.47), channel_id=1, source_target_pairs={{0,8},{8,16},{16,24},{24,32},{32,40},{40,48},{48,56},{1,9},{9,17},... | collective-permute-start | bytes 92168 | tf_op jit(solution)/shard_map/ppermute | solution.py:29
  15.9 1.5 %fusion.123 = (bf16[5,4,8,1]{3,2,1,0:T(8,128)(2,1)}, bf16[5,4,8,1]{3,2,1,0:T(8,128)(2,1)}) fusion(bf16[5,4,8,768]{3,2,1,0:T(8,128)(2,1)} %param.8), kind=kLoop, calls=%fused_computation.158 | loop fusion | bytes 1280 | tf_op jit(solution)/shard_map/slice | solution.py:28
  17.4 4.2 %collective-permute-start.4 = (bf16[5,4,8,1]{3,2,1,0:T(8,128)(2,1)}, bf16[5,4,8,1]{3,2,1,0:T(8,128)(2,1)}, u32[]{:S(2)}, u32[]{:S(2)}) collective-permute-start(bf16[5,4,8,1]{3,2,1,0:T(8,128)(2,1)} %get-tuple-element.51), channel_id=1, source_target_pairs={{0,1},{1,2},{2,3},{3,4},{4,5},{5,6},{6,7},{8,9},{9,10},{10,11},{11... | collective-permute-start | bytes 968 | tf_op jit(solution)/shard_map/ppermute | solution.py:29
  23.3 1.8 %pad_maximum_fusion = bf16[128,5,5,128]{3,2,1,0:T(8,128)(2,1)} fusion(bf16[128,5,1,128]{3,2,1,0:T(2,128)(2,1)S(1)} %broadcast_in_dim.64, bf16[128,5,4,128]{3,2,1,0:T(4,128)(2,1)S(1)} %bitcast.27), kind=kLoop, calls=%fused_computation.6 | loop fusion | flops 1638400 | bytes 1638400 | tf_op jit(solution)/shard_map/concatenate | solution.py:119
  25.0 11.7 %all-to-all-start = ((bf16[128,5,5,128]{3,2,1,0:T(8,128)(2,1)}), bf16[128,5,5,128]{3,2,1,0:T(8,128)(2,1)S(1)}, u32[]{:S(2)}, u32[]{:S(2)}) async-start(bf16[128,5,5,128]{3,2,1,0:T(8,128)(2,1)} %pad_maximum_fusion), calls=%async_computation | async-start | bytes 2621440 | tf_op jit(solution)/shard_map/all_to_all | solution.py:126
  41.6 2.4 %collective-permute-start.5 = (bf16[5,4,8,1]{3,2,1,0:T(8,128)(2,1)}, bf16[5,4,8,1]{3,2,1,0:T(8,128)(2,1)S(1)}, u32[]{:S(2)}, u32[]{:S(2)}) collective-permute-start(bf16[5,4,8,1]{3,2,1,0:T(8,128)(2,1)} %get-tuple-element.52), channel_id=1, source_target_pairs={{1,0},{2,1},{3,2},{4,3},{5,4},{6,5},{7,6},{9,8},{10,9},{11,10},{12... | collective-permute-start | bytes 968 | tf_op jit(solution)/shard_map/ppermute | solution.py:30
  46.1 1.5 %collective-permute-done.5 = bf16[5,4,8,1]{3,2,1,0:T(8,128)(2,1)S(1)} collective-permute-done((bf16[5,4,8,1]{3,2,1,0:T(8,128)(2,1)}, bf16[5,4,8,1]{3,2,1,0:T(8,128)(2,1)S(1)}, u32[]{:S(2)}, u32[]{:S(2)}) %collective-permute-start.5) | collective-permute-done | bytes 352 | tf_op jit(solution)/shard_map/ppermute | solution.py:30
  51.1 1.9 %fusion.99 = (bf16[5,4,8,768]{3,2,1,0:T(8,128)(2,1)S(1)}, f32[5,4,8,768]{3,2,1,0:T(8,128)S(1)}) fusion(f32[5,4,8,768]{3,2,1,0:T(8,128)S(1)} %multiply_reduce_fusion.4, f32[5,4,8,1]{3,2,1,0:T(8,128)S(1)} %convert_element_type.110, f32[5,4,8,767]{3,2,1,0:T(8,128)} %get-tuple-element.54, f32[5,4,8,767]{3,2,1,0:T(8,128)} %get-tuple-element.53, ...), kind=kLoop, calls=%fused_computation.135 | loop fusion | flops 2334720 | bytes 4521984 | tf_op jit(solution)/shard_map/convert_element_type | solution.py:134
  53.0 4.3 %collective-permute-start.6 = (bf16[5,1,8,768]{3,2,1,0:T(8,128)(2,1)S(1)}, bf16[5,1,8,768]{3,2,1,0:T(8,128)(2,1)S(1)}, u32[]{:S(2)}, u32[]{:S(2)}) collective-permute-start(bf16[5,1,8,768]{3,2,1,0:T(8,128)(2,1)S(1)} %get-tuple-element.42), channel_id=1, source_target_pairs={{0,64},{64,128},{128,192},{192,256},{256,320},{320,384},{384,448},... | collective-permute-start | bytes 184328 | tf_op jit(solution)/shard_map/ppermute | solution.py:29
  57.4 2.0 %collective-permute-start.10 = (bf16[5,4,8,1]{3,2,1,0:T(8,128)(2,1)S(1)}, bf16[5,4,8,1]{3,2,1,0:T(8,128)(2,1)S(1)}, u32[]{:S(2)}, u32[]{:S(2)}) collective-permute-start(bf16[5,4,8,1]{3,2,1,0:T(8,128)(2,1)S(1)} %get-tuple-element.38), channel_id=1, source_target_pairs={{0,1},{1,2},{2,3},{3,4},{4,5},{5,6},{6,7},{8,9},{9,10},{10,11},{11... | collective-permute-start | bytes 968 | tf_op jit(solution)/shard_map/ppermute | solution.py:29
  63.7 3.3 %collective-permute-start.8 = (bf16[5,4,1,768]{3,2,1,0:T(2,128)(2,1)S(1)}, bf16[5,4,1,768]{3,2,1,0:T(2,128)(2,1)S(1)}, u32[]{:S(2)}, u32[]{:S(2)}) collective-permute-start(bf16[5,4,1,768]{3,2,1,0:T(2,128)(2,1)S(1)} %get-tuple-element.40), channel_id=1, source_target_pairs={{0,8},{8,16},{16,24},{24,32},{32,40},{40,48},{48,56},{1,9},{9,17},... | collective-permute-start | bytes 92168 | tf_op jit(solution)/shard_map/ppermute | solution.py:29
  67.0 1.3 collective-permute-start.9
  68.4 2.6 %collective-permute-start.11 = (bf16[5,4,8,1]{3,2,1,0:T(8,128)(2,1)S(1)}, bf16[5,4,8,1]{3,2,1,0:T(8,128)(2,1)S(1)}, u32[]{:S(2)}, u32[]{:S(2)}) collective-permute-start(bf16[5,4,8,1]{3,2,1,0:T(8,128)(2,1)S(1)} %get-tuple-element.37), channel_id=1, source_target_pairs={{1,0},{2,1},{3,2},{4,3},{5,4},{6,5},{7,6},{9,8},{10,9},{11,10},{12... | collective-permute-start | bytes 968 | tf_op jit(solution)/shard_map/ppermute | solution.py:30
  71.2 2.6 %collective-permute-done.11 = bf16[5,4,8,1]{3,2,1,0:T(8,128)(2,1)S(1)} collective-permute-done((bf16[5,4,8,1]{3,2,1,0:T(8,128)(2,1)S(1)}, bf16[5,4,8,1]{3,2,1,0:T(8,128)(2,1)S(1)}, u32[]{:S(2)}, u32[]{:S(2)}) %collective-permute-start.11) | collective-permute-done | bytes 352 | tf_op jit(solution)/shard_map/ppermute | solution.py:30
  77.2 1.5 %gather_fusion = bf16[48,5,5,128]{3,2,1,0:T(8,128)(2,1)} fusion(bf16[128,5,5,128]{3,2,1,0:T(8,128)(2,1)S(1)} %all-to-all-done, s32[1024]{0:T(1024)} %pad_clamp_fusion), kind=kCustom, calls=%fused_computation | custom fusion | bytes 614592 | tf_op jit(solution)/shard_map/gather | solution.py:150
  85.8 2.3 %fusion.32 = f32[5,4,8,768]{3,2,1,0:T(8,128)S(1)} fusion(f32[5,4,8,768]{3,2,1,0:T(8,128)S(1)} %reshape.58, f32[5,4,8,768]{3,2,1,0:T(8,128)} %multiply_reduce_fusion.3, f32[5,4,8,768]{3,2,1,0:T(8,128)S(1)} %convert_element_type.116, f32[5,4,8,767]{3,2,1,0:T(8,128)} %get-tuple-element.30, f32[5,4,8,767]{3,2,1,0:T(8,128)} %get-tuple-element.29, ...), kind=kLoop, calls=%fused_computation.45 | loop fusion | flops 3563520 | bytes 4650604 | tf_op jit(solution)/shard_map/add | solution.py:157
  92.6 1.6 %fusion.84 = (f32[4,8,768]{2,1,0:T(8,128)S(1)}, bf16[5,4,8,768]{3,2,1,0:T(8,128)(2,1)}) fusion(f32[5,4,8,768]{3,2,1,0:T(8,128)S(1)} %multiply_reduce_fusion, f32[5,3,8,768]{3,2,1,0:T(8,128)S(1)} %copy-done.5, f32[5,1,8,768]{3,2,1,0:T(8,128)S(1)} %copy-done.8, f32[5,1,8,768]{3,2,1,0:T(8,128)S(1)} %copy-done.9, f32[5,3,8,768]{3,2,1,0:T(8,128)S(1)} %copy-done.4, ...), kind=kLoop, calls=%fused_computation.101 | loop fusion | flops 5873664 | bytes 7698028 | tf_op jit(solution)/shard_map/reduce_sum | solution.py:111
  96.3 12.4 %all-to-all-start.1 = ((f32[64,1,1]{2,1,0:T(1,128)}), f32[64,1,1]{2,1,0:T(1,128)S(1)}, u32[]{:S(2)}, u32[]{:S(2)}) async-start(f32[64,1,1]{2,1,0:T(1,128)} %broadcast_in_dim.67), calls=%async_computation.1 | async-start | bytes 65536 | tf_op jit(solution)/shard_map/all_to_all | solution.py:79
  109.3 8.7 %all-to-all-done.1 = f32[64,1,1]{2,1,0:T(1,128)S(1)} async-done(((f32[64,1,1]{2,1,0:T(1,128)}), f32[64,1,1]{2,1,0:T(1,128)S(1)}, u32[]{:S(2)}, u32[]{:S(2)}) %all-to-all-start.1) | async-done | bytes 288 | tf_op jit(solution)/shard_map/all_to_all | solution.py:79
  120.0 11.8 %all-to-all-start.2 = ((f32[8,1,1]{2,1,0:T(1,128)}), f32[8,1,1]{2,1,0:T(1,128)S(1)}, u32[]{:S(2)}, u32[]{:S(2)}) async-start(f32[8,1,1]{2,1,0:T(1,128)} %broadcast_in_dim.68), calls=%async_computation.2 | async-start | bytes 8192 | tf_op jit(solution)/shard_map/all_to_all | solution.py:79
  131.8 6.5 %all-to-all-done.2 = f32[8,1,1]{2,1,0:T(1,128)S(1)} async-done(((f32[8,1,1]{2,1,0:T(1,128)}), f32[8,1,1]{2,1,0:T(1,128)S(1)}, u32[]{:S(2)}, u32[]{:S(2)}) %all-to-all-start.2) | async-done | bytes 64 | tf_op jit(solution)/shard_map/all_to_all | solution.py:79
  (135 shorter events, 39.8 us)
Async XLA Ops:
  0.6 22.6 %copy-start.7 = (bf16[128,5,2,2,128]{4,3,2,1,0:T(2,128)(2,1)S(1)}, bf16[128,5,2,2,128]{4,3,2,1,0:T(2,128)(2,1)}, u32[]{:S(2)}) copy-start(bf16[128,5,2,2,128]{4,3,2,1,0:T(2,128)(2,1)} %param.14) | copy-start | bytes 1966084
  2.2 47.2 %collective-permute-start = (bf16[5,1,8,768]{3,2,1,0:T(8,128)(2,1)}, bf16[5,1,8,768]{3,2,1,0:T(8,128)(2,1)}, u32[]{:S(2)}, u32[]{:S(2)}) collective-permute-start(bf16[5,1,8,768]{3,2,1,0:T(8,128)(2,1)} %get-tuple-element.43), channel_id=1, source_target_pairs={{0,64},{64,128},{128,192},{192,256},{256,320},{320,384},{384,448},... | collective-permute-start | bytes 184328 | tf_op jit(solution)/shard_map/ppermute | solution.py:29
  7.7 42.6 %collective-permute-start.1 = (bf16[5,1,8,768]{3,2,1,0:T(8,128)(2,1)}, bf16[5,1,8,768]{3,2,1,0:T(8,128)(2,1)}, u32[]{:S(2)}, u32[]{:S(2)}) collective-permute-start(bf16[5,1,8,768]{3,2,1,0:T(8,128)(2,1)} %get-tuple-element.44), channel_id=1, source_target_pairs={{64,0},{128,64},{192,128},{256,192},{320,256},{384,320},{448,384},... | collective-permute-start | bytes 184328 | tf_op jit(solution)/shard_map/ppermute | solution.py:30
  10.7 36.8 %collective-permute-start.2 = (bf16[5,4,1,768]{3,2,1,0:T(2,128)(2,1)}, bf16[5,4,1,768]{3,2,1,0:T(2,128)(2,1)}, u32[]{:S(2)}, u32[]{:S(2)}) collective-permute-start(bf16[5,4,1,768]{3,2,1,0:T(2,128)(2,1)} %get-tuple-element.47), channel_id=1, source_target_pairs={{0,8},{8,16},{16,24},{24,32},{32,40},{40,48},{48,56},{1,9},{9,17},... | collective-permute-start | bytes 92168 | tf_op jit(solution)/shard_map/ppermute | solution.py:29
  14.6 33.9 %collective-permute-start.3 = (bf16[5,4,1,768]{3,2,1,0:T(2,128)(2,1)}, bf16[5,4,1,768]{3,2,1,0:T(2,128)(2,1)}, u32[]{:S(2)}, u32[]{:S(2)}) collective-permute-start(bf16[5,4,1,768]{3,2,1,0:T(2,128)(2,1)} %get-tuple-element.48), channel_id=1, source_target_pairs={{8,0},{16,8},{24,16},{32,24},{40,32},{48,40},{56,48},{9,1},{17,9},... | collective-permute-start | bytes 92168 | tf_op jit(solution)/shard_map/ppermute | solution.py:30
  17.4 24.3 %collective-permute-start.4 = (bf16[5,4,8,1]{3,2,1,0:T(8,128)(2,1)}, bf16[5,4,8,1]{3,2,1,0:T(8,128)(2,1)}, u32[]{:S(2)}, u32[]{:S(2)}) collective-permute-start(bf16[5,4,8,1]{3,2,1,0:T(8,128)(2,1)} %get-tuple-element.51), channel_id=1, source_target_pairs={{0,1},{1,2},{2,3},{3,4},{4,5},{5,6},{6,7},{8,9},{9,10},{10,11},{11... | collective-permute-start | bytes 968 | tf_op jit(solution)/shard_map/ppermute | solution.py:29
  25.0 11.7 %copy-start = (bf16[5,4,8,768]{3,2,1,0:T(8,128)(2,1)S(1)}, bf16[5,4,8,768]{3,2,1,0:T(8,128)(2,1)}, u32[]{:S(2)}) copy-start(bf16[5,4,8,768]{3,2,1,0:T(8,128)(2,1)} %param.8) | copy-start | bytes 737284
  25.0 52.1 %all-to-all-start = ((bf16[128,5,5,128]{3,2,1,0:T(8,128)(2,1)}), bf16[128,5,5,128]{3,2,1,0:T(8,128)(2,1)S(1)}, u32[]{:S(2)}, u32[]{:S(2)}) async-start(bf16[128,5,5,128]{3,2,1,0:T(8,128)(2,1)} %pad_maximum_fusion), calls=%async_computation | async-start | bytes 2621440 | tf_op jit(solution)/shard_map/all_to_all | solution.py:126
  37.9 2.1 %copy-start.23 = (s32[48,1]{0,1:T(1,128)S(1)}, s32[48,1]{0,1:T(1,128)}, u32[]{:S(2)}) copy-start(s32[48,1]{0,1:T(1,128)} %param.11) | copy-start | bytes 580
  38.0 2.9 %copy-start.15 = (f32[5,5]{1,0:T(8,128)S(1)}, f32[5,5]{1,0:T(8,128)}, u32[]{:S(2)}) copy-start(f32[5,5]{1,0:T(8,128)} %param.10) | copy-start | bytes 304
  38.0 6.6 %copy-start.13 = (bf16[4,8,768]{2,1,0:T(8,128)(2,1)S(1)}, bf16[4,8,768]{2,1,0:T(8,128)(2,1)}, u32[]{:S(2)}) copy-start(bf16[4,8,768]{2,1,0:T(8,128)(2,1)} %param.9) | copy-start | bytes 147460
  41.6 5.9 %collective-permute-start.5 = (bf16[5,4,8,1]{3,2,1,0:T(8,128)(2,1)}, bf16[5,4,8,1]{3,2,1,0:T(8,128)(2,1)S(1)}, u32[]{:S(2)}, u32[]{:S(2)}) collective-permute-start(bf16[5,4,8,1]{3,2,1,0:T(8,128)(2,1)} %get-tuple-element.52), channel_id=1, source_target_pairs={{1,0},{2,1},{3,2},{4,3},{5,4},{6,5},{7,6},{9,8},{10,9},{11,10},{12... | collective-permute-start | bytes 968 | tf_op jit(solution)/shard_map/ppermute | solution.py:30
  51.1 8.3 %copy-start.14 = (bf16[4,8,768]{2,1,0:T(8,128)(2,1)S(1)}, bf16[4,8,768]{2,1,0:T(8,128)(2,1)}, u32[]{:S(2)}) copy-start(bf16[4,8,768]{2,1,0:T(8,128)(2,1)} %param.9) | copy-start | bytes 147460
  53.0 22.8 %collective-permute-start.6 = (bf16[5,1,8,768]{3,2,1,0:T(8,128)(2,1)S(1)}, bf16[5,1,8,768]{3,2,1,0:T(8,128)(2,1)S(1)}, u32[]{:S(2)}, u32[]{:S(2)}) collective-permute-start(bf16[5,1,8,768]{3,2,1,0:T(8,128)(2,1)S(1)} %get-tuple-element.42), channel_id=1, source_target_pairs={{0,64},{64,128},{128,192},{192,256},{256,320},{320,384},{384,448},... | collective-permute-start | bytes 184328 | tf_op jit(solution)/shard_map/ppermute | solution.py:29
  57.4 11.0 %collective-permute-start.10 = (bf16[5,4,8,1]{3,2,1,0:T(8,128)(2,1)S(1)}, bf16[5,4,8,1]{3,2,1,0:T(8,128)(2,1)S(1)}, u32[]{:S(2)}, u32[]{:S(2)}) collective-permute-start(bf16[5,4,8,1]{3,2,1,0:T(8,128)(2,1)S(1)} %get-tuple-element.38), channel_id=1, source_target_pairs={{0,1},{1,2},{2,3},{3,4},{4,5},{5,6},{6,7},{8,9},{9,10},{10,11},{11... | collective-permute-start | bytes 968 | tf_op jit(solution)/shard_map/ppermute | solution.py:29
  62.5 14.0 %collective-permute-start.7 = (bf16[5,1,8,768]{3,2,1,0:T(8,128)(2,1)S(1)}, bf16[5,1,8,768]{3,2,1,0:T(8,128)(2,1)S(1)}, u32[]{:S(2)}, u32[]{:S(2)}) collective-permute-start(bf16[5,1,8,768]{3,2,1,0:T(8,128)(2,1)S(1)} %get-tuple-element.41), channel_id=1, source_target_pairs={{64,0},{128,64},{192,128},{256,192},{320,256},{384,320},{448,384},... | collective-permute-start | bytes 184328 | tf_op jit(solution)/shard_map/ppermute | solution.py:30
  63.7 10.7 %collective-permute-start.8 = (bf16[5,4,1,768]{3,2,1,0:T(2,128)(2,1)S(1)}, bf16[5,4,1,768]{3,2,1,0:T(2,128)(2,1)S(1)}, u32[]{:S(2)}, u32[]{:S(2)}) collective-permute-start(bf16[5,4,1,768]{3,2,1,0:T(2,128)(2,1)S(1)} %get-tuple-element.40), channel_id=1, source_target_pairs={{0,8},{8,16},{16,24},{24,32},{32,40},{40,48},{48,56},{1,9},{9,17},... | collective-permute-start | bytes 92168 | tf_op jit(solution)/shard_map/ppermute | solution.py:29
  67.0 8.1 %collective-permute-start.9 = (bf16[5,4,1,768]{3,2,1,0:T(2,128)(2,1)S(1)}, bf16[5,4,1,768]{3,2,1,0:T(2,128)(2,1)S(1)}, u32[]{:S(2)}, u32[]{:S(2)}) collective-permute-start(bf16[5,4,1,768]{3,2,1,0:T(2,128)(2,1)S(1)} %get-tuple-element.39), channel_id=1, source_target_pairs={{8,0},{16,8},{24,16},{32,24},{40,32},{48,40},{56,48},{9,1},{17,9},... | collective-permute-start | bytes 92168 | tf_op jit(solution)/shard_map/ppermute | solution.py:30
  68.4 5.5 %collective-permute-start.11 = (bf16[5,4,8,1]{3,2,1,0:T(8,128)(2,1)S(1)}, bf16[5,4,8,1]{3,2,1,0:T(8,128)(2,1)S(1)}, u32[]{:S(2)}, u32[]{:S(2)}) collective-permute-start(bf16[5,4,8,1]{3,2,1,0:T(8,128)(2,1)S(1)} %get-tuple-element.37), channel_id=1, source_target_pairs={{1,0},{2,1},{3,2},{4,3},{5,4},{6,5},{7,6},{9,8},{10,9},{11,10},{12... | collective-permute-start | bytes 968 | tf_op jit(solution)/shard_map/ppermute | solution.py:30
  91.0 1.6 %copy-start.10 = (f32[5,4,8,1]{3,2,1,0:T(8,128)S(1)}, f32[5,4,8,1]{3,2,1,0:T(8,128)}, u32[]{:S(2)}) copy-start(f32[5,4,8,1]{3,2,1,0:T(8,128)} %convert_element_type.125) | copy-start | bytes 1924
  91.0 1.6 %copy-start.11 = (f32[5,4,1,768]{3,2,1,0:T(1,128)S(1)}, f32[5,4,1,768]{3,2,1,0:T(1,128)}, u32[]{:S(2)}) copy-start(f32[5,4,1,768]{3,2,1,0:T(1,128)} %convert_element_type.122) | copy-start | bytes 184324
  92.6 1.8 %copy-start.22 = (s32[48]{0:T(128)S(1)}, s32[48]{0:T(128)}, u32[]{:S(2)}) copy-start(s32[48]{0:T(128)} %param.12) | copy-start | bytes 580
  96.3 21.8 %all-to-all-start.1 = ((f32[64,1,1]{2,1,0:T(1,128)}), f32[64,1,1]{2,1,0:T(1,128)S(1)}, u32[]{:S(2)}, u32[]{:S(2)}) async-start(f32[64,1,1]{2,1,0:T(1,128)} %broadcast_in_dim.67), calls=%async_computation.1 | async-start | bytes 65536 | tf_op jit(solution)/shard_map/all_to_all | solution.py:79
  120.0 18.4 %all-to-all-start.2 = ((f32[8,1,1]{2,1,0:T(1,128)}), f32[8,1,1]{2,1,0:T(1,128)S(1)}, u32[]{:S(2)}, u32[]{:S(2)}) async-start(f32[8,1,1]{2,1,0:T(1,128)} %broadcast_in_dim.68), calls=%async_computation.2 | async-start | bytes 8192 | tf_op jit(solution)/shard_map/all_to_all | solution.py:79
  (15 other events, 16.7 us)

commit v3 on v2

--- a/solution.py
+++ b/solution.py
@@ -1,6 +1,8 @@
 import jax
 import jax.numpy as jnp
 from jax import lax
+from jax.experimental import pallas as pl
+from jax.experimental.pallas import tpu as pltpu
 from jax.sharding import PartitionSpec as P
 
 BX = 2
@@ -111,6 +113,130 @@
     return jnp.sum(shaped, axis=(0, 2, 4, 6)).reshape(NBX * NBY * NBZ)
 
 
+def _masks(rows_n, lanes_n):
+    rows = lax.broadcasted_iota(jnp.int32, (rows_n, lanes_n), 0)
+    lanes = lax.broadcasted_iota(jnp.int32, (rows_n, lanes_n), 1)
+    r_src = (pltpu.roll(rows, 1, 0), pltpu.roll(rows, rows_n - 1, 0))
+    l_src = (pltpu.roll(lanes, 1, 1), pltpu.roll(lanes, lanes_n - 1, 1))
+    return rows, lanes, r_src, l_src
+
+
+def _rolled(v):
+    rows_n, lanes_n = v.shape
+    return (
+        (pltpu.roll(v, 1, 0), pltpu.roll(v, rows_n - 1, 0)),
+        (pltpu.roll(v, 1, 1), pltpu.roll(v, lanes_n - 1, 1)),
+    )
+
+
+def _lap_halo(c, xm, xp, ylo, yhi, zlo, zhi, geo):
+    rows, lanes, r_src, l_src = geo
+    rows_n, lanes_n = c.shape
+    (r1, r2), (l1, l2) = _rolled(c)
+    y_out = jnp.where(rows == 0, ylo, yhi)
+    z_out = jnp.where(lanes == 0, zlo, zhi)
+    t1 = jnp.where(jnp.abs(r_src[0] - rows) == 1, r1, y_out)
+    t2 = jnp.where(jnp.abs(r_src[1] - rows) == 1, r2, y_out)
+    u1 = jnp.where(jnp.abs(l_src[0] - lanes) == 1, l1, z_out)
+    u2 = jnp.where(jnp.abs(l_src[1] - lanes) == 1, l2, z_out)
+    return (xp + xm) + (t1 + t2) + (u1 + u2) - 6.0 * c
+
+
+def _lap_block(c, partner_x, geo):
+    rows, lanes, r_src, l_src = geo
+    (r1, r2), (l1, l2) = _rolled(c)
+    t1 = jnp.where(r_src[0] // BY == rows // BY, r1, 0.0)
+    t2 = jnp.where(r_src[1] // BY == rows // BY, r2, 0.0)
+    u1 = jnp.where(l_src[0] // BZ == lanes // BZ, l1, 0.0)
+    u2 = jnp.where(l_src[1] // BZ == lanes // BZ, l2, 0.0)
+    return partner_x + (t1 + t2) + (u1 + u2) - 6.0 * c
+
+
+def _couple(c_ref, vals, transpose):
+    out = []
+    for f in range(len(vals)):
+        def m(g):
+            return c_ref[g, f] if transpose else c_ref[f, g]
+        acc = m(0) * vals[0]
+        for g in range(1, len(vals)):
+            acc = acc + m(g) * vals[g]
+        out.append(acc)
+    return out
+
+
+def primal_kernel(c_ref, s_ref, d_ref, xlo, xhi, ylo, yhi, zlo, zhi,
+                  s1_ref, eff_ref, oxlo, oxhi, oylo, oyhi, ozlo, ozhi):
+    nf, nx, ny, nz = s_ref.shape
+    geo = _masks(ny, nz)
+    f32 = jnp.float32
+    s = [[s_ref[f, x].astype(f32) for x in range(nx)] for f in range(nf)]
+    for x in range(nx):
+        d = d_ref[x].astype(f32)
+        col = [s[f][x] for f in range(nf)]
+        cs = _couple(c_ref, col, False)
+        s1 = []
+        for f in range(nf):
+            xm = s[f][x - 1] if x > 0 else xlo[f, 0].astype(f32)
+            xp = s[f][x + 1] if x < nx - 1 else xhi[f, 0].astype(f32)
+            lap = _lap_halo(s[f][x], xm, xp, ylo[f, x].astype(f32), yhi[f, x].astype(f32),
+                            zlo[f, x].astype(f32), zhi[f, x].astype(f32), geo)
+            v = s[f][x] + primal_step * (d * lap + cs[f])
+            s1.append(v)
+            s1_ref[f, x] = v
+            low = v.astype(jnp.bfloat16)
+            if x == 0:
+                oxlo[f, 0] = low
+            if x == nx - 1:
+                oxhi[f, 0] = low
+            oylo[f, x] = low[0:1, :]
+            oyhi[f, x] = low[ny - 1:ny, :]
+            ozlo[f, x] = low[:, 0:1]
+            ozhi[f, x] = low[:, nz - 1:nz]
+        eff_ref[x] = (d * (1.0 + 0.5 * jnp.tanh(s1[0]))).astype(jnp.bfloat16)
+
+
+def adjoint_kernel(c_ref, s1_ref, s_ref, d_ref, xlo, xhi, ylo, yhi, zlo, zhi, eff_ref, goal_ref, react_ref,
+                   enr_ref, part_ref):
+    nf, nx, ny, nz = s_ref.shape
+    geo = _masks(ny, nz)
+    f32 = jnp.float32
+    s1 = [[s1_ref[f, x] for x in range(nx)] for f in range(nf)]
+    residual = [[None] * nx for _ in range(nf)]
+    for x in range(nx):
+        d = d_ref[x].astype(f32)
+        cs = _couple(c_ref, [s1[f][x] for f in range(nf)], False)
+        for f in range(nf):
+            xm = s1[f][x - 1] if x > 0 else xlo[f, 0].astype(f32)
+            xp = s1[f][x + 1] if x < nx - 1 else xhi[f, 0].astype(f32)
+            lap = _lap_halo(s1[f][x], xm, xp, ylo[f, x].astype(f32), yhi[f, x].astype(f32),
+                            zlo[f, x].astype(f32), zhi[f, x].astype(f32), geo)
+            residual[f][x] = d * lap + cs[f] - (s1[f][x] - s_ref[f, x].astype(f32)) / primal_step
+    eff = [eff_ref[x].astype(f32) for x in range(nx)]
+    goal = [[goal_ref[f, x].astype(f32) for x in range(nx)] for f in range(nf)]
+    react = [[react_ref[f, x].astype(f32) for x in range(nx)] for f in range(nf)]
+    dual = [list(row) for row in goal]
+    for _ in range(SECTIONS):
+        new = [[None] * nx for _ in range(nf)]
+        for x in range(nx):
+            ct = _couple(c_ref, [dual[f][x] for f in range(nf)], True)
+            for f in range(nf):
+                lap = _lap_block(dual[f][x], dual[f][x ^ 1], geo)
+                new[f][x] = dual[f][x] + dual_step * (
+                    eff[x] * lap + ct[f] - react[f][x] * dual[f][x] + goal[f][x]
+                )
+        dual = new
+    for bx in range(nx // BX):
+        acc = None
+        for x in range(bx * BX, bx * BX + BX):
+            for f in range(nf):
+                lap = _lap_block(dual[f][x], dual[f][x ^ 1], geo)
+                e = (dual[f][x] + 0.125 * lap).astype(jnp.bfloat16)
+                enr_ref[f, x] = e
+                term = jnp.abs(residual[f][x] * e.astype(f32))
+                acc = term if acc is None else acc + term
+        part_ref[bx] = acc
+
+
 def shards(state, diffusivity, coupling, owner, levels, mark_count, goal_weight, reaction):
     sides = (("gx", 1), ("gy", 2), ("gz", 3))
     dims = (1, 2, 3)
@@ -125,19 +251,25 @@
     )
     arrived = lax.all_to_all(packed, ("gy", "gz"), 0, 0, tiled=True)
 
-    state_now = state.astype(jnp.float32)
-    diffuse = diffusivity.astype(jnp.float32)[None]
-    state_halo = faces(state, sides)
-    section_one = state_now + primal_step * (
-        diffuse * laplace_halo(state_now, state_halo, dims) + couple(coupling, state_now)
-    )
-    section_halo = faces(section_one.astype(jnp.bfloat16), sides)
-    residual = (
-        diffuse * laplace_halo(section_one, section_halo, dims)
-        + couple(coupling, section_one)
-        - (section_one - state_now) / primal_step
-    )
-    effective = (diffuse[0] * (1.0 + 0.5 * jnp.tanh(section_one[0]))).astype(jnp.bfloat16)
+    f32, bf16 = jnp.float32, jnp.bfloat16
+    nf, nx, ny, nz = state.shape
+    vmem = pl.BlockSpec(memory_space=pltpu.VMEM)
+    smem = pl.BlockSpec(memory_space=pltpu.SMEM)
+    face_shapes = [(nf, 1, ny, nz)] * 2 + [(nf, nx, 1, nz)] * 2 + [(nf, nx, ny, 1)] * 2
+    state_halo = [h for pair in faces(state, sides) for h in pair]
+    primal = pl.pallas_call(
+        primal_kernel,
+        out_shape=[jax.ShapeDtypeStruct(state.shape, f32), jax.ShapeDtypeStruct((nx, ny, nz), bf16)]
+        + [jax.ShapeDtypeStruct(shape, bf16) for shape in face_shapes],
+        in_specs=[smem] + [vmem] * 8,
+        out_specs=[vmem] * 8,
+    )(coupling, state, diffusivity, *state_halo)
+    section_one, effective = primal[0], primal[1]
+    section_halo = []
+    for (axis, _), low, high in zip(sides, primal[2::2], primal[3::2]):
+        ends = lax.axis_size(axis) - 1
+        section_halo.append(lax.ppermute(high, axis, [(i, i + 1) for i in range(ends)]))
+        section_halo.append(lax.ppermute(low, axis, [(i + 1, i) for i in range(ends)]))
 
     targets = owner[:, 0]
     order = jnp.arange(targets.shape[0], dtype=jnp.int32)
@@ -148,19 +280,18 @@
     slot_of = targets * capacity + rank
 
     mine = arrived[slot_of]
-    goal = to_cells(mine[:, :, : BX * BY].reshape(-1, FIELDS, BX, BY, BZ)).astype(jnp.float32)
-    react = per_block_cells(mine[:, :, BX * BY, 0]).astype(jnp.float32)
-    eff = effective.astype(jnp.float32)[None]
-    transposed = coupling.T
-    dual = goal
-    for _ in range(SECTIONS):
-        dual = dual + dual_step * (
-            eff * laplace_blocks(dual) + couple(transposed, dual) - react * dual + goal
-        )
-    enriched = (dual + 0.125 * laplace_blocks(dual)).astype(jnp.bfloat16)
+    goal = to_cells(mine[:, :, : BX * BY].reshape(-1, FIELDS, BX, BY, BZ))
+    react = per_block_cells(mine[:, :, BX * BY, 0])
+    enriched, part = pl.pallas_call(
+        adjoint_kernel,
+        out_shape=[jax.ShapeDtypeStruct(state.shape, bf16), jax.ShapeDtypeStruct((nx // BX, ny, nz), f32)],
+        in_specs=[smem] + [vmem] * 12,
+        out_specs=[vmem] * 2,
+    )(coupling, section_one, state, diffusivity, *section_halo, effective, goal, react)
+    sums = jnp.sum(part.reshape(nx // BX, ny // BY, BY, nz // BZ, BZ), axis=(2, 4)).reshape(-1)
 
     weights = jnp.exp2(2.0 * levels.astype(jnp.float32))
-    indicator = weights * block_sums(jnp.abs(residual * enriched.astype(jnp.float32)))
+    indicator = weights * sums
     overall = global_sum(jnp.sum(indicator))
     block_count = owner.shape[0] * lax.axis_size("gx") * lax.axis_size("gy") * lax.axis_size("gz")
     share = indicator * block_count / overall

time: 141 us -> 126 us (0.89)
  other arithmetic: 26.4 us -> 6.31 us
  local copies, waits for them, and re-layouts: 23.6 us -> 10.4 us
  waiting for transfers between devices: 19.3 us -> 32.4 us
  Pallas kernels: 0 us -> 7.9 us
  starting transfers between devices: 69.1 us -> 66.2 us
    ppermute x0 -> x6, starting transfers between devices: none -> 15.3 us  [the longest x3 10.8 us: shards(): lax.ppermute(high, axis, [(i, i + 1) for i in range(ends)])]
    slice x22 -> x3, local copies, waits for them, and re-layouts: 15.1 us -> 0.36 us  [the longest x2 0.27 us: shards(): react = per_block_cells(mine[:, :, BX * BY, 0])]
    ppermute x6 -> x3, starting transfers between devices: 23 us -> 11.2 us  [faces(): below = lax.ppermute(tail, axis, [(i, i + 1) for i in range(ends)])]
    convert_element_type x18 -> x0, other arithmetic: 11.3 us -> none  [the longest x12 7.6 us: laplace_halo(): minus, plus = shifted(v, dim, below.astype(v.dtype), above.astype(v.dtype))]
    pallas_call x0 -> x2, Pallas kernels: none -> 7.9 us  [the longest x1 4.86 us: shards(): pl.pallas_call(adjoint_kernel, out_shape=[jax.ShapeDtypeStruct(state.shap...]
    ppermute x6 -> x3, waiting for transfers between devices: 0.02 us -> 6.41 us  [faces(): below = lax.ppermute(tail, axis, [(i, i + 1) for i in range(ends)])]
    ppermute x6 -> x3, starting transfers between devices: 10.1 us -> 4.49 us  [faces(): above = lax.ppermute(head, axis, [(i + 1, i) for i in range(ends)])]
    ppermute x6 -> x3, waiting for transfers between devices: 4.07 us -> 8.78 us  [faces(): above = lax.ppermute(head, axis, [(i + 1, i) for i in range(ends)])]
  transfers between devices with their start and end apart: 15 -> 15, of which waited for: 4 -> 8; matrix products, arithmetic and copies ran while one was open for 18% -> 3% of each run, Pallas kernels for 0% -> 2%
where the time goes in v3:
time: 126 us; the launch traced here: 125 us
  starting transfers between devices  66.2 us (53%)
  waiting for transfers between devices  32.4 us (26%)
  local copies, waits for them, and re-layouts  10.4 us (8%)
  Pallas kernels  7.9 us (6%)
  other arithmetic  6.31 us (5%)
  between operations  1.6 us (1%)
    all_to_all x2, starting transfers between devices, global_sum(): x = jnp.sum(lax.all_to_all(spread, group, 0, 0, tiled=True))  23.5 us
    all_to_all x2, waiting for transfers between devices, global_sum(): x = jnp.sum(lax.all_to_all(spread, group, 0, 0, tiled=True))  15.3 us
    all_to_all x1, starting transfers between devices, shards(): arrived = lax.all_to_all(packed, ('gy', 'gz'), 0, 0, tiled=True)  11.8 us
    ppermute x3, starting transfers between devices, faces(): below = lax.ppermute(tail, axis, [(i, i + 1) for i in range(ends)])  11.2 us
    ppermute x3, starting transfers between devices, shards(): lax.ppermute(high, axis, [(i, i + 1) for i in range(ends)])  10.8 us
    ppermute x3, waiting for transfers between devices, faces(): above = lax.ppermute(head, axis, [(i + 1, i) for i in range(ends)])  8.78 us
    ppermute x3, waiting for transfers between devices, faces(): below = lax.ppermute(tail, axis, [(i, i + 1) for i in range(ends)])  6.41 us
    pallas_call x1, Pallas kernels, shards(): pl.pallas_call(adjoint_kernel, out_shape=[jax.ShapeDtypeStruct(state.shap...  4.86 us
  transfers between devices with their start and end apart: 15, of which 8 were waited for; matrix products, arithmetic and copies ran while one was open for 3% of the time, Pallas kernels for 2%

profile of v3, /device:TPU:1, one launch (start us, length us, event | category | flops | bytes accessed | tf_op | source)
XLA Modules:
  0.0 124.8 jit_solution(6183671228470909563)
XLA Ops:
  2.3 2.8 %pad_maximum_fusion = bf16[128,5,5,128]{3,2,1,0:T(8,128)(2,1)} fusion(bf16[128,5,1,128]{3,2,1,0:T(2,128)(2,1)S(1)} %broadcast_in_dim.8, bf16[128,5,4,128]{3,2,1,0:T(4,128)(2,1)} %bitcast.16), kind=kLoop, calls=%fused_computation.1 | loop fusion | flops 1638400 | bytes 1638400 | tf_op jit(solution)/shard_map/concatenate | solution.py:245
  5.1 11.8 %all-to-all-start = ((bf16[128,5,5,128]{3,2,1,0:T(8,128)(2,1)}), bf16[128,5,5,128]{3,2,1,0:T(8,128)(2,1)S(1)}, u32[]{:S(2)}, u32[]{:S(2)}) async-start(bf16[128,5,5,128]{3,2,1,0:T(8,128)(2,1)} %pad_maximum_fusion), calls=%async_computation | async-start | bytes 2621440 | tf_op jit(solution)/shard_map/all_to_all | solution.py:252
  16.9 4.0 %collective-permute-start = (bf16[5,1,8,768]{3,2,1,0:T(8,128)(2,1)S(1)}, bf16[5,1,8,768]{3,2,1,0:T(8,128)(2,1)S(1)}, u32[]{:S(2)}, u32[]{:S(2)}) collective-permute-start(bf16[5,1,8,768]{3,2,1,0:T(8,128)(2,1)S(1)} %get-tuple-element.28), channel_id=1, source_target_pairs={{0,64},{64,128},{128,192},{192,256},{256,320},{320,384},{384,448},... | collective-permute-start | bytes 184328 | tf_op jit(solution)/shard_map/ppermute | solution.py:31
  20.9 1.3 %collective-permute-start.1 = (bf16[5,1,8,768]{3,2,1,0:T(8,128)(2,1)S(1)}, bf16[5,1,8,768]{3,2,1,0:T(8,128)(2,1)S(1)}, u32[]{:S(2)}, u32[]{:S(2)}) collective-permute-start(bf16[5,1,8,768]{3,2,1,0:T(8,128)(2,1)S(1)} %get-tuple-element.27), channel_id=1, source_target_pairs={{64,0},{128,64},{192,128},{256,192},{320,256},{384,320},{448,384},... | collective-permute-start | bytes 184328 | tf_op jit(solution)/shard_map/ppermute | solution.py:32
  22.3 3.3 %collective-permute-start.2 = (bf16[5,4,1,768]{3,2,1,0:T(2,128)(2,1)S(1)}, bf16[5,4,1,768]{3,2,1,0:T(2,128)(2,1)S(1)}, u32[]{:S(2)}, u32[]{:S(2)}) collective-permute-start(bf16[5,4,1,768]{3,2,1,0:T(2,128)(2,1)S(1)} %get-tuple-element.26), channel_id=1, source_target_pairs={{0,8},{8,16},{16,24},{24,32},{32,40},{40,48},{48,56},{1,9},{9,17},... | collective-permute-start | bytes 92168 | tf_op jit(solution)/shard_map/ppermute | solution.py:31
  25.6 1.3 %collective-permute-start.3 = (bf16[5,4,1,768]{3,2,1,0:T(2,128)(2,1)S(1)}, bf16[5,4,1,768]{3,2,1,0:T(2,128)(2,1)S(1)}, u32[]{:S(2)}, u32[]{:S(2)}) collective-permute-start(bf16[5,4,1,768]{3,2,1,0:T(2,128)(2,1)S(1)} %get-tuple-element.25), channel_id=1, source_target_pairs={{8,0},{16,8},{24,16},{32,24},{40,32},{48,40},{56,48},{9,1},{17,9},... | collective-permute-start | bytes 92168 | tf_op jit(solution)/shard_map/ppermute | solution.py:32
  27.0 3.9 %collective-permute-start.4 = (bf16[5,4,8,1]{3,2,1,0:T(8,128)(2,1)S(1)}, bf16[5,4,8,1]{3,2,1,0:T(8,128)(2,1)S(1)}, u32[]{:S(2)}, u32[]{:S(2)}) collective-permute-start(bf16[5,4,8,1]{3,2,1,0:T(8,128)(2,1)S(1)} %get-tuple-element.24), channel_id=1, source_target_pairs={{0,1},{1,2},{2,3},{3,4},{4,5},{5,6},{6,7},{8,9},{9,10},{10,11},{11... | collective-permute-start | bytes 968 | tf_op jit(solution)/shard_map/ppermute | solution.py:31
  32.0 1.9 %collective-permute-start.5 = (bf16[5,4,8,1]{3,2,1,0:T(8,128)(2,1)S(1)}, bf16[5,4,8,1]{3,2,1,0:T(8,128)(2,1)S(1)}, u32[]{:S(2)}, u32[]{:S(2)}) collective-permute-start(bf16[5,4,8,1]{3,2,1,0:T(8,128)(2,1)S(1)} %get-tuple-element.23), channel_id=1, source_target_pairs={{1,0},{2,1},{3,2},{4,3},{5,4},{6,5},{7,6},{9,8},{10,9},{11,10},{12... | collective-permute-start | bytes 968 | tf_op jit(solution)/shard_map/ppermute | solution.py:32
  33.9 4.6 %collective-permute-done.5.zhi = bf16[5,4,8,1]{3,2,1,0:T(8,128)(2,1)S(1)} collective-permute-done((bf16[5,4,8,1]{3,2,1,0:T(8,128)(2,1)S(1)}, bf16[5,4,8,1]{3,2,1,0:T(8,128)(2,1)S(1)}, u32[]{:S(2)}, u32[]{:S(2)}) %collective-permute-start.5) | collective-permute-done | bytes 352 | tf_op jit(solution)/shard_map/ppermute | solution.py:32
  38.5 5.5 %collective-permute-done.2.ylo = bf16[5,4,1,768]{3,2,1,0:T(2,128)(2,1)S(1)} collective-permute-done((bf16[5,4,1,768]{3,2,1,0:T(2,128)(2,1)S(1)}, bf16[5,4,1,768]{3,2,1,0:T(2,128)(2,1)S(1)}, u32[]{:S(2)}, u32[]{:S(2)}) %collective-permute-start.2) | collective-permute-done | bytes 30752 | tf_op jit(solution)/shard_map/ppermute | solution.py:31
  44.1 4.1 %collective-permute-done.3.yhi = bf16[5,4,1,768]{3,2,1,0:T(2,128)(2,1)S(1)} collective-permute-done((bf16[5,4,1,768]{3,2,1,0:T(2,128)(2,1)S(1)}, bf16[5,4,1,768]{3,2,1,0:T(2,128)(2,1)S(1)}, u32[]{:S(2)}, u32[]{:S(2)}) %collective-permute-start.3) | collective-permute-done | bytes 30752 | tf_op jit(solution)/shard_map/ppermute | solution.py:32
  49.5 3.0 %shard_map.103 = (f32[5,4,8,768]{3,2,1,0:T(8,128)}, bf16[4,8,768]{2,1,0:T(8,128)(2,1)}, bf16[5,1,8,768]{3,2,1,0:T(8,128)(2,1)}, bf16[5,1,8,768]{3,2,1,0:T(8,128)...) custom-call(f32[5,5]{1,0:T(8,128)} %c_ref.3, ...), custom_call_target="tpu_custom_call" | custom-call | tf_op jit(solution)/shard_map/pallas_call | solution.py:260
  52.5 4.1 %collective-permute-start.6 = (bf16[5,1,8,768]{3,2,1,0:T(8,128)(2,1)}, bf16[5,1,8,768]{3,2,1,0:T(8,128)(2,1)S(1)}, u32[]{:S(2)}, u32[]{:S(2)}) collective-permute-start(bf16[5,1,8,768]{3,2,1,0:T(8,128)(2,1)} %get-tuple-element.14), channel_id=1, source_target_pairs={{0,64},{64,128},{128,192},{192,256},{256,320},{320,384},{384,448},... | collective-permute-start | bytes 184328 | tf_op jit(solution)/shard_map/ppermute | solution.py:271
  56.7 1.3 %collective-permute-start.7 = (bf16[5,1,8,768]{3,2,1,0:T(8,128)(2,1)}, bf16[5,1,8,768]{3,2,1,0:T(8,128)(2,1)S(1)}, u32[]{:S(2)}, u32[]{:S(2)}) collective-permute-start(bf16[5,1,8,768]{3,2,1,0:T(8,128)(2,1)} %get-tuple-element.15), channel_id=1, source_target_pairs={{64,0},{128,64},{192,128},{256,192},{320,256},{384,320},{448,384},... | collective-permute-start | bytes 184328 | tf_op jit(solution)/shard_map/ppermute | solution.py:272
  58.0 2.2 %collective-permute-start.8 = (bf16[5,4,1,768]{3,2,1,0:T(2,128)(2,1)}, bf16[5,4,1,768]{3,2,1,0:T(2,128)(2,1)S(1)}, u32[]{:S(2)}, u32[]{:S(2)}) collective-permute-start(bf16[5,4,1,768]{3,2,1,0:T(2,128)(2,1)} %get-tuple-element.16), channel_id=1, source_target_pairs={{0,8},{8,16},{16,24},{24,32},{32,40},{40,48},{48,56},{1,9},{9,17},... | collective-permute-start | bytes 92168 | tf_op jit(solution)/shard_map/ppermute | solution.py:271
  60.2 1.3 %collective-permute-start.9 = (bf16[5,4,1,768]{3,2,1,0:T(2,128)(2,1)}, bf16[5,4,1,768]{3,2,1,0:T(2,128)(2,1)S(1)}, u32[]{:S(2)}, u32[]{:S(2)}) collective-permute-start(bf16[5,4,1,768]{3,2,1,0:T(2,128)(2,1)} %get-tuple-element.17), channel_id=1, source_target_pairs={{8,0},{16,8},{24,16},{32,24},{40,32},{48,40},{56,48},{9,1},{17,9},... | collective-permute-start | bytes 92168 | tf_op jit(solution)/shard_map/ppermute | solution.py:272
  61.5 4.5 %collective-permute-start.10 = (bf16[5,4,8,1]{3,2,1,0:T(8,128)(2,1)}, bf16[5,4,8,1]{3,2,1,0:T(8,128)(2,1)S(1)}, u32[]{:S(2)}, u32[]{:S(2)}) collective-permute-start(bf16[5,4,8,1]{3,2,1,0:T(8,128)(2,1)} %get-tuple-element.18), channel_id=1, source_target_pairs={{0,1},{1,2},{2,3},{3,4},{4,5},{5,6},{6,7},{8,9},{9,10},{10,11},{11... | collective-permute-start | bytes 968 | tf_op jit(solution)/shard_map/ppermute | solution.py:271
  67.4 1.9 %collective-permute-start.11 = (bf16[5,4,8,1]{3,2,1,0:T(8,128)(2,1)S(1)}, bf16[5,4,8,1]{3,2,1,0:T(8,128)(2,1)S(1)}, u32[]{:S(2)}, u32[]{:S(2)}) collective-permute-start(bf16[5,4,8,1]{3,2,1,0:T(8,128)(2,1)S(1)} %copy-done.14), channel_id=1, source_target_pairs={{1,0},{2,1},{3,2},{4,3},{5,4},{6,5},{7,6},{9,8},{10,9},{11,10},{12... | collective-permute-start | bytes 968 | tf_op jit(solution)/shard_map/ppermute | solution.py:272
  71.7 1.5 %collective-permute-done.11.zhi = bf16[5,4,8,1]{3,2,1,0:T(8,128)(2,1)S(1)} collective-permute-done((bf16[5,4,8,1]{3,2,1,0:T(8,128)(2,1)S(1)}, bf16[5,4,8,1]{3,2,1,0:T(8,128)(2,1)S(1)}, u32[]{:S(2)}, u32[]{:S(2)}) %collective-permute-start.11) | collective-permute-done | bytes 352 | tf_op jit(solution)/shard_map/ppermute | solution.py:272
  73.9 4.9 %shard_map.104 = (bf16[5,4,8,768]{3,2,1,0:T(8,128)(2,1)}, f32[2,8,768]{2,1,0:T(8,128)}) custom-call(f32[5,5]{1,0:T(8,128)} %c_ref.3, f32[5,4,8,768]{3,2,1,0:T(8,128)} %get-tuple-element.13.s1_ref, bf16[5,4,8,768]{3,2,1,0:T(8,128)(2,1)} %s_ref.3, bf16[4,8,768]{2,1,0:T(8,128)(2,1)} %d_ref.3, bf16[5,1,8,768]{3,2,1,0:T(8,128)(2,1)} %copy-done.1, ...), custom_call_target="tpu_custom_call" | custom-call | tf_op jit(solution)/shard_map/pallas_call | solution.py:285
  81.6 12.0 %all-to-all-start.1 = ((f32[64,1,1]{2,1,0:T(1,128)}), f32[64,1,1]{2,1,0:T(1,128)S(1)}, u32[]{:S(2)}, u32[]{:S(2)}) async-start(f32[64,1,1]{2,1,0:T(1,128)} %broadcast_in_dim.10), calls=%async_computation.1 | async-start | bytes 65536 | tf_op jit(solution)/shard_map/all_to_all | solution.py:81
  94.3 8.7 %all-to-all-done.1 = f32[64,1,1]{2,1,0:T(1,128)S(1)} async-done(((f32[64,1,1]{2,1,0:T(1,128)}), f32[64,1,1]{2,1,0:T(1,128)S(1)}, u32[]{:S(2)}, u32[]{:S(2)}) %all-to-all-start.1) | async-done | bytes 288 | tf_op jit(solution)/shard_map/all_to_all | solution.py:81
  104.9 11.5 %all-to-all-start.2 = ((f32[8,1,1]{2,1,0:T(1,128)}), f32[8,1,1]{2,1,0:T(1,128)S(1)}, u32[]{:S(2)}, u32[]{:S(2)}) async-start(f32[8,1,1]{2,1,0:T(1,128)} %broadcast_in_dim.11), calls=%async_computation.2 | async-start | bytes 8192 | tf_op jit(solution)/shard_map/all_to_all | solution.py:81
  116.4 6.5 %all-to-all-done.2 = f32[8,1,1]{2,1,0:T(1,128)S(1)} async-done(((f32[8,1,1]{2,1,0:T(1,128)}), f32[8,1,1]{2,1,0:T(1,128)S(1)}, u32[]{:S(2)}, u32[]{:S(2)}) %all-to-all-start.2) | async-done | bytes 64 | tf_op jit(solution)/shard_map/all_to_all | solution.py:81
  (67 shorter events, 15.2 us)
Async XLA Ops:
  5.1 11.8 %copy-start = (bf16[5,4,8,768]{3,2,1,0:T(8,128)(2,1)S(1)}, bf16[5,4,8,768]{3,2,1,0:T(8,128)(2,1)}, u32[]{:S(2)}) copy-start(bf16[5,4,8,768]{3,2,1,0:T(8,128)(2,1)} %s_ref.3) | copy-start | bytes 737284
  5.1 25.8 %copy-start.15 = (s32[48,1]{0,1:T(1,128)S(1)}, s32[48,1]{0,1:T(1,128)}, u32[]{:S(2)}) copy-start(s32[48,1]{0,1:T(1,128)} %param.11) | copy-start | bytes 580
  5.1 60.9 %all-to-all-start = ((bf16[128,5,5,128]{3,2,1,0:T(8,128)(2,1)}), bf16[128,5,5,128]{3,2,1,0:T(8,128)(2,1)S(1)}, u32[]{:S(2)}, u32[]{:S(2)}) async-start(bf16[128,5,5,128]{3,2,1,0:T(8,128)(2,1)} %pad_maximum_fusion), calls=%async_computation | async-start | bytes 2621440 | tf_op jit(solution)/shard_map/all_to_all | solution.py:252
  16.9 31.3 %collective-permute-start = (bf16[5,1,8,768]{3,2,1,0:T(8,128)(2,1)S(1)}, bf16[5,1,8,768]{3,2,1,0:T(8,128)(2,1)S(1)}, u32[]{:S(2)}, u32[]{:S(2)}) collective-permute-start(bf16[5,1,8,768]{3,2,1,0:T(8,128)(2,1)S(1)} %get-tuple-element.28), channel_id=1, source_target_pairs={{0,64},{64,128},{128,192},{192,256},{256,320},{320,384},{384,448},... | collective-permute-start | bytes 184328 | tf_op jit(solution)/shard_map/ppermute | solution.py:31
  20.9 27.3 %collective-permute-start.1 = (bf16[5,1,8,768]{3,2,1,0:T(8,128)(2,1)S(1)}, bf16[5,1,8,768]{3,2,1,0:T(8,128)(2,1)S(1)}, u32[]{:S(2)}, u32[]{:S(2)}) collective-permute-start(bf16[5,1,8,768]{3,2,1,0:T(8,128)(2,1)S(1)} %get-tuple-element.27), channel_id=1, source_target_pairs={{64,0},{128,64},{192,128},{256,192},{320,256},{384,320},{448,384},... | collective-permute-start | bytes 184328 | tf_op jit(solution)/shard_map/ppermute | solution.py:32
  22.3 21.7 %collective-permute-start.2 = (bf16[5,4,1,768]{3,2,1,0:T(2,128)(2,1)S(1)}, bf16[5,4,1,768]{3,2,1,0:T(2,128)(2,1)S(1)}, u32[]{:S(2)}, u32[]{:S(2)}) collective-permute-start(bf16[5,4,1,768]{3,2,1,0:T(2,128)(2,1)S(1)} %get-tuple-element.26), channel_id=1, source_target_pairs={{0,8},{8,16},{16,24},{24,32},{32,40},{40,48},{48,56},{1,9},{9,17},... | collective-permute-start | bytes 92168 | tf_op jit(solution)/shard_map/ppermute | solution.py:31
  25.6 22.6 %collective-permute-start.3 = (bf16[5,4,1,768]{3,2,1,0:T(2,128)(2,1)S(1)}, bf16[5,4,1,768]{3,2,1,0:T(2,128)(2,1)S(1)}, u32[]{:S(2)}, u32[]{:S(2)}) collective-permute-start(bf16[5,4,1,768]{3,2,1,0:T(2,128)(2,1)S(1)} %get-tuple-element.25), channel_id=1, source_target_pairs={{8,0},{16,8},{24,16},{32,24},{40,32},{48,40},{56,48},{9,1},{17,9},... | collective-permute-start | bytes 92168 | tf_op jit(solution)/shard_map/ppermute | solution.py:32
  27.0 5.0 %collective-permute-start.4 = (bf16[5,4,8,1]{3,2,1,0:T(8,128)(2,1)S(1)}, bf16[5,4,8,1]{3,2,1,0:T(8,128)(2,1)S(1)}, u32[]{:S(2)}, u32[]{:S(2)}) collective-permute-start(bf16[5,4,8,1]{3,2,1,0:T(8,128)(2,1)S(1)} %get-tuple-element.24), channel_id=1, source_target_pairs={{0,1},{1,2},{2,3},{3,4},{4,5},{5,6},{6,7},{8,9},{9,10},{10,11},{11... | collective-permute-start | bytes 968 | tf_op jit(solution)/shard_map/ppermute | solution.py:31
  32.0 16.2 %copy-start.10 = (bf16[5,4,8,1]{3,2,1,0:T(8,128)(2,1)}, bf16[5,4,8,1]{3,2,1,0:T(8,128)(2,1)S(1)}, u32[]{:S(2)}) copy-start(bf16[5,4,8,1]{3,2,1,0:T(8,128)(2,1)S(1)} %collective-permute-done.4.zlo) | copy-start | bytes 964
  32.0 6.6 %collective-permute-start.5 = (bf16[5,4,8,1]{3,2,1,0:T(8,128)(2,1)S(1)}, bf16[5,4,8,1]{3,2,1,0:T(8,128)(2,1)S(1)}, u32[]{:S(2)}, u32[]{:S(2)}) collective-permute-start(bf16[5,4,8,1]{3,2,1,0:T(8,128)(2,1)S(1)} %get-tuple-element.23), channel_id=1, source_target_pairs={{1,0},{2,1},{3,2},{4,3},{5,4},{6,5},{7,6},{9,8},{10,9},{11,10},{12... | collective-permute-start | bytes 968 | tf_op jit(solution)/shard_map/ppermute | solution.py:32
  38.5 9.7 %copy-start.12 = (bf16[5,4,8,1]{3,2,1,0:T(8,128)(2,1)}, bf16[5,4,8,1]{3,2,1,0:T(8,128)(2,1)S(1)}, u32[]{:S(2)}) copy-start(bf16[5,4,8,1]{3,2,1,0:T(8,128)(2,1)S(1)} %collective-permute-done.5.zhi) | copy-start | bytes 964
  44.1 4.2 %copy-start.7 = (bf16[5,4,1,768]{3,2,1,0:T(2,128)(2,1)}, bf16[5,4,1,768]{3,2,1,0:T(2,128)(2,1)S(1)}, u32[]{:S(2)}) copy-start(bf16[5,4,1,768]{3,2,1,0:T(2,128)(2,1)S(1)} %collective-permute-done.2.ylo) | copy-start | bytes 92164
  52.5 14.9 %copy-start.14 = (bf16[5,4,8,1]{3,2,1,0:T(8,128)(2,1)S(1)}, bf16[5,4,8,1]{3,2,1,0:T(8,128)(2,1)}, u32[]{:S(2)}) copy-start(bf16[5,4,8,1]{3,2,1,0:T(8,128)(2,1)} %get-tuple-element.19) | copy-start | bytes 964
  52.5 20.7 %collective-permute-start.6 = (bf16[5,1,8,768]{3,2,1,0:T(8,128)(2,1)}, bf16[5,1,8,768]{3,2,1,0:T(8,128)(2,1)S(1)}, u32[]{:S(2)}, u32[]{:S(2)}) collective-permute-start(bf16[5,1,8,768]{3,2,1,0:T(8,128)(2,1)} %get-tuple-element.14), channel_id=1, source_target_pairs={{0,64},{64,128},{128,192},{192,256},{256,320},{320,384},{384,448},... | collective-permute-start | bytes 184328 | tf_op jit(solution)/shard_map/ppermute | solution.py:271
  56.7 16.6 %collective-permute-start.7 = (bf16[5,1,8,768]{3,2,1,0:T(8,128)(2,1)}, bf16[5,1,8,768]{3,2,1,0:T(8,128)(2,1)S(1)}, u32[]{:S(2)}, u32[]{:S(2)}) collective-permute-start(bf16[5,1,8,768]{3,2,1,0:T(8,128)(2,1)} %get-tuple-element.15), channel_id=1, source_target_pairs={{64,0},{128,64},{192,128},{256,192},{320,256},{384,320},{448,384},... | collective-permute-start | bytes 184328 | tf_op jit(solution)/shard_map/ppermute | solution.py:272
  58.0 15.2 %collective-permute-start.8 = (bf16[5,4,1,768]{3,2,1,0:T(2,128)(2,1)}, bf16[5,4,1,768]{3,2,1,0:T(2,128)(2,1)S(1)}, u32[]{:S(2)}, u32[]{:S(2)}) collective-permute-start(bf16[5,4,1,768]{3,2,1,0:T(2,128)(2,1)} %get-tuple-element.16), channel_id=1, source_target_pairs={{0,8},{8,16},{16,24},{24,32},{32,40},{40,48},{48,56},{1,9},{9,17},... | collective-permute-start | bytes 92168 | tf_op jit(solution)/shard_map/ppermute | solution.py:271
  60.2 13.0 %collective-permute-start.9 = (bf16[5,4,1,768]{3,2,1,0:T(2,128)(2,1)}, bf16[5,4,1,768]{3,2,1,0:T(2,128)(2,1)S(1)}, u32[]{:S(2)}, u32[]{:S(2)}) collective-permute-start(bf16[5,4,1,768]{3,2,1,0:T(2,128)(2,1)} %get-tuple-element.17), channel_id=1, source_target_pairs={{8,0},{16,8},{24,16},{32,24},{40,32},{48,40},{56,48},{9,1},{17,9},... | collective-permute-start | bytes 92168 | tf_op jit(solution)/shard_map/ppermute | solution.py:272
  61.5 5.9 %collective-permute-start.10 = (bf16[5,4,8,1]{3,2,1,0:T(8,128)(2,1)}, bf16[5,4,8,1]{3,2,1,0:T(8,128)(2,1)S(1)}, u32[]{:S(2)}, u32[]{:S(2)}) collective-permute-start(bf16[5,4,8,1]{3,2,1,0:T(8,128)(2,1)} %get-tuple-element.18), channel_id=1, source_target_pairs={{0,1},{1,2},{2,3},{3,4},{4,5},{5,6},{6,7},{8,9},{9,10},{10,11},{11... | collective-permute-start | bytes 968 | tf_op jit(solution)/shard_map/ppermute | solution.py:271
  67.4 5.9 %copy-start.9 = (bf16[5,4,8,1]{3,2,1,0:T(8,128)(2,1)}, bf16[5,4,8,1]{3,2,1,0:T(8,128)(2,1)S(1)}, u32[]{:S(2)}) copy-start(bf16[5,4,8,1]{3,2,1,0:T(8,128)(2,1)S(1)} %collective-permute-done.10.zlo) | copy-start | bytes 964
  67.4 5.8 %collective-permute-start.11 = (bf16[5,4,8,1]{3,2,1,0:T(8,128)(2,1)S(1)}, bf16[5,4,8,1]{3,2,1,0:T(8,128)(2,1)S(1)}, u32[]{:S(2)}, u32[]{:S(2)}) collective-permute-start(bf16[5,4,8,1]{3,2,1,0:T(8,128)(2,1)S(1)} %copy-done.14), channel_id=1, source_target_pairs={{1,0},{2,1},{3,2},{4,3},{5,4},{6,5},{7,6},{9,8},{10,9},{11,10},{12... | collective-permute-start | bytes 968 | tf_op jit(solution)/shard_map/ppermute | solution.py:272
  70.5 9.2 %copy-start.13 = (s32[48]{0:T(128)S(1)}, s32[48]{0:T(128)}, u32[]{:S(2)}) copy-start(s32[48]{0:T(128)} %param.12) | copy-start | bytes 580
  73.2 0.7 copy-start.4
  81.6 21.4 %all-to-all-start.1 = ((f32[64,1,1]{2,1,0:T(1,128)}), f32[64,1,1]{2,1,0:T(1,128)S(1)}, u32[]{:S(2)}, u32[]{:S(2)}) async-start(f32[64,1,1]{2,1,0:T(1,128)} %broadcast_in_dim.10), calls=%async_computation.1 | async-start | bytes 65536 | tf_op jit(solution)/shard_map/all_to_all | solution.py:81
  104.9 18.0 %all-to-all-start.2 = ((f32[8,1,1]{2,1,0:T(1,128)}), f32[8,1,1]{2,1,0:T(1,128)S(1)}, u32[]{:S(2)}, u32[]{:S(2)}) async-start(f32[8,1,1]{2,1,0:T(1,128)} %broadcast_in_dim.11), calls=%async_computation.2 | async-start | bytes 8192 | tf_op jit(solution)/shard_map/all_to_all | solution.py:81
  (7 other events, 4.4 us)

commit v4 on v3

--- a/solution.py
+++ b/solution.py
@@ -249,7 +249,6 @@
         ],
         axis=2,
     )
-    arrived = lax.all_to_all(packed, ("gy", "gz"), 0, 0, tiled=True)
 
     f32, bf16 = jnp.float32, jnp.bfloat16
     nf, nx, ny, nz = state.shape
@@ -257,6 +256,8 @@
     smem = pl.BlockSpec(memory_space=pltpu.SMEM)
     face_shapes = [(nf, 1, ny, nz)] * 2 + [(nf, nx, 1, nz)] * 2 + [(nf, nx, ny, 1)] * 2
     state_halo = [h for pair in faces(state, sides) for h in pair]
+    packed, *state_halo = lax.optimization_barrier((packed, *state_halo))
+    arrived = lax.all_to_all(packed, ("gy", "gz"), 0, 0, tiled=True)
     primal = pl.pallas_call(
         primal_kernel,
         out_shape=[jax.ShapeDtypeStruct(state.shape, f32), jax.ShapeDtypeStruct((nx, ny, nz), bf16)]

time: 126 us -> 122 us (0.968)
  starting transfers between devices: 66.2 us -> 59.6 us
  local copies, waits for them, and re-layouts: 10.4 us -> 12.6 us
  waiting for transfers between devices: 32.4 us -> 34 us
    all_to_all x1, waiting for transfers between devices: 0.01 us -> 17.8 us  [shards(): arrived = lax.all_to_all(packed, ('gy', 'gz'), 0, 0, tiled=True)]
    all_to_all x2, starting transfers between devices: 23.5 us -> 14.1 us  [global_sum(): x = jnp.sum(lax.all_to_all(spread, group, 0, 0, tiled=True))]
    ppermute x3, waiting for transfers between devices: 8.78 us -> 0.01 us  [faces(): above = lax.ppermute(head, axis, [(i + 1, i) for i in range(ends)])]
    ppermute x3, starting transfers between devices: 4.49 us -> 11.4 us  [faces(): above = lax.ppermute(head, axis, [(i + 1, i) for i in range(ends)])]
    ppermute x3, waiting for transfers between devices: 6.41 us -> 0.01 us  [faces(): below = lax.ppermute(tail, axis, [(i, i + 1) for i in range(ends)])]
    all_to_all x1, starting transfers between devices: 11.8 us -> 8.09 us  [shards(): arrived = lax.all_to_all(packed, ('gy', 'gz'), 0, 0, tiled=True)]
    slice x3, local copies, waits for them, and re-layouts: 0.18 us -> 2.98 us  [faces(): head = lax.slice_in_dim(cells, 0, 1, axis=dim)]
    ppermute x3, starting transfers between devices: 11.2 us -> 9.9 us  [faces(): below = lax.ppermute(tail, axis, [(i, i + 1) for i in range(ends)])]
  transfers between devices with their start and end apart: 15 -> 15, of which waited for: 8 -> 4; matrix products, arithmetic and copies ran while one was open for 3% -> 7% of each run, Pallas kernels for 2% -> 3%
where the time goes in v4:
time: 122 us; the launch traced here: 121 us
  starting transfers between devices  59.6 us (49%)
  waiting for transfers between devices  34 us (28%)
  local copies, waits for them, and re-layouts  12.6 us (10%)
  Pallas kernels  7.92 us (6%)
  other arithmetic  5.23 us (4%)
  between operations  1.64 us (1%)
    all_to_all x1, waiting for transfers between devices, shards(): arrived = lax.all_to_all(packed, ('gy', 'gz'), 0, 0, tiled=True)  17.8 us
    all_to_all x2, waiting for transfers between devices, global_sum(): x = jnp.sum(lax.all_to_all(spread, group, 0, 0, tiled=True))  15.3 us
    all_to_all x2, starting transfers between devices, global_sum(): x = jnp.sum(lax.all_to_all(spread, group, 0, 0, tiled=True))  14.1 us
    ppermute x3, starting transfers between devices, faces(): above = lax.ppermute(head, axis, [(i + 1, i) for i in range(ends)])  11.4 us
    ppermute x3, starting transfers between devices, shards(): lax.ppermute(high, axis, [(i, i + 1) for i in range(ends)])  11.3 us
    ppermute x3, starting transfers between devices, faces(): below = lax.ppermute(tail, axis, [(i, i + 1) for i in range(ends)])  9.9 us
    all_to_all x1, starting transfers between devices, shards(): arrived = lax.all_to_all(packed, ('gy', 'gz'), 0, 0, tiled=True)  8.09 us
    pallas_call x1, Pallas kernels, shards(): pl.pallas_call(adjoint_kernel, out_shape=[jax.ShapeDtypeStruct(state.shap...  4.86 us
  transfers between devices with their start and end apart: 15, of which 4 were waited for; matrix products, arithmetic and copies ran while one was open for 7% of the time, Pallas kernels for 3%

profile of v4, /device:TPU:1, one launch (start us, length us, event | category | flops | bytes accessed | tf_op | source)
XLA Modules:
  0.0 120.9 jit_solution(5135580155992195565)
XLA Ops:
  1.6 8.8 %collective-permute-start.5 = (bf16[5,4,8,1]{3,2,1,0:T(8,128)(2,1)S(1)}, bf16[5,4,8,1]{3,2,1,0:T(8,128)(2,1)S(1)}, u32[]{:S(2)}, u32[]{:S(2)}) collective-permute-start(bf16[5,4,8,1]{3,2,1,0:T(8,128)(2,1)S(1)} %get-tuple-element.37), channel_id=1, source_target_pairs={{1,0},{2,1},{3,2},{4,3},{5,4},{6,5},{7,6},{9,8},{10,9},{11,10},{12... | collective-permute-start | bytes 968 | tf_op jit(solution)/shard_map/ppermute | solution.py:32
  10.4 1.9 %collective-permute-start.4 = (bf16[5,4,8,1]{3,2,1,0:T(8,128)(2,1)S(1)}, bf16[5,4,8,1]{3,2,1,0:T(8,128)(2,1)S(1)}, u32[]{:S(2)}, u32[]{:S(2)}) collective-permute-start(bf16[5,4,8,1]{3,2,1,0:T(8,128)(2,1)S(1)} %get-tuple-element.38), channel_id=1, source_target_pairs={{0,1},{1,2},{2,3},{3,4},{4,5},{5,6},{6,7},{8,9},{9,10},{10,11},{11... | collective-permute-start | bytes 968 | tf_op jit(solution)/shard_map/ppermute | solution.py:31
  13.2 1.3 %collective-permute-start.1 = (bf16[5,1,8,768]{3,2,1,0:T(8,128)(2,1)S(1)}, bf16[5,1,8,768]{3,2,1,0:T(8,128)(2,1)S(1)}, u32[]{:S(2)}, u32[]{:S(2)}) collective-permute-start(bf16[5,1,8,768]{3,2,1,0:T(8,128)(2,1)S(1)} %get-tuple-element.41), channel_id=1, source_target_pairs={{64,0},{128,64},{192,128},{256,192},{320,256},{384,320},{448,384},... | collective-permute-start | bytes 184328 | tf_op jit(solution)/shard_map/ppermute | solution.py:32
  14.5 4.0 %collective-permute-start = (bf16[5,1,8,768]{3,2,1,0:T(8,128)(2,1)S(1)}, bf16[5,1,8,768]{3,2,1,0:T(8,128)(2,1)S(1)}, u32[]{:S(2)}, u32[]{:S(2)}) collective-permute-start(bf16[5,1,8,768]{3,2,1,0:T(8,128)(2,1)S(1)} %get-tuple-element.42), channel_id=1, source_target_pairs={{0,64},{64,128},{128,192},{192,256},{256,320},{320,384},{384,448},... | collective-permute-start | bytes 184328 | tf_op jit(solution)/shard_map/ppermute | solution.py:31
  19.6 1.3 %collective-permute-start.3 = (bf16[5,4,1,768]{3,2,1,0:T(2,128)(2,1)S(1)}, bf16[5,4,1,768]{3,2,1,0:T(2,128)(2,1)S(1)}, u32[]{:S(2)}, u32[]{:S(2)}) collective-permute-start(bf16[5,4,1,768]{3,2,1,0:T(2,128)(2,1)S(1)} %get-tuple-element.39), channel_id=1, source_target_pairs={{8,0},{16,8},{24,16},{32,24},{40,32},{48,40},{56,48},{9,1},{17,9},... | collective-permute-start | bytes 92168 | tf_op jit(solution)/shard_map/ppermute | solution.py:32
  21.8 4.0 %collective-permute-start.2 = (bf16[5,4,1,768]{3,2,1,0:T(2,128)(2,1)S(1)}, bf16[5,4,1,768]{3,2,1,0:T(2,128)(2,1)S(1)}, u32[]{:S(2)}, u32[]{:S(2)}) collective-permute-start(bf16[5,4,1,768]{3,2,1,0:T(2,128)(2,1)S(1)} %get-tuple-element.40), channel_id=1, source_target_pairs={{0,8},{8,16},{16,24},{24,32},{32,40},{40,48},{48,56},{1,9},{9,17},... | collective-permute-start | bytes 92168 | tf_op jit(solution)/shard_map/ppermute | solution.py:31
  26.6 1.7 %pad_maximum_fusion = bf16[128,5,5,128]{3,2,1,0:T(8,128)(2,1)} fusion(bf16[128,5,1,128]{3,2,1,0:T(2,128)(2,1)S(1)} %broadcast_in_dim.8, bf16[128,5,4,128]{3,2,1,0:T(4,128)(2,1)S(1)} %bitcast.16), kind=kLoop, calls=%fused_computation.1 | loop fusion | flops 1638400 | bytes 1638400 | tf_op jit(solution)/shard_map/concatenate | solution.py:245
  29.1 8.1 %all-to-all-start = ((bf16[128,5,5,128]{3,2,1,0:T(8,128)(2,1)}), bf16[128,5,5,128]{3,2,1,0:T(8,128)(2,1)S(1)}, u32[]{:S(2)}, u32[]{:S(2)}) async-start(bf16[128,5,5,128]{3,2,1,0:T(8,128)(2,1)} %pad_maximum_fusion), calls=%async_computation | async-start | bytes 2621440 | tf_op jit(solution)/shard_map/all_to_all | solution.py:260
  37.4 3.1 %shard_map.103 = (f32[5,4,8,768]{3,2,1,0:T(8,128)}, bf16[4,8,768]{2,1,0:T(8,128)(2,1)}, bf16[5,1,8,768]{3,2,1,0:T(8,128)(2,1)}, bf16[5,1,8,768]{3,2,1,0:T(8,128)...) custom-call(f32[5,5]{1,0:T(8,128)} %c_ref.3, ...), custom_call_target="tpu_custom_call" | custom-call | tf_op jit(solution)/shard_map/pallas_call | solution.py:261
  40.5 4.1 %collective-permute-start.6 = (bf16[5,1,8,768]{3,2,1,0:T(8,128)(2,1)}, bf16[5,1,8,768]{3,2,1,0:T(8,128)(2,1)S(1)}, u32[]{:S(2)}, u32[]{:S(2)}) collective-permute-start(bf16[5,1,8,768]{3,2,1,0:T(8,128)(2,1)} %get-tuple-element.27), channel_id=1, source_target_pairs={{0,64},{64,128},{128,192},{192,256},{256,320},{320,384},{384,448},... | collective-permute-start | bytes 184328 | tf_op jit(solution)/shard_map/ppermute | solution.py:272
  44.6 1.3 %collective-permute-start.7 = (bf16[5,1,8,768]{3,2,1,0:T(8,128)(2,1)}, bf16[5,1,8,768]{3,2,1,0:T(8,128)(2,1)S(1)}, u32[]{:S(2)}, u32[]{:S(2)}) collective-permute-start(bf16[5,1,8,768]{3,2,1,0:T(8,128)(2,1)} %get-tuple-element.28), channel_id=1, source_target_pairs={{64,0},{128,64},{192,128},{256,192},{320,256},{384,320},{448,384},... | collective-permute-start | bytes 184328 | tf_op jit(solution)/shard_map/ppermute | solution.py:273
  45.9 3.3 %collective-permute-start.8 = (bf16[5,4,1,768]{3,2,1,0:T(2,128)(2,1)}, bf16[5,4,1,768]{3,2,1,0:T(2,128)(2,1)S(1)}, u32[]{:S(2)}, u32[]{:S(2)}) collective-permute-start(bf16[5,4,1,768]{3,2,1,0:T(2,128)(2,1)} %get-tuple-element.29), channel_id=1, source_target_pairs={{0,8},{8,16},{16,24},{24,32},{32,40},{40,48},{48,56},{1,9},{9,17},... | collective-permute-start | bytes 92168 | tf_op jit(solution)/shard_map/ppermute | solution.py:272
  49.2 1.3 %collective-permute-start.9 = (bf16[5,4,1,768]{3,2,1,0:T(2,128)(2,1)}, bf16[5,4,1,768]{3,2,1,0:T(2,128)(2,1)S(1)}, u32[]{:S(2)}, u32[]{:S(2)}) collective-permute-start(bf16[5,4,1,768]{3,2,1,0:T(2,128)(2,1)} %get-tuple-element.30), channel_id=1, source_target_pairs={{8,0},{16,8},{24,16},{32,24},{40,32},{48,40},{56,48},{9,1},{17,9},... | collective-permute-start | bytes 92168 | tf_op jit(solution)/shard_map/ppermute | solution.py:273
  50.5 3.9 %collective-permute-start.10 = (bf16[5,4,8,1]{3,2,1,0:T(8,128)(2,1)}, bf16[5,4,8,1]{3,2,1,0:T(8,128)(2,1)S(1)}, u32[]{:S(2)}, u32[]{:S(2)}) collective-permute-start(bf16[5,4,8,1]{3,2,1,0:T(8,128)(2,1)} %get-tuple-element.31), channel_id=1, source_target_pairs={{0,1},{1,2},{2,3},{3,4},{4,5},{5,6},{6,7},{8,9},{9,10},{10,11},{11... | collective-permute-start | bytes 968 | tf_op jit(solution)/shard_map/ppermute | solution.py:272
  54.4 17.8 %all-to-all-done = bf16[128,5,5,128]{3,2,1,0:T(8,128)(2,1)S(1)} async-done(((bf16[128,5,5,128]{3,2,1,0:T(8,128)(2,1)}), bf16[128,5,5,128]{3,2,1,0:T(8,128)(2,1)S(1)}, u32[]{:S(2)}, u32[]{:S(2)}) %all-to-all-start) | async-done | bytes 819232 | tf_op jit(solution)/shard_map/all_to_all | solution.py:260
  73.4 2.2 %collective-permute-start.11 = (bf16[5,4,8,1]{3,2,1,0:T(8,128)(2,1)S(1)}, bf16[5,4,8,1]{3,2,1,0:T(8,128)(2,1)S(1)}, u32[]{:S(2)}, u32[]{:S(2)}) collective-permute-start(bf16[5,4,8,1]{3,2,1,0:T(8,128)(2,1)S(1)} %copy-done.14), channel_id=1, source_target_pairs={{1,0},{2,1},{3,2},{4,3},{5,4},{6,5},{7,6},{9,8},{10,9},{11,10},{12... | collective-permute-start | bytes 968 | tf_op jit(solution)/shard_map/ppermute | solution.py:273
  79.4 4.9 %shard_map.104 = (bf16[5,4,8,768]{3,2,1,0:T(8,128)(2,1)}, f32[2,8,768]{2,1,0:T(8,128)}) custom-call(f32[5,5]{1,0:T(8,128)} %c_ref.3, f32[5,4,8,768]{3,2,1,0:T(8,128)} %get-tuple-element.26.s1_ref, bf16[5,4,8,768]{3,2,1,0:T(8,128)(2,1)} %s_ref.3, bf16[4,8,768]{2,1,0:T(8,128)(2,1)} %d_ref.3, bf16[5,1,8,768]{3,2,1,0:T(8,128)(2,1)} %copy-done.1, ...), custom_call_target="tpu_custom_call" | custom-call | tf_op jit(solution)/shard_map/pallas_call | solution.py:286
  85.9 1.3 %broadcast_in_dim.10 = f32[64,1,1]{2,1,0:T(1,128)} broadcast(f32[]{:T(128)} %fusion.2), dimensions={} | broadcast | bytes 260 | tf_op jit(solution)/shard_map/broadcast_in_dim | solution.py:80
  87.2 4.6 %all-to-all-start.1 = ((f32[64,1,1]{2,1,0:T(1,128)}), f32[64,1,1]{2,1,0:T(1,128)S(1)}, u32[]{:S(2)}, u32[]{:S(2)}) async-start(f32[64,1,1]{2,1,0:T(1,128)} %broadcast_in_dim.10), calls=%async_computation.1 | async-start | bytes 65536 | tf_op jit(solution)/shard_map/all_to_all | solution.py:81
  92.4 8.7 %all-to-all-done.1 = f32[64,1,1]{2,1,0:T(1,128)S(1)} async-done(((f32[64,1,1]{2,1,0:T(1,128)}), f32[64,1,1]{2,1,0:T(1,128)S(1)}, u32[]{:S(2)}, u32[]{:S(2)}) %all-to-all-start.1) | async-done | bytes 288 | tf_op jit(solution)/shard_map/all_to_all | solution.py:81
  101.8 1.2 %broadcast_in_dim.11 = f32[8,1,1]{2,1,0:T(1,128)} broadcast(f32[]{:T(128)} %reduce_sum.51), dimensions={} | broadcast | bytes 36 | tf_op jit(solution)/shard_map/broadcast_in_dim | solution.py:80
  103.0 9.5 %all-to-all-start.2 = ((f32[8,1,1]{2,1,0:T(1,128)}), f32[8,1,1]{2,1,0:T(1,128)S(1)}, u32[]{:S(2)}, u32[]{:S(2)}) async-start(f32[8,1,1]{2,1,0:T(1,128)} %broadcast_in_dim.11), calls=%async_computation.2 | async-start | bytes 8192 | tf_op jit(solution)/shard_map/all_to_all | solution.py:81
  112.5 6.5 %all-to-all-done.2 = f32[8,1,1]{2,1,0:T(1,128)S(1)} async-done(((f32[8,1,1]{2,1,0:T(1,128)}), f32[8,1,1]{2,1,0:T(1,128)S(1)}, u32[]{:S(2)}, u32[]{:S(2)}) %all-to-all-start.2) | async-done | bytes 64 | tf_op jit(solution)/shard_map/all_to_all | solution.py:81
  119.7 1.2 %divide_minimum_fusion = (f32[48]{0:T(128)}, f32[48]{0:T(128)}) fusion(f32[]{:T(128)} %bitcast.7, f32[]{:T(128)} %reduce_sum.52, f32[48]{0:T(128)S(1)} %reshape.40, s32[48]{0:T(128)S(1)} %copy-done.13), kind=kLoop, calls=%fused_computation.9 | loop fusion | flops 384 | bytes 776 | tf_op jit(solution)/shard_map/min | solution.py:299
  (67 shorter events, 13.3 us)
Async XLA Ops:
  0.6 26.0 %copy-start = (bf16[128,5,2,2,128]{4,3,2,1,0:T(2,128)(2,1)S(1)}, bf16[128,5,2,2,128]{4,3,2,1,0:T(2,128)(2,1)}, u32[]{:S(2)}) copy-start(bf16[128,5,2,2,128]{4,3,2,1,0:T(2,128)(2,1)} %param.14) | copy-start | bytes 1966084
  1.6 20.2 %collective-permute-start.5 = (bf16[5,4,8,1]{3,2,1,0:T(8,128)(2,1)S(1)}, bf16[5,4,8,1]{3,2,1,0:T(8,128)(2,1)S(1)}, u32[]{:S(2)}, u32[]{:S(2)}) collective-permute-start(bf16[5,4,8,1]{3,2,1,0:T(8,128)(2,1)S(1)} %get-tuple-element.37), channel_id=1, source_target_pairs={{1,0},{2,1},{3,2},{4,3},{5,4},{6,5},{7,6},{9,8},{10,9},{11,10},{12... | collective-permute-start | bytes 968 | tf_op jit(solution)/shard_map/ppermute | solution.py:32
  10.4 18.0 %collective-permute-start.4 = (bf16[5,4,8,1]{3,2,1,0:T(8,128)(2,1)S(1)}, bf16[5,4,8,1]{3,2,1,0:T(8,128)(2,1)S(1)}, u32[]{:S(2)}, u32[]{:S(2)}) collective-permute-start(bf16[5,4,8,1]{3,2,1,0:T(8,128)(2,1)S(1)} %get-tuple-element.38), channel_id=1, source_target_pairs={{0,1},{1,2},{2,3},{3,4},{4,5},{5,6},{6,7},{8,9},{9,10},{10,11},{11... | collective-permute-start | bytes 968 | tf_op jit(solution)/shard_map/ppermute | solution.py:31
  13.2 15.3 %collective-permute-start.1 = (bf16[5,1,8,768]{3,2,1,0:T(8,128)(2,1)S(1)}, bf16[5,1,8,768]{3,2,1,0:T(8,128)(2,1)S(1)}, u32[]{:S(2)}, u32[]{:S(2)}) collective-permute-start(bf16[5,1,8,768]{3,2,1,0:T(8,128)(2,1)S(1)} %get-tuple-element.41), channel_id=1, source_target_pairs={{64,0},{128,64},{192,128},{256,192},{320,256},{384,320},{448,384},... | collective-permute-start | bytes 184328 | tf_op jit(solution)/shard_map/ppermute | solution.py:32
  14.5 14.0 %collective-permute-start = (bf16[5,1,8,768]{3,2,1,0:T(8,128)(2,1)S(1)}, bf16[5,1,8,768]{3,2,1,0:T(8,128)(2,1)S(1)}, u32[]{:S(2)}, u32[]{:S(2)}) collective-permute-start(bf16[5,1,8,768]{3,2,1,0:T(8,128)(2,1)S(1)} %get-tuple-element.42), channel_id=1, source_target_pairs={{0,64},{64,128},{128,192},{192,256},{256,320},{320,384},{384,448},... | collective-permute-start | bytes 184328 | tf_op jit(solution)/shard_map/ppermute | solution.py:31
  19.6 8.7 %collective-permute-start.3 = (bf16[5,4,1,768]{3,2,1,0:T(2,128)(2,1)S(1)}, bf16[5,4,1,768]{3,2,1,0:T(2,128)(2,1)S(1)}, u32[]{:S(2)}, u32[]{:S(2)}) collective-permute-start(bf16[5,4,1,768]{3,2,1,0:T(2,128)(2,1)S(1)} %get-tuple-element.39), channel_id=1, source_target_pairs={{8,0},{16,8},{24,16},{32,24},{40,32},{48,40},{56,48},{9,1},{17,9},... | collective-permute-start | bytes 92168 | tf_op jit(solution)/shard_map/ppermute | solution.py:32
  21.8 6.6 %copy-start.9 = (bf16[5,4,8,1]{3,2,1,0:T(8,128)(2,1)}, bf16[5,4,8,1]{3,2,1,0:T(8,128)(2,1)S(1)}, u32[]{:S(2)}) copy-start(bf16[5,4,8,1]{3,2,1,0:T(8,128)(2,1)S(1)} %collective-permute-done.5.zhi) | copy-start | bytes 964
  21.8 6.6 %collective-permute-start.2 = (bf16[5,4,1,768]{3,2,1,0:T(2,128)(2,1)S(1)}, bf16[5,4,1,768]{3,2,1,0:T(2,128)(2,1)S(1)}, u32[]{:S(2)}, u32[]{:S(2)}) collective-permute-start(bf16[5,4,1,768]{3,2,1,0:T(2,128)(2,1)S(1)} %get-tuple-element.40), channel_id=1, source_target_pairs={{0,8},{8,16},{16,24},{24,32},{32,40},{40,48},{48,56},{1,9},{9,17},... | collective-permute-start | bytes 92168 | tf_op jit(solution)/shard_map/ppermute | solution.py:31
  28.4 8.8 %copy-start.15 = (s32[48,1]{0,1:T(1,128)S(1)}, s32[48,1]{0,1:T(1,128)}, u32[]{:S(2)}) copy-start(s32[48,1]{0,1:T(1,128)} %param.11) | copy-start | bytes 580
  29.1 43.1 %all-to-all-start = ((bf16[128,5,5,128]{3,2,1,0:T(8,128)(2,1)}), bf16[128,5,5,128]{3,2,1,0:T(8,128)(2,1)S(1)}, u32[]{:S(2)}, u32[]{:S(2)}) async-start(bf16[128,5,5,128]{3,2,1,0:T(8,128)(2,1)} %pad_maximum_fusion), calls=%async_computation | async-start | bytes 2621440 | tf_op jit(solution)/shard_map/all_to_all | solution.py:260
  40.5 32.9 %copy-start.14 = (bf16[5,4,8,1]{3,2,1,0:T(8,128)(2,1)S(1)}, bf16[5,4,8,1]{3,2,1,0:T(8,128)(2,1)}, u32[]{:S(2)}) copy-start(bf16[5,4,8,1]{3,2,1,0:T(8,128)(2,1)} %get-tuple-element.32) | copy-start | bytes 964
  40.5 38.3 %collective-permute-start.6 = (bf16[5,1,8,768]{3,2,1,0:T(8,128)(2,1)}, bf16[5,1,8,768]{3,2,1,0:T(8,128)(2,1)S(1)}, u32[]{:S(2)}, u32[]{:S(2)}) collective-permute-start(bf16[5,1,8,768]{3,2,1,0:T(8,128)(2,1)} %get-tuple-element.27), channel_id=1, source_target_pairs={{0,64},{64,128},{128,192},{192,256},{256,320},{320,384},{384,448},... | collective-permute-start | bytes 184328 | tf_op jit(solution)/shard_map/ppermute | solution.py:272
  44.6 34.2 %collective-permute-start.7 = (bf16[5,1,8,768]{3,2,1,0:T(8,128)(2,1)}, bf16[5,1,8,768]{3,2,1,0:T(8,128)(2,1)S(1)}, u32[]{:S(2)}, u32[]{:S(2)}) collective-permute-start(bf16[5,1,8,768]{3,2,1,0:T(8,128)(2,1)} %get-tuple-element.28), channel_id=1, source_target_pairs={{64,0},{128,64},{192,128},{256,192},{320,256},{384,320},{448,384},... | collective-permute-start | bytes 184328 | tf_op jit(solution)/shard_map/ppermute | solution.py:273
  45.9 32.8 %collective-permute-start.8 = (bf16[5,4,1,768]{3,2,1,0:T(2,128)(2,1)}, bf16[5,4,1,768]{3,2,1,0:T(2,128)(2,1)S(1)}, u32[]{:S(2)}, u32[]{:S(2)}) collective-permute-start(bf16[5,4,1,768]{3,2,1,0:T(2,128)(2,1)} %get-tuple-element.29), channel_id=1, source_target_pairs={{0,8},{8,16},{16,24},{24,32},{32,40},{40,48},{48,56},{1,9},{9,17},... | collective-permute-start | bytes 92168 | tf_op jit(solution)/shard_map/ppermute | solution.py:272
  49.2 29.5 %collective-permute-start.9 = (bf16[5,4,1,768]{3,2,1,0:T(2,128)(2,1)}, bf16[5,4,1,768]{3,2,1,0:T(2,128)(2,1)S(1)}, u32[]{:S(2)}, u32[]{:S(2)}) collective-permute-start(bf16[5,4,1,768]{3,2,1,0:T(2,128)(2,1)} %get-tuple-element.30), channel_id=1, source_target_pairs={{8,0},{16,8},{24,16},{32,24},{40,32},{48,40},{56,48},{9,1},{17,9},... | collective-permute-start | bytes 92168 | tf_op jit(solution)/shard_map/ppermute | solution.py:273
  50.5 22.9 %collective-permute-start.10 = (bf16[5,4,8,1]{3,2,1,0:T(8,128)(2,1)}, bf16[5,4,8,1]{3,2,1,0:T(8,128)(2,1)S(1)}, u32[]{:S(2)}, u32[]{:S(2)}) collective-permute-start(bf16[5,4,8,1]{3,2,1,0:T(8,128)(2,1)} %get-tuple-element.31), channel_id=1, source_target_pairs={{0,1},{1,2},{2,3},{3,4},{4,5},{5,6},{6,7},{8,9},{9,10},{10,11},{11... | collective-permute-start | bytes 968 | tf_op jit(solution)/shard_map/ppermute | solution.py:272
  73.4 5.4 %copy-start.11 = (bf16[5,4,8,1]{3,2,1,0:T(8,128)(2,1)}, bf16[5,4,8,1]{3,2,1,0:T(8,128)(2,1)S(1)}, u32[]{:S(2)}) copy-start(bf16[5,4,8,1]{3,2,1,0:T(8,128)(2,1)S(1)} %collective-permute-done.10.zlo) | copy-start | bytes 964
  73.4 5.3 %collective-permute-start.11 = (bf16[5,4,8,1]{3,2,1,0:T(8,128)(2,1)S(1)}, bf16[5,4,8,1]{3,2,1,0:T(8,128)(2,1)S(1)}, u32[]{:S(2)}, u32[]{:S(2)}) collective-permute-start(bf16[5,4,8,1]{3,2,1,0:T(8,128)(2,1)S(1)} %copy-done.14), channel_id=1, source_target_pairs={{1,0},{2,1},{3,2},{4,3},{5,4},{6,5},{7,6},{9,8},{10,9},{11,10},{12... | collective-permute-start | bytes 968 | tf_op jit(solution)/shard_map/ppermute | solution.py:273
  76.7 8.6 %copy-start.13 = (s32[48]{0:T(128)S(1)}, s32[48]{0:T(128)}, u32[]{:S(2)}) copy-start(s32[48]{0:T(128)} %param.12) | copy-start | bytes 580
  78.7 0.7 copy-start.4
  78.8 0.7 copy-start.1
  78.8 0.7 copy-start.2
  87.2 14.0 %all-to-all-start.1 = ((f32[64,1,1]{2,1,0:T(1,128)}), f32[64,1,1]{2,1,0:T(1,128)S(1)}, u32[]{:S(2)}, u32[]{:S(2)}) async-start(f32[64,1,1]{2,1,0:T(1,128)} %broadcast_in_dim.10), calls=%async_computation.1 | async-start | bytes 65536 | tf_op jit(solution)/shard_map/all_to_all | solution.py:81
  103.0 16.0 %all-to-all-start.2 = ((f32[8,1,1]{2,1,0:T(1,128)}), f32[8,1,1]{2,1,0:T(1,128)S(1)}, u32[]{:S(2)}, u32[]{:S(2)}) async-start(f32[8,1,1]{2,1,0:T(1,128)} %broadcast_in_dim.11), calls=%async_computation.2 | async-start | bytes 8192 | tf_op jit(solution)/shard_map/all_to_all | solution.py:81
  (7 other events, 4.4 us)

commit v5 on v4

--- a/solution.py
+++ b/solution.py
@@ -242,12 +242,13 @@
     dims = (1, 2, 3)
 
     slots = goal_weight.shape[0]
+    cells = FIELDS * BX * BY * BZ
     packed = jnp.concatenate(
         [
-            goal_weight.reshape(slots, FIELDS, BX * BY, BZ),
-            jnp.broadcast_to(reaction[:, :, None, None], (slots, FIELDS, 1, BZ)),
+            goal_weight.reshape(slots, cells),
+            jnp.pad(reaction, ((0, 0), (0, BZ - FIELDS))),
         ],
-        axis=2,
+        axis=1,
     )
 
     f32, bf16 = jnp.float32, jnp.bfloat16
@@ -281,8 +282,8 @@
     slot_of = targets * capacity + rank
 
     mine = arrived[slot_of]
-    goal = to_cells(mine[:, :, : BX * BY].reshape(-1, FIELDS, BX, BY, BZ))
-    react = per_block_cells(mine[:, :, BX * BY, 0])
+    goal = to_cells(mine[:, :cells].reshape(-1, FIELDS, BX, BY, BZ))
+    react = per_block_cells(mine[:, cells : cells + FIELDS])
     enriched, part = pl.pallas_call(
         adjoint_kernel,
         out_shape=[jax.ShapeDtypeStruct(state.shape, bf16), jax.ShapeDtypeStruct((nx // BX, ny, nz), f32)],

time: 122 us -> 116 us (0.951)
  waiting for transfers between devices: 34 us -> 23.3 us
  starting transfers between devices: 59.6 us -> 65.8 us
  other arithmetic: 5.23 us -> 3.33 us
    all_to_all x1, waiting for transfers between devices: 17.8 us -> 3.86 us  [shards(): arrived = lax.all_to_all(packed, ('gy', 'gz'), 0, 0, tiled=True)]
    ppermute x3, starting transfers between devices: 11.4 us -> 4.5 us  [faces(): above = lax.ppermute(head, axis, [(i + 1, i) for i in range(ends)])]
    all_to_all x2, starting transfers between devices: 14.1 us -> 20.5 us  [global_sum(): x = jnp.sum(lax.all_to_all(spread, group, 0, 0, tiled=True))]
    all_to_all x1, starting transfers between devices: 8.09 us -> 11.9 us  [shards(): arrived = lax.all_to_all(packed, ('gy', 'gz'), 0, 0, tiled=True)]
    ppermute x3, waiting for transfers between devices: 0.01 us -> 3.33 us  [faces(): above = lax.ppermute(head, axis, [(i + 1, i) for i in range(ends)])]
    ppermute x3, starting transfers between devices: 9.9 us -> 12.3 us  [faces(): below = lax.ppermute(tail, axis, [(i, i + 1) for i in range(ends)])]
    concatenate x1, other arithmetic: 1.75 us -> 0.05 us  [shards(): jnp.concatenate([goal_weight.reshape(slots, cells), jnp.pad(reaction, ((0...]
    all_to_all x0 -> x2, local copies, waits for them, and re-layouts: none -> 1.37 us  [shards(): arrived = lax.all_to_all(packed, ('gy', 'gz'), 0, 0, tiled=True)]
  transfers between devices with their start and end apart: 15 -> 15, of which waited for: 4 -> 5; matrix products, arithmetic and copies ran while one was open for 7% -> 5% of each run, Pallas kernels for 3% -> 3%
where the time goes in v5:
time: 116 us; the launch traced here: 115 us
  starting transfers between devices  65.8 us (57%)
  waiting for transfers between devices  23.3 us (20%)
  local copies, waits for them, and re-layouts  12.6 us (11%)
  Pallas kernels  7.98 us (7%)
  other arithmetic  3.33 us (3%)
  between operations  1.67 us (1%)
    all_to_all x2, starting transfers between devices, global_sum(): x = jnp.sum(lax.all_to_all(spread, group, 0, 0, tiled=True))  20.5 us
    all_to_all x2, waiting for transfers between devices, global_sum(): x = jnp.sum(lax.all_to_all(spread, group, 0, 0, tiled=True))  15.3 us
    ppermute x3, starting transfers between devices, faces(): below = lax.ppermute(tail, axis, [(i, i + 1) for i in range(ends)])  12.3 us
    all_to_all x1, starting transfers between devices, shards(): arrived = lax.all_to_all(packed, ('gy', 'gz'), 0, 0, tiled=True)  11.9 us
    ppermute x3, starting transfers between devices, shards(): lax.ppermute(high, axis, [(i, i + 1) for i in range(ends)])  11.8 us
    pallas_call x1, Pallas kernels, shards(): pl.pallas_call(adjoint_kernel, out_shape=[jax.ShapeDtypeStruct(state.shap...  4.87 us
    ppermute x3, starting transfers between devices, shards(): lax.ppermute(low, axis, [(i + 1, i) for i in range(ends)])  4.77 us
    ppermute x3, starting transfers between devices, faces(): above = lax.ppermute(head, axis, [(i + 1, i) for i in range(ends)])  4.5 us
  transfers between devices with their start and end apart: 15, of which 5 were waited for; matrix products, arithmetic and copies ran while one was open for 5% of the time, Pallas kernels for 3%

profile of v5, /device:TPU:1, one launch (start us, length us, event | category | flops | bytes accessed | tf_op | source)
XLA Modules:
  0.0 114.7 jit_solution(6033716055941591794)
XLA Ops:
  1.6 4.8 %collective-permute-start = (bf16[5,1,8,768]{3,2,1,0:T(8,128)(2,1)S(1)}, bf16[5,1,8,768]{3,2,1,0:T(8,128)(2,1)S(1)}, u32[]{:S(2)}, u32[]{:S(2)}) collective-permute-start(bf16[5,1,8,768]{3,2,1,0:T(8,128)(2,1)S(1)} %get-tuple-element.42), channel_id=1, source_target_pairs={{0,64},{64,128},{128,192},{192,256},{256,320},{320,384},{384,448},... | collective-permute-start | bytes 184328 | tf_op jit(solution)/shard_map/ppermute | solution.py:31
  6.4 1.3 %collective-permute-start.1 = (bf16[5,1,8,768]{3,2,1,0:T(8,128)(2,1)S(1)}, bf16[5,1,8,768]{3,2,1,0:T(8,128)(2,1)S(1)}, u32[]{:S(2)}, u32[]{:S(2)}) collective-permute-start(bf16[5,1,8,768]{3,2,1,0:T(8,128)(2,1)S(1)} %get-tuple-element.41), channel_id=1, source_target_pairs={{64,0},{128,64},{192,128},{256,192},{320,256},{384,320},{448,384},... | collective-permute-start | bytes 184328 | tf_op jit(solution)/shard_map/ppermute | solution.py:32
  7.7 1.2 %fusion.6 = (bf16[5,4,1,768]{3,2,1,0:T(2,128)(2,1)S(1)}, bf16[5,4,1,768]{3,2,1,0:T(2,128)(2,1)S(1)}) fusion(bf16[5,4,8,768]{3,2,1,0:T(8,128)(2,1)} %s_ref.3), kind=kLoop, calls=%fused_computation.17 | loop fusion | bytes 122880 | tf_op jit(solution)/shard_map/slice | solution.py:29
  8.9 3.2 %collective-permute-start.2 = (bf16[5,4,1,768]{3,2,1,0:T(2,128)(2,1)S(1)}, bf16[5,4,1,768]{3,2,1,0:T(2,128)(2,1)S(1)}, u32[]{:S(2)}, u32[]{:S(2)}) collective-permute-start(bf16[5,4,1,768]{3,2,1,0:T(2,128)(2,1)S(1)} %get-tuple-element.40), channel_id=1, source_target_pairs={{0,8},{8,16},{16,24},{24,32},{32,40},{40,48},{48,56},{1,9},{9,17},... | collective-permute-start | bytes 92168 | tf_op jit(solution)/shard_map/ppermute | solution.py:31
  13.0 4.2 %collective-permute-start.4 = (bf16[5,4,8,1]{3,2,1,0:T(8,128)(2,1)S(1)}, bf16[5,4,8,1]{3,2,1,0:T(8,128)(2,1)S(1)}, u32[]{:S(2)}, u32[]{:S(2)}) collective-permute-start(bf16[5,4,8,1]{3,2,1,0:T(8,128)(2,1)S(1)} %get-tuple-element.38), channel_id=1, source_target_pairs={{0,1},{1,2},{2,3},{3,4},{4,5},{5,6},{6,7},{8,9},{9,10},{10,11},{11... | collective-permute-start | bytes 968 | tf_op jit(solution)/shard_map/ppermute | solution.py:31
  17.2 1.3 %collective-permute-start.3 = (bf16[5,4,1,768]{3,2,1,0:T(2,128)(2,1)S(1)}, bf16[5,4,1,768]{3,2,1,0:T(2,128)(2,1)S(1)}, u32[]{:S(2)}, u32[]{:S(2)}) collective-permute-start(bf16[5,4,1,768]{3,2,1,0:T(2,128)(2,1)S(1)} %get-tuple-element.39), channel_id=1, source_target_pairs={{8,0},{16,8},{24,16},{32,24},{40,32},{48,40},{56,48},{9,1},{17,9},... | collective-permute-start | bytes 92168 | tf_op jit(solution)/shard_map/ppermute | solution.py:32
  19.0 1.9 %collective-permute-start.5 = (bf16[5,4,8,1]{3,2,1,0:T(8,128)(2,1)S(1)}, bf16[5,4,8,1]{3,2,1,0:T(8,128)(2,1)S(1)}, u32[]{:S(2)}, u32[]{:S(2)}) collective-permute-start(bf16[5,4,8,1]{3,2,1,0:T(8,128)(2,1)S(1)} %get-tuple-element.37), channel_id=1, source_target_pairs={{1,0},{2,1},{3,2},{4,3},{5,4},{6,5},{7,6},{9,8},{10,9},{11,10},{12... | collective-permute-start | bytes 968 | tf_op jit(solution)/shard_map/ppermute | solution.py:32
  20.9 3.3 %collective-permute-done.5.zhi = bf16[5,4,8,1]{3,2,1,0:T(8,128)(2,1)S(1)} collective-permute-done((bf16[5,4,8,1]{3,2,1,0:T(8,128)(2,1)S(1)}, bf16[5,4,8,1]{3,2,1,0:T(8,128)(2,1)S(1)}, u32[]{:S(2)}, u32[]{:S(2)}) %collective-permute-start.5) | collective-permute-done | bytes 352 | tf_op jit(solution)/shard_map/ppermute | solution.py:32
  25.5 11.9 %all-to-all-start = ((bf16[64,2,2688]{2,1,0:T(2,128)(2,1)}), bf16[64,2,2688]{2,1,0:T(2,128)(2,1)S(1)}, u32[]{:S(2)}, u32[]{:S(2)}) async-start(bf16[64,2,2688]{2,1,0:T(2,128)(2,1)} %all_to_all.16), calls=%async_computation | async-start | bytes 1376256 | tf_op jit(solution)/shard_map/all_to_all | solution.py:261
  37.6 3.1 %shard_map.103 = (f32[5,4,8,768]{3,2,1,0:T(8,128)}, bf16[4,8,768]{2,1,0:T(8,128)(2,1)}, bf16[5,1,8,768]{3,2,1,0:T(8,128)(2,1)}, bf16[5,1,8,768]{3,2,1,0:T(8,128)...) custom-call(f32[5,5]{1,0:T(8,128)} %c_ref.3, ...), custom_call_target="tpu_custom_call" | custom-call | tf_op jit(solution)/shard_map/pallas_call | solution.py:262
  40.7 4.6 %collective-permute-start.6 = (bf16[5,1,8,768]{3,2,1,0:T(8,128)(2,1)}, bf16[5,1,8,768]{3,2,1,0:T(8,128)(2,1)S(1)}, u32[]{:S(2)}, u32[]{:S(2)}) collective-permute-start(bf16[5,1,8,768]{3,2,1,0:T(8,128)(2,1)} %get-tuple-element.27), channel_id=1, source_target_pairs={{0,64},{64,128},{128,192},{192,256},{256,320},{320,384},{384,448},... | collective-permute-start | bytes 184328 | tf_op jit(solution)/shard_map/ppermute | solution.py:273
  45.4 1.3 %collective-permute-start.7 = (bf16[5,1,8,768]{3,2,1,0:T(8,128)(2,1)}, bf16[5,1,8,768]{3,2,1,0:T(8,128)(2,1)S(1)}, u32[]{:S(2)}, u32[]{:S(2)}) collective-permute-start(bf16[5,1,8,768]{3,2,1,0:T(8,128)(2,1)} %get-tuple-element.28), channel_id=1, source_target_pairs={{64,0},{128,64},{192,128},{256,192},{320,256},{384,320},{448,384},... | collective-permute-start | bytes 184328 | tf_op jit(solution)/shard_map/ppermute | solution.py:274
  46.7 3.3 %collective-permute-start.8 = (bf16[5,4,1,768]{3,2,1,0:T(2,128)(2,1)}, bf16[5,4,1,768]{3,2,1,0:T(2,128)(2,1)S(1)}, u32[]{:S(2)}, u32[]{:S(2)}) collective-permute-start(bf16[5,4,1,768]{3,2,1,0:T(2,128)(2,1)} %get-tuple-element.29), channel_id=1, source_target_pairs={{0,8},{8,16},{16,24},{24,32},{32,40},{40,48},{48,56},{1,9},{9,17},... | collective-permute-start | bytes 92168 | tf_op jit(solution)/shard_map/ppermute | solution.py:273
  50.0 1.3 %collective-permute-start.9 = (bf16[5,4,1,768]{3,2,1,0:T(2,128)(2,1)}, bf16[5,4,1,768]{3,2,1,0:T(2,128)(2,1)S(1)}, u32[]{:S(2)}, u32[]{:S(2)}) collective-permute-start(bf16[5,4,1,768]{3,2,1,0:T(2,128)(2,1)} %get-tuple-element.30), channel_id=1, source_target_pairs={{8,0},{16,8},{24,16},{32,24},{40,32},{48,40},{56,48},{9,1},{17,9},... | collective-permute-start | bytes 92168 | tf_op jit(solution)/shard_map/ppermute | solution.py:274
  51.3 3.9 %collective-permute-start.10 = (bf16[5,4,8,1]{3,2,1,0:T(8,128)(2,1)}, bf16[5,4,8,1]{3,2,1,0:T(8,128)(2,1)S(1)}, u32[]{:S(2)}, u32[]{:S(2)}) collective-permute-start(bf16[5,4,8,1]{3,2,1,0:T(8,128)(2,1)} %get-tuple-element.31), channel_id=1, source_target_pairs={{0,1},{1,2},{2,3},{3,4},{4,5},{5,6},{6,7},{8,9},{9,10},{10,11},{11... | collective-permute-start | bytes 968 | tf_op jit(solution)/shard_map/ppermute | solution.py:273
  55.2 3.9 %all-to-all-done = bf16[64,2,2688]{2,1,0:T(2,128)(2,1)S(1)} async-done(((bf16[64,2,2688]{2,1,0:T(2,128)(2,1)}), bf16[64,2,2688]{2,1,0:T(2,128)(2,1)S(1)}, u32[]{:S(2)}, u32[]{:S(2)}) %all-to-all-start) | async-done | bytes 688160 | tf_op jit(solution)/shard_map/all_to_all | solution.py:261
  60.8 2.2 %collective-permute-start.11 = (bf16[5,4,8,1]{3,2,1,0:T(8,128)(2,1)S(1)}, bf16[5,4,8,1]{3,2,1,0:T(8,128)(2,1)S(1)}, u32[]{:S(2)}, u32[]{:S(2)}) collective-permute-start(bf16[5,4,8,1]{3,2,1,0:T(8,128)(2,1)S(1)} %copy-done.15), channel_id=1, source_target_pairs={{1,0},{2,1},{3,2},{4,3},{5,4},{6,5},{7,6},{9,8},{10,9},{11,10},{12... | collective-permute-start | bytes 968 | tf_op jit(solution)/shard_map/ppermute | solution.py:274
  66.9 4.9 %shard_map.104 = (bf16[5,4,8,768]{3,2,1,0:T(8,128)(2,1)}, f32[2,8,768]{2,1,0:T(8,128)}) custom-call(f32[5,5]{1,0:T(8,128)} %c_ref.3, f32[5,4,8,768]{3,2,1,0:T(8,128)} %get-tuple-element.26.s1_ref, bf16[5,4,8,768]{3,2,1,0:T(8,128)(2,1)} %s_ref.3, bf16[4,8,768]{2,1,0:T(8,128)(2,1)} %d_ref.3, bf16[5,1,8,768]{3,2,1,0:T(8,128)(2,1)} %copy-done.1, ...), custom_call_target="tpu_custom_call" | custom-call | tf_op jit(solution)/shard_map/pallas_call | solution.py:287
  73.3 1.3 %broadcast_in_dim.7 = f32[64,1,1]{2,1,0:T(1,128)} broadcast(f32[]{:T(128)} %fusion.4), dimensions={} | broadcast | bytes 260 | tf_op jit(solution)/shard_map/broadcast_in_dim | solution.py:80
  74.6 8.2 %all-to-all-start.1 = ((f32[64,1,1]{2,1,0:T(1,128)}), f32[64,1,1]{2,1,0:T(1,128)S(1)}, u32[]{:S(2)}, u32[]{:S(2)}) async-start(f32[64,1,1]{2,1,0:T(1,128)} %broadcast_in_dim.7), calls=%async_computation.1 | async-start | bytes 65536 | tf_op jit(solution)/shard_map/all_to_all | solution.py:81
  83.5 8.7 %all-to-all-done.1 = f32[64,1,1]{2,1,0:T(1,128)S(1)} async-done(((f32[64,1,1]{2,1,0:T(1,128)}), f32[64,1,1]{2,1,0:T(1,128)S(1)}, u32[]{:S(2)}, u32[]{:S(2)}) %all-to-all-start.1) | async-done | bytes 288 | tf_op jit(solution)/shard_map/all_to_all | solution.py:81
  92.9 1.2 %broadcast_in_dim.8 = f32[8,1,1]{2,1,0:T(1,128)} broadcast(f32[]{:T(128)} %reduce_sum.51), dimensions={} | broadcast | bytes 36 | tf_op jit(solution)/shard_map/broadcast_in_dim | solution.py:80
  94.1 12.3 %all-to-all-start.2 = ((f32[8,1,1]{2,1,0:T(1,128)}), f32[8,1,1]{2,1,0:T(1,128)S(1)}, u32[]{:S(2)}, u32[]{:S(2)}) async-start(f32[8,1,1]{2,1,0:T(1,128)} %broadcast_in_dim.8), calls=%async_computation.2 | async-start | bytes 8192 | tf_op jit(solution)/shard_map/all_to_all | solution.py:81
  106.4 6.5 %all-to-all-done.2 = f32[8,1,1]{2,1,0:T(1,128)S(1)} async-done(((f32[8,1,1]{2,1,0:T(1,128)}), f32[8,1,1]{2,1,0:T(1,128)S(1)}, u32[]{:S(2)}, u32[]{:S(2)}) %all-to-all-start.2) | async-done | bytes 64 | tf_op jit(solution)/shard_map/all_to_all | solution.py:81
  (72 shorter events, 13.1 us)
Async XLA Ops:
  0.6 17.9 %copy-start = (bf16[128,5,2,2,128]{4,3,2,1,0:T(2,128)(2,1)S(1)}, bf16[128,5,2,2,128]{4,3,2,1,0:T(2,128)(2,1)}, u32[]{:S(2)}) copy-start(bf16[128,5,2,2,128]{4,3,2,1,0:T(2,128)(2,1)} %param.14) | copy-start | bytes 1966084
  1.6 22.7 %collective-permute-start = (bf16[5,1,8,768]{3,2,1,0:T(8,128)(2,1)S(1)}, bf16[5,1,8,768]{3,2,1,0:T(8,128)(2,1)S(1)}, u32[]{:S(2)}, u32[]{:S(2)}) collective-permute-start(bf16[5,1,8,768]{3,2,1,0:T(8,128)(2,1)S(1)} %get-tuple-element.42), channel_id=1, source_target_pairs={{0,64},{64,128},{128,192},{192,256},{256,320},{320,384},{384,448},... | collective-permute-start | bytes 184328 | tf_op jit(solution)/shard_map/ppermute | solution.py:31
  6.4 17.9 %collective-permute-start.1 = (bf16[5,1,8,768]{3,2,1,0:T(8,128)(2,1)S(1)}, bf16[5,1,8,768]{3,2,1,0:T(8,128)(2,1)S(1)}, u32[]{:S(2)}, u32[]{:S(2)}) collective-permute-start(bf16[5,1,8,768]{3,2,1,0:T(8,128)(2,1)S(1)} %get-tuple-element.41), channel_id=1, source_target_pairs={{64,0},{128,64},{192,128},{256,192},{320,256},{384,320},{448,384},... | collective-permute-start | bytes 184328 | tf_op jit(solution)/shard_map/ppermute | solution.py:32
  8.9 15.4 %collective-permute-start.2 = (bf16[5,4,1,768]{3,2,1,0:T(2,128)(2,1)S(1)}, bf16[5,4,1,768]{3,2,1,0:T(2,128)(2,1)S(1)}, u32[]{:S(2)}, u32[]{:S(2)}) collective-permute-start(bf16[5,4,1,768]{3,2,1,0:T(2,128)(2,1)S(1)} %get-tuple-element.40), channel_id=1, source_target_pairs={{0,8},{8,16},{16,24},{24,32},{32,40},{40,48},{48,56},{1,9},{9,17},... | collective-permute-start | bytes 92168 | tf_op jit(solution)/shard_map/ppermute | solution.py:31
  13.0 5.8 %copy-start.13 = (bf16[128,5]{0,1:T(8,128)(2,1)S(1)}, bf16[128,5]{0,1:T(8,128)(2,1)}, u32[]{:S(2)}) copy-start(bf16[128,5]{0,1:T(8,128)(2,1)} %param.15) | copy-start | bytes 3844
  13.0 6.0 %collective-permute-start.4 = (bf16[5,4,8,1]{3,2,1,0:T(8,128)(2,1)S(1)}, bf16[5,4,8,1]{3,2,1,0:T(8,128)(2,1)S(1)}, u32[]{:S(2)}, u32[]{:S(2)}) collective-permute-start(bf16[5,4,8,1]{3,2,1,0:T(8,128)(2,1)S(1)} %get-tuple-element.38), channel_id=1, source_target_pairs={{0,1},{1,2},{2,3},{3,4},{4,5},{5,6},{6,7},{8,9},{9,10},{10,11},{11... | collective-permute-start | bytes 968 | tf_op jit(solution)/shard_map/ppermute | solution.py:31
  17.2 7.1 %collective-permute-start.3 = (bf16[5,4,1,768]{3,2,1,0:T(2,128)(2,1)S(1)}, bf16[5,4,1,768]{3,2,1,0:T(2,128)(2,1)S(1)}, u32[]{:S(2)}, u32[]{:S(2)}) collective-permute-start(bf16[5,4,1,768]{3,2,1,0:T(2,128)(2,1)S(1)} %get-tuple-element.39), channel_id=1, source_target_pairs={{8,0},{16,8},{24,16},{32,24},{40,32},{48,40},{56,48},{9,1},{17,9},... | collective-permute-start | bytes 92168 | tf_op jit(solution)/shard_map/ppermute | solution.py:32
  18.9 2.0 %copy-start.10 = (bf16[5,4,8,1]{3,2,1,0:T(8,128)(2,1)}, bf16[5,4,8,1]{3,2,1,0:T(8,128)(2,1)S(1)}, u32[]{:S(2)}) copy-start(bf16[5,4,8,1]{3,2,1,0:T(8,128)(2,1)S(1)} %collective-permute-done.4.zlo) | copy-start | bytes 964
  19.0 5.3 %collective-permute-start.5 = (bf16[5,4,8,1]{3,2,1,0:T(8,128)(2,1)S(1)}, bf16[5,4,8,1]{3,2,1,0:T(8,128)(2,1)S(1)}, u32[]{:S(2)}, u32[]{:S(2)}) collective-permute-start(bf16[5,4,8,1]{3,2,1,0:T(8,128)(2,1)S(1)} %get-tuple-element.37), channel_id=1, source_target_pairs={{1,0},{2,1},{3,2},{4,3},{5,4},{6,5},{7,6},{9,8},{10,9},{11,10},{12... | collective-permute-start | bytes 968 | tf_op jit(solution)/shard_map/ppermute | solution.py:32
  24.3 1.2 %copy-start.11 = (bf16[5,4,8,1]{3,2,1,0:T(8,128)(2,1)}, bf16[5,4,8,1]{3,2,1,0:T(8,128)(2,1)S(1)}, u32[]{:S(2)}) copy-start(bf16[5,4,8,1]{3,2,1,0:T(8,128)(2,1)S(1)} %collective-permute-done.5.zhi) | copy-start | bytes 964
  24.3 1.2 %copy-start.7 = (bf16[5,4,1,768]{3,2,1,0:T(2,128)(2,1)}, bf16[5,4,1,768]{3,2,1,0:T(2,128)(2,1)S(1)}, u32[]{:S(2)}) copy-start(bf16[5,4,1,768]{3,2,1,0:T(2,128)(2,1)S(1)} %collective-permute-done.2.ylo) | copy-start | bytes 92164
  24.3 1.2 %copy-start.8 = (bf16[5,4,1,768]{3,2,1,0:T(2,128)(2,1)}, bf16[5,4,1,768]{3,2,1,0:T(2,128)(2,1)S(1)}, u32[]{:S(2)}) copy-start(bf16[5,4,1,768]{3,2,1,0:T(2,128)(2,1)S(1)} %collective-permute-done.3.yhi) | copy-start | bytes 92164
  25.5 12.0 %copy-start.16 = (s32[48,1]{0,1:T(1,128)S(1)}, s32[48,1]{0,1:T(1,128)}, u32[]{:S(2)}) copy-start(s32[48,1]{0,1:T(1,128)} %param.11) | copy-start | bytes 580
  25.5 33.6 %all-to-all-start = ((bf16[64,2,2688]{2,1,0:T(2,128)(2,1)}), bf16[64,2,2688]{2,1,0:T(2,128)(2,1)S(1)}, u32[]{:S(2)}, u32[]{:S(2)}) async-start(bf16[64,2,2688]{2,1,0:T(2,128)(2,1)} %all_to_all.16), calls=%async_computation | async-start | bytes 1376256 | tf_op jit(solution)/shard_map/all_to_all | solution.py:261
  40.7 25.4 %collective-permute-start.6 = (bf16[5,1,8,768]{3,2,1,0:T(8,128)(2,1)}, bf16[5,1,8,768]{3,2,1,0:T(8,128)(2,1)S(1)}, u32[]{:S(2)}, u32[]{:S(2)}) collective-permute-start(bf16[5,1,8,768]{3,2,1,0:T(8,128)(2,1)} %get-tuple-element.27), channel_id=1, source_target_pairs={{0,64},{64,128},{128,192},{192,256},{256,320},{320,384},{384,448},... | collective-permute-start | bytes 184328 | tf_op jit(solution)/shard_map/ppermute | solution.py:273
  45.4 20.8 %collective-permute-start.7 = (bf16[5,1,8,768]{3,2,1,0:T(8,128)(2,1)}, bf16[5,1,8,768]{3,2,1,0:T(8,128)(2,1)S(1)}, u32[]{:S(2)}, u32[]{:S(2)}) collective-permute-start(bf16[5,1,8,768]{3,2,1,0:T(8,128)(2,1)} %get-tuple-element.28), channel_id=1, source_target_pairs={{64,0},{128,64},{192,128},{256,192},{320,256},{384,320},{448,384},... | collective-permute-start | bytes 184328 | tf_op jit(solution)/shard_map/ppermute | solution.py:274
  46.7 19.5 %collective-permute-start.8 = (bf16[5,4,1,768]{3,2,1,0:T(2,128)(2,1)}, bf16[5,4,1,768]{3,2,1,0:T(2,128)(2,1)S(1)}, u32[]{:S(2)}, u32[]{:S(2)}) collective-permute-start(bf16[5,4,1,768]{3,2,1,0:T(2,128)(2,1)} %get-tuple-element.29), channel_id=1, source_target_pairs={{0,8},{8,16},{16,24},{24,32},{32,40},{40,48},{48,56},{1,9},{9,17},... | collective-permute-start | bytes 92168 | tf_op jit(solution)/shard_map/ppermute | solution.py:273
  50.0 16.2 %collective-permute-start.9 = (bf16[5,4,1,768]{3,2,1,0:T(2,128)(2,1)}, bf16[5,4,1,768]{3,2,1,0:T(2,128)(2,1)S(1)}, u32[]{:S(2)}, u32[]{:S(2)}) collective-permute-start(bf16[5,4,1,768]{3,2,1,0:T(2,128)(2,1)} %get-tuple-element.30), channel_id=1, source_target_pairs={{8,0},{16,8},{24,16},{32,24},{40,32},{48,40},{56,48},{9,1},{17,9},... | collective-permute-start | bytes 92168 | tf_op jit(solution)/shard_map/ppermute | solution.py:274
  51.3 8.9 %collective-permute-start.10 = (bf16[5,4,8,1]{3,2,1,0:T(8,128)(2,1)}, bf16[5,4,8,1]{3,2,1,0:T(8,128)(2,1)S(1)}, u32[]{:S(2)}, u32[]{:S(2)}) collective-permute-start(bf16[5,4,8,1]{3,2,1,0:T(8,128)(2,1)} %get-tuple-element.31), channel_id=1, source_target_pairs={{0,1},{1,2},{2,3},{3,4},{4,5},{5,6},{6,7},{8,9},{9,10},{10,11},{11... | collective-permute-start | bytes 968 | tf_op jit(solution)/shard_map/ppermute | solution.py:273
  60.2 5.1 %copy-start.9 = (bf16[5,4,8,1]{3,2,1,0:T(8,128)(2,1)}, bf16[5,4,8,1]{3,2,1,0:T(8,128)(2,1)S(1)}, u32[]{:S(2)}) copy-start(bf16[5,4,8,1]{3,2,1,0:T(8,128)(2,1)S(1)} %collective-permute-done.10.zlo) | copy-start | bytes 964
  60.8 5.3 %collective-permute-start.11 = (bf16[5,4,8,1]{3,2,1,0:T(8,128)(2,1)S(1)}, bf16[5,4,8,1]{3,2,1,0:T(8,128)(2,1)S(1)}, u32[]{:S(2)}, u32[]{:S(2)}) collective-permute-start(bf16[5,4,8,1]{3,2,1,0:T(8,128)(2,1)S(1)} %copy-done.15), channel_id=1, source_target_pairs={{1,0},{2,1},{3,2},{4,3},{5,4},{6,5},{7,6},{9,8},{10,9},{11,10},{12... | collective-permute-start | bytes 968 | tf_op jit(solution)/shard_map/ppermute | solution.py:274
  66.8 5.9 %copy-start.14 = (s32[48]{0:T(128)S(1)}, s32[48]{0:T(128)}, u32[]{:S(2)}) copy-start(s32[48]{0:T(128)} %param.12) | copy-start | bytes 580
  74.6 17.6 %all-to-all-start.1 = ((f32[64,1,1]{2,1,0:T(1,128)}), f32[64,1,1]{2,1,0:T(1,128)S(1)}, u32[]{:S(2)}, u32[]{:S(2)}) async-start(f32[64,1,1]{2,1,0:T(1,128)} %broadcast_in_dim.7), calls=%async_computation.1 | async-start | bytes 65536 | tf_op jit(solution)/shard_map/all_to_all | solution.py:81
  94.1 18.9 %all-to-all-start.2 = ((f32[8,1,1]{2,1,0:T(1,128)}), f32[8,1,1]{2,1,0:T(1,128)S(1)}, u32[]{:S(2)}, u32[]{:S(2)}) async-start(f32[8,1,1]{2,1,0:T(1,128)} %broadcast_in_dim.8), calls=%async_computation.2 | async-start | bytes 8192 | tf_op jit(solution)/shard_map/all_to_all | solution.py:81
  (8 other events, 6.3 us)

commit v6 on v5

--- a/solution.py
+++ b/solution.py
@@ -196,7 +196,7 @@
 
 
 def adjoint_kernel(c_ref, s1_ref, s_ref, d_ref, xlo, xhi, ylo, yhi, zlo, zhi, eff_ref, goal_ref, react_ref,
-                   enr_ref, part_ref):
+                   w_ref, enr_ref, part_ref, spread_ref):
     nf, nx, ny, nz = s_ref.shape
     geo = _masks(ny, nz)
     f32 = jnp.float32
@@ -235,6 +235,10 @@
                 term = jnp.abs(residual[f][x] * e.astype(f32))
                 acc = term if acc is None else acc + term
         part_ref[bx] = acc
+        weighted = acc * w_ref[bx]
+        total = weighted if bx == 0 else total + weighted
+    total = jnp.sum(jnp.sum(total, axis=1, keepdims=True), axis=0, keepdims=True)
+    spread_ref[...] = jnp.broadcast_to(total, spread_ref.shape)
 
 
 def shards(state, diffusivity, coupling, owner, levels, mark_count, goal_weight, reaction):
@@ -284,17 +288,30 @@
     mine = arrived[slot_of]
     goal = to_cells(mine[:, :cells].reshape(-1, FIELDS, BX, BY, BZ))
     react = per_block_cells(mine[:, cells : cells + FIELDS])
-    enriched, part = pl.pallas_call(
+    weights = jnp.exp2(2.0 * levels.astype(jnp.float32))
+    weight_cells = jnp.broadcast_to(
+        weights.reshape(NBX, NBY, 1, NBZ, 1), (NBX, NBY, BY, NBZ, BZ)
+    ).reshape(nx // BX, ny, nz)
+    plane = lax.axis_size("gy") * lax.axis_size("gz")
+    enriched, part, spread = pl.pallas_call(
         adjoint_kernel,
-        out_shape=[jax.ShapeDtypeStruct(state.shape, bf16), jax.ShapeDtypeStruct((nx // BX, ny, nz), f32)],
-        in_specs=[smem] + [vmem] * 12,
-        out_specs=[vmem] * 2,
-    )(coupling, section_one, state, diffusivity, *section_halo, effective, goal, react)
+        out_shape=[
+            jax.ShapeDtypeStruct(state.shape, bf16),
+            jax.ShapeDtypeStruct((nx // BX, ny, nz), f32),
+            jax.ShapeDtypeStruct((plane, 1), f32),
+        ],
+        in_specs=[smem] + [vmem] * 13,
+        out_specs=[vmem] * 3,
+    )(coupling, section_one, state, diffusivity, *section_halo, effective, goal, react, weight_cells)
     sums = jnp.sum(part.reshape(nx // BX, ny // BY, BY, nz // BZ, BZ), axis=(2, 4)).reshape(-1)
-
-    weights = jnp.exp2(2.0 * levels.astype(jnp.float32))
     indicator = weights * sums
-    overall = global_sum(jnp.sum(indicator))
+
+    across = lax.axis_size("gx")
+    level_one = lax.all_to_all(spread, ("gy", "gz"), 0, 0, tiled=True)
+    level_two = lax.all_to_all(
+        jnp.broadcast_to(level_one.reshape(1, plane), (across, plane)), ("gx",), 0, 0, tiled=True
+    )
+    overall = jnp.sum(level_two)
     block_count = owner.shape[0] * lax.axis_size("gx") * lax.axis_size("gy") * lax.axis_size("gz")
     share = indicator * block_count / overall
     marked = jnp.minimum(1.0, mark_count[0].astype(jnp.float32) * indicator / overall)

time: 116 us -> 113 us (0.974)
  blocking collectives: 0 us -> 18.4 us
  waiting for transfers between devices: 23.3 us -> 12 us
  starting transfers between devices: 65.8 us -> 57.7 us
    all_to_all x0 -> x1, blocking collectives: none -> 18.4 us  [shards(): level_one = lax.all_to_all(spread, ('gy', 'gz'), 0, 0, tiled=True)]
    all_to_all x2 -> x1, waiting for transfers between devices: 15.3 us -> 4.88 us  [shards(): lax.all_to_all(jnp.broadcast_to(level_one.reshape(1, plane), (across, pla...]
    all_to_all x2 -> x1, starting transfers between devices: 20.5 us -> 12.3 us  [shards(): lax.all_to_all(jnp.broadcast_to(level_one.reshape(1, plane), (across, pla...]
    broadcast_in_dim x2 -> x3, local copies, waits for them, and re-layouts: 2.52 us -> 0.75 us  [the longest x1 0.59 us: shards(): jnp.broadcast_to(level_one.reshape(1, plane), (across, plane))]
    reduce_sum x3 -> x1, other arithmetic: 1.9 us -> 0.66 us  [shards(): overall = jnp.sum(level_two)]
  transfers between devices with their start and end apart: 15 -> 14, of which waited for: 5 -> 4; matrix products, arithmetic and copies ran while one was open for 5% -> 7% of each run, Pallas kernels for 3% -> 3%
where the time goes in v6:
time: 113 us; the launch traced here: 112 us
  starting transfers between devices  57.7 us (51%)
  blocking collectives  18.4 us (16%)
  waiting for transfers between devices  12 us (11%)
  local copies, waits for them, and re-layouts  11.5 us (10%)
  Pallas kernels  8.01 us (7%)
  other arithmetic  2.76 us (2%)
  between operations  1.69 us (1%)
    all_to_all x1, blocking collectives, shards(): level_one = lax.all_to_all(spread, ('gy', 'gz'), 0, 0, tiled=True)  18.4 us
    all_to_all x1, starting transfers between devices, shards(): lax.all_to_all(jnp.broadcast_to(level_one.reshape(1, plane), (across, pla...  12.3 us
    ppermute x3, starting transfers between devices, faces(): below = lax.ppermute(tail, axis, [(i, i + 1) for i in range(ends)])  12.3 us
    all_to_all x1, starting transfers between devices, shards(): arrived = lax.all_to_all(packed, ('gy', 'gz'), 0, 0, tiled=True)  11.9 us
    ppermute x3, starting transfers between devices, shards(): lax.ppermute(high, axis, [(i, i + 1) for i in range(ends)])  11.8 us
    pallas_call x1, Pallas kernels, shards(): pl.pallas_call(adjoint_kernel, out_shape=[jax.ShapeDtypeStruct(state.shap...  4.89 us
    all_to_all x1, waiting for transfers between devices, shards(): lax.all_to_all(jnp.broadcast_to(level_one.reshape(1, plane), (across, pla...  4.88 us
    ppermute x3, starting transfers between devices, shards(): lax.ppermute(low, axis, [(i + 1, i) for i in range(ends)])  4.8 us
  transfers between devices with their start and end apart: 14, of which 4 were waited for; matrix products, arithmetic and copies ran while one was open for 7% of the time, Pallas kernels for 3%

profile of v6, /device:TPU:1, one launch (start us, length us, event | category | flops | bytes accessed | tf_op | source)
XLA Modules:
  0.0 112.0 jit_solution(1472720182523008943)
XLA Ops:
  1.6 4.8 %collective-permute-start = (bf16[5,1,8,768]{3,2,1,0:T(8,128)(2,1)S(1)}, bf16[5,1,8,768]{3,2,1,0:T(8,128)(2,1)S(1)}, u32[]{:S(2)}, u32[]{:S(2)}) collective-permute-start(bf16[5,1,8,768]{3,2,1,0:T(8,128)(2,1)S(1)} %get-tuple-element.44), channel_id=1, source_target_pairs={{0,64},{64,128},{128,192},{192,256},{256,320},{320,384},{384,448},... | collective-permute-start | bytes 184328 | tf_op jit(solution)/shard_map/ppermute | solution.py:31
  6.4 1.3 %collective-permute-start.1 = (bf16[5,1,8,768]{3,2,1,0:T(8,128)(2,1)S(1)}, bf16[5,1,8,768]{3,2,1,0:T(8,128)(2,1)S(1)}, u32[]{:S(2)}, u32[]{:S(2)}) collective-permute-start(bf16[5,1,8,768]{3,2,1,0:T(8,128)(2,1)S(1)} %get-tuple-element.43), channel_id=1, source_target_pairs={{64,0},{128,64},{192,128},{256,192},{320,256},{384,320},{448,384},... | collective-permute-start | bytes 184328 | tf_op jit(solution)/shard_map/ppermute | solution.py:32
  7.7 1.2 %fusion.5 = (bf16[5,4,1,768]{3,2,1,0:T(2,128)(2,1)S(1)}, bf16[5,4,1,768]{3,2,1,0:T(2,128)(2,1)S(1)}) fusion(bf16[5,4,8,768]{3,2,1,0:T(8,128)(2,1)} %s_ref.3), kind=kLoop, calls=%fused_computation.16 | loop fusion | bytes 122880 | tf_op jit(solution)/shard_map/slice | solution.py:29
  8.9 3.2 %collective-permute-start.2 = (bf16[5,4,1,768]{3,2,1,0:T(2,128)(2,1)S(1)}, bf16[5,4,1,768]{3,2,1,0:T(2,128)(2,1)S(1)}, u32[]{:S(2)}, u32[]{:S(2)}) collective-permute-start(bf16[5,4,1,768]{3,2,1,0:T(2,128)(2,1)S(1)} %get-tuple-element.42), channel_id=1, source_target_pairs={{0,8},{8,16},{16,24},{24,32},{32,40},{40,48},{48,56},{1,9},{9,17},... | collective-permute-start | bytes 92168 | tf_op jit(solution)/shard_map/ppermute | solution.py:31
  13.0 4.2 %collective-permute-start.4 = (bf16[5,4,8,1]{3,2,1,0:T(8,128)(2,1)S(1)}, bf16[5,4,8,1]{3,2,1,0:T(8,128)(2,1)S(1)}, u32[]{:S(2)}, u32[]{:S(2)}) collective-permute-start(bf16[5,4,8,1]{3,2,1,0:T(8,128)(2,1)S(1)} %get-tuple-element.40), channel_id=1, source_target_pairs={{0,1},{1,2},{2,3},{3,4},{4,5},{5,6},{6,7},{8,9},{9,10},{10,11},{11... | collective-permute-start | bytes 968 | tf_op jit(solution)/shard_map/ppermute | solution.py:31
  17.2 1.3 %collective-permute-start.3 = (bf16[5,4,1,768]{3,2,1,0:T(2,128)(2,1)S(1)}, bf16[5,4,1,768]{3,2,1,0:T(2,128)(2,1)S(1)}, u32[]{:S(2)}, u32[]{:S(2)}) collective-permute-start(bf16[5,4,1,768]{3,2,1,0:T(2,128)(2,1)S(1)} %get-tuple-element.41), channel_id=1, source_target_pairs={{8,0},{16,8},{24,16},{32,24},{40,32},{48,40},{56,48},{9,1},{17,9},... | collective-permute-start | bytes 92168 | tf_op jit(solution)/shard_map/ppermute | solution.py:32
  19.0 1.9 %collective-permute-start.5 = (bf16[5,4,8,1]{3,2,1,0:T(8,128)(2,1)S(1)}, bf16[5,4,8,1]{3,2,1,0:T(8,128)(2,1)S(1)}, u32[]{:S(2)}, u32[]{:S(2)}) collective-permute-start(bf16[5,4,8,1]{3,2,1,0:T(8,128)(2,1)S(1)} %get-tuple-element.39), channel_id=1, source_target_pairs={{1,0},{2,1},{3,2},{4,3},{5,4},{6,5},{7,6},{9,8},{10,9},{11,10},{12... | collective-permute-start | bytes 968 | tf_op jit(solution)/shard_map/ppermute | solution.py:32
  20.9 3.3 %collective-permute-done.5.zhi = bf16[5,4,8,1]{3,2,1,0:T(8,128)(2,1)S(1)} collective-permute-done((bf16[5,4,8,1]{3,2,1,0:T(8,128)(2,1)S(1)}, bf16[5,4,8,1]{3,2,1,0:T(8,128)(2,1)S(1)}, u32[]{:S(2)}, u32[]{:S(2)}) %collective-permute-start.5) | collective-permute-done | bytes 352 | tf_op jit(solution)/shard_map/ppermute | solution.py:32
  24.3 1.1 all_to_all.18
  25.5 11.9 %all-to-all-start = ((bf16[64,2,2688]{2,1,0:T(2,128)(2,1)}), bf16[64,2,2688]{2,1,0:T(2,128)(2,1)S(1)}, u32[]{:S(2)}, u32[]{:S(2)}) async-start(bf16[64,2,2688]{2,1,0:T(2,128)(2,1)} %all_to_all.18), calls=%async_computation | async-start | bytes 1376256 | tf_op jit(solution)/shard_map/all_to_all | solution.py:265
  37.7 3.1 %shard_map.103 = (f32[5,4,8,768]{3,2,1,0:T(8,128)}, bf16[4,8,768]{2,1,0:T(8,128)(2,1)}, bf16[5,1,8,768]{3,2,1,0:T(8,128)(2,1)}, bf16[5,1,8,768]{3,2,1,0:T(8,128)...) custom-call(f32[5,5]{1,0:T(8,128)} %c_ref.3, ...), custom_call_target="tpu_custom_call" | custom-call | tf_op jit(solution)/shard_map/pallas_call | solution.py:266
  40.8 4.6 %collective-permute-start.6 = (bf16[5,1,8,768]{3,2,1,0:T(8,128)(2,1)}, bf16[5,1,8,768]{3,2,1,0:T(8,128)(2,1)S(1)}, u32[]{:S(2)}, u32[]{:S(2)}) collective-permute-start(bf16[5,1,8,768]{3,2,1,0:T(8,128)(2,1)} %get-tuple-element.28), channel_id=1, source_target_pairs={{0,64},{64,128},{128,192},{192,256},{256,320},{320,384},{384,448},... | collective-permute-start | bytes 184328 | tf_op jit(solution)/shard_map/ppermute | solution.py:277
  45.4 1.3 %collective-permute-start.7 = (bf16[5,1,8,768]{3,2,1,0:T(8,128)(2,1)}, bf16[5,1,8,768]{3,2,1,0:T(8,128)(2,1)S(1)}, u32[]{:S(2)}, u32[]{:S(2)}) collective-permute-start(bf16[5,1,8,768]{3,2,1,0:T(8,128)(2,1)} %get-tuple-element.29), channel_id=1, source_target_pairs={{64,0},{128,64},{192,128},{256,192},{320,256},{384,320},{448,384},... | collective-permute-start | bytes 184328 | tf_op jit(solution)/shard_map/ppermute | solution.py:278
  46.7 3.3 %collective-permute-start.8 = (bf16[5,4,1,768]{3,2,1,0:T(2,128)(2,1)}, bf16[5,4,1,768]{3,2,1,0:T(2,128)(2,1)S(1)}, u32[]{:S(2)}, u32[]{:S(2)}) collective-permute-start(bf16[5,4,1,768]{3,2,1,0:T(2,128)(2,1)} %get-tuple-element.30), channel_id=1, source_target_pairs={{0,8},{8,16},{16,24},{24,32},{32,40},{40,48},{48,56},{1,9},{9,17},... | collective-permute-start | bytes 92168 | tf_op jit(solution)/shard_map/ppermute | solution.py:277
  50.0 1.3 %collective-permute-start.9 = (bf16[5,4,1,768]{3,2,1,0:T(2,128)(2,1)}, bf16[5,4,1,768]{3,2,1,0:T(2,128)(2,1)S(1)}, u32[]{:S(2)}, u32[]{:S(2)}) collective-permute-start(bf16[5,4,1,768]{3,2,1,0:T(2,128)(2,1)} %get-tuple-element.31), channel_id=1, source_target_pairs={{8,0},{16,8},{24,16},{32,24},{40,32},{48,40},{56,48},{9,1},{17,9},... | collective-permute-start | bytes 92168 | tf_op jit(solution)/shard_map/ppermute | solution.py:278
  52.1 3.9 %collective-permute-start.10 = (bf16[5,4,8,1]{3,2,1,0:T(8,128)(2,1)}, bf16[5,4,8,1]{3,2,1,0:T(8,128)(2,1)S(1)}, u32[]{:S(2)}, u32[]{:S(2)}) collective-permute-start(bf16[5,4,8,1]{3,2,1,0:T(8,128)(2,1)} %get-tuple-element.32), channel_id=1, source_target_pairs={{0,1},{1,2},{2,3},{3,4},{4,5},{5,6},{6,7},{8,9},{9,10},{10,11},{11... | collective-permute-start | bytes 968 | tf_op jit(solution)/shard_map/ppermute | solution.py:277
  56.0 3.0 %all-to-all-done = bf16[64,2,2688]{2,1,0:T(2,128)(2,1)S(1)} async-done(((bf16[64,2,2688]{2,1,0:T(2,128)(2,1)}), bf16[64,2,2688]{2,1,0:T(2,128)(2,1)S(1)}, u32[]{:S(2)}, u32[]{:S(2)}) %all-to-all-start) | async-done | bytes 688160 | tf_op jit(solution)/shard_map/all_to_all | solution.py:265
  60.8 2.2 %collective-permute-start.11 = (bf16[5,4,8,1]{3,2,1,0:T(8,128)(2,1)S(1)}, bf16[5,4,8,1]{3,2,1,0:T(8,128)(2,1)S(1)}, u32[]{:S(2)}, u32[]{:S(2)}) collective-permute-start(bf16[5,4,8,1]{3,2,1,0:T(8,128)(2,1)S(1)} %copy-done.15), channel_id=1, source_target_pairs={{1,0},{2,1},{3,2},{4,3},{5,4},{6,5},{7,6},{9,8},{10,9},{11,10},{12... | collective-permute-start | bytes 968 | tf_op jit(solution)/shard_map/ppermute | solution.py:278
  63.0 1.0 reshape.48.goal_ref
  66.8 4.9 %shard_map.104 = (bf16[5,4,8,768]{3,2,1,0:T(8,128)(2,1)}, f32[2,8,768]{2,1,0:T(8,128)}, f32[64,1]{1,0:T(8,128)}) custom-call(f32[5,5]{1,0:T(8,128)} %c_ref.3, f32[5,4,8,768]{3,2,1,0:T(8,128)} %get-tuple-element.27.s1_ref, bf16[5,4,8,768]{3,2,1,0:T(8,128)(2,1)} %s_ref.3, bf16[4,8,768]{2,1,0:T(8,128)(2,1)} %d_ref.3, bf16[5,1,8,768]{3,2,1,0:T(8,128)(2,1)} %copy-done.5, ...), custom_call_target="tpu_custom_call" | custom-call | tf_op jit(solution)/shard_map/pallas_call | solution.py:296
  71.7 18.4 %all_to_all.27 = f32[64,1,1]{2,1,0:T(1,128)S(1)} all-to-all(f32[64,1,1]{2,1,0:T(1,128)} %bitcast.18), channel_id=1, replica_groups=mesh['gx'=8,'gy'=8,'gz'=8] {'gy','gz'}, dimensions={0} | all-to-all | bytes 512 | tf_op jit(solution)/shard_map/all_to_all | solution.py:310
  91.3 12.3 %all-to-all-start.2 = ((f32[8,1,64]{2,1,0:T(1,128)}), f32[8,1,64]{2,1,0:T(1,128)S(1)}, u32[]{:S(2)}, u32[]{:S(2)}) async-start(f32[8,1,64]{2,1,0:T(1,128)} %broadcast_in_dim.27), calls=%async_computation.2 | async-start | bytes 8192 | tf_op jit(solution)/shard_map/all_to_all | solution.py:311
  105.3 4.9 %all-to-all-done.2 = f32[8,1,64]{2,1,0:T(1,128)S(1)} async-done(((f32[8,1,64]{2,1,0:T(1,128)}), f32[8,1,64]{2,1,0:T(1,128)S(1)}, u32[]{:S(2)}, u32[]{:S(2)}) %all-to-all-start.2) | async-done | bytes 2080 | tf_op jit(solution)/shard_map/all_to_all | solution.py:311
  110.8 1.2 %divide_minimum_fusion = (f32[48]{0:T(128)}, f32[48]{0:T(128)}) fusion(f32[]{:T(128)} %bitcast.7, f32[]{:T(128)} %reduce_sum.32, f32[48]{0:T(128)S(1)} %reshape.53, s32[48]{0:T(128)S(1)} %copy-done.14), kind=kLoop, calls=%fused_computation.12 | loop fusion | flops 384 | bytes 776 | tf_op jit(solution)/shard_map/min | solution.py:317
  (73 shorter events, 10.6 us)
Async XLA Ops:
  0.6 17.9 %copy-start = (bf16[128,5,2,2,128]{4,3,2,1,0:T(2,128)(2,1)S(1)}, bf16[128,5,2,2,128]{4,3,2,1,0:T(2,128)(2,1)}, u32[]{:S(2)}) copy-start(bf16[128,5,2,2,128]{4,3,2,1,0:T(2,128)(2,1)} %param.14) | copy-start | bytes 1966084
  1.6 22.7 %collective-permute-start = (bf16[5,1,8,768]{3,2,1,0:T(8,128)(2,1)S(1)}, bf16[5,1,8,768]{3,2,1,0:T(8,128)(2,1)S(1)}, u32[]{:S(2)}, u32[]{:S(2)}) collective-permute-start(bf16[5,1,8,768]{3,2,1,0:T(8,128)(2,1)S(1)} %get-tuple-element.44), channel_id=1, source_target_pairs={{0,64},{64,128},{128,192},{192,256},{256,320},{320,384},{384,448},... | collective-permute-start | bytes 184328 | tf_op jit(solution)/shard_map/ppermute | solution.py:31
  6.4 17.9 %collective-permute-start.1 = (bf16[5,1,8,768]{3,2,1,0:T(8,128)(2,1)S(1)}, bf16[5,1,8,768]{3,2,1,0:T(8,128)(2,1)S(1)}, u32[]{:S(2)}, u32[]{:S(2)}) collective-permute-start(bf16[5,1,8,768]{3,2,1,0:T(8,128)(2,1)S(1)} %get-tuple-element.43), channel_id=1, source_target_pairs={{64,0},{128,64},{192,128},{256,192},{320,256},{384,320},{448,384},... | collective-permute-start | bytes 184328 | tf_op jit(solution)/shard_map/ppermute | solution.py:32
  8.9 15.4 %collective-permute-start.2 = (bf16[5,4,1,768]{3,2,1,0:T(2,128)(2,1)S(1)}, bf16[5,4,1,768]{3,2,1,0:T(2,128)(2,1)S(1)}, u32[]{:S(2)}, u32[]{:S(2)}) collective-permute-start(bf16[5,4,1,768]{3,2,1,0:T(2,128)(2,1)S(1)} %get-tuple-element.42), channel_id=1, source_target_pairs={{0,8},{8,16},{16,24},{24,32},{32,40},{40,48},{48,56},{1,9},{9,17},... | collective-permute-start | bytes 92168 | tf_op jit(solution)/shard_map/ppermute | solution.py:31
  13.0 5.8 %copy-start.13 = (bf16[128,5]{0,1:T(8,128)(2,1)S(1)}, bf16[128,5]{0,1:T(8,128)(2,1)}, u32[]{:S(2)}) copy-start(bf16[128,5]{0,1:T(8,128)(2,1)} %param.15) | copy-start | bytes 3844
  13.0 6.0 %collective-permute-start.4 = (bf16[5,4,8,1]{3,2,1,0:T(8,128)(2,1)S(1)}, bf16[5,4,8,1]{3,2,1,0:T(8,128)(2,1)S(1)}, u32[]{:S(2)}, u32[]{:S(2)}) collective-permute-start(bf16[5,4,8,1]{3,2,1,0:T(8,128)(2,1)S(1)} %get-tuple-element.40), channel_id=1, source_target_pairs={{0,1},{1,2},{2,3},{3,4},{4,5},{5,6},{6,7},{8,9},{9,10},{10,11},{11... | collective-permute-start | bytes 968 | tf_op jit(solution)/shard_map/ppermute | solution.py:31
  17.2 7.1 %collective-permute-start.3 = (bf16[5,4,1,768]{3,2,1,0:T(2,128)(2,1)S(1)}, bf16[5,4,1,768]{3,2,1,0:T(2,128)(2,1)S(1)}, u32[]{:S(2)}, u32[]{:S(2)}) collective-permute-start(bf16[5,4,1,768]{3,2,1,0:T(2,128)(2,1)S(1)} %get-tuple-element.41), channel_id=1, source_target_pairs={{8,0},{16,8},{24,16},{32,24},{40,32},{48,40},{56,48},{9,1},{17,9},... | collective-permute-start | bytes 92168 | tf_op jit(solution)/shard_map/ppermute | solution.py:32
  18.9 2.0 %copy-start.9 = (bf16[5,4,8,1]{3,2,1,0:T(8,128)(2,1)}, bf16[5,4,8,1]{3,2,1,0:T(8,128)(2,1)S(1)}, u32[]{:S(2)}) copy-start(bf16[5,4,8,1]{3,2,1,0:T(8,128)(2,1)S(1)} %collective-permute-done.4.zlo) | copy-start | bytes 964
  19.0 5.3 %collective-permute-start.5 = (bf16[5,4,8,1]{3,2,1,0:T(8,128)(2,1)S(1)}, bf16[5,4,8,1]{3,2,1,0:T(8,128)(2,1)S(1)}, u32[]{:S(2)}, u32[]{:S(2)}) collective-permute-start(bf16[5,4,8,1]{3,2,1,0:T(8,128)(2,1)S(1)} %get-tuple-element.39), channel_id=1, source_target_pairs={{1,0},{2,1},{3,2},{4,3},{5,4},{6,5},{7,6},{9,8},{10,9},{11,10},{12... | collective-permute-start | bytes 968 | tf_op jit(solution)/shard_map/ppermute | solution.py:32
  24.3 1.2 %copy-start.10 = (bf16[5,4,8,1]{3,2,1,0:T(8,128)(2,1)}, bf16[5,4,8,1]{3,2,1,0:T(8,128)(2,1)S(1)}, u32[]{:S(2)}) copy-start(bf16[5,4,8,1]{3,2,1,0:T(8,128)(2,1)S(1)} %collective-permute-done.5.zhi) | copy-start | bytes 964
  24.3 1.2 %copy-start.3 = (bf16[5,4,1,768]{3,2,1,0:T(2,128)(2,1)}, bf16[5,4,1,768]{3,2,1,0:T(2,128)(2,1)S(1)}, u32[]{:S(2)}) copy-start(bf16[5,4,1,768]{3,2,1,0:T(2,128)(2,1)S(1)} %collective-permute-done.2.ylo) | copy-start | bytes 92164
  24.3 1.2 %copy-start.4 = (bf16[5,4,1,768]{3,2,1,0:T(2,128)(2,1)}, bf16[5,4,1,768]{3,2,1,0:T(2,128)(2,1)S(1)}, u32[]{:S(2)}) copy-start(bf16[5,4,1,768]{3,2,1,0:T(2,128)(2,1)S(1)} %collective-permute-done.3.yhi) | copy-start | bytes 92164
  24.3 1.1 %copy-start.1 = (bf16[5,1,8,768]{3,2,1,0:T(8,128)(2,1)}, bf16[5,1,8,768]{3,2,1,0:T(8,128)(2,1)S(1)}, u32[]{:S(2)}) copy-start(bf16[5,1,8,768]{3,2,1,0:T(8,128)(2,1)S(1)} %collective-permute-done.xlo) | copy-start | bytes 184324
  25.5 12.0 %copy-start.16 = (s32[48,1]{0,1:T(1,128)S(1)}, s32[48,1]{0,1:T(1,128)}, u32[]{:S(2)}) copy-start(s32[48,1]{0,1:T(1,128)} %param.11) | copy-start | bytes 580
  25.5 12.2 %copy-start.14 = (s32[48]{0:T(128)S(1)}, s32[48]{0:T(128)}, u32[]{:S(2)}) copy-start(s32[48]{0:T(128)} %param.12) | copy-start | bytes 580
  25.5 33.5 %all-to-all-start = ((bf16[64,2,2688]{2,1,0:T(2,128)(2,1)}), bf16[64,2,2688]{2,1,0:T(2,128)(2,1)S(1)}, u32[]{:S(2)}, u32[]{:S(2)}) async-start(bf16[64,2,2688]{2,1,0:T(2,128)(2,1)} %all_to_all.18), calls=%async_computation | async-start | bytes 1376256 | tf_op jit(solution)/shard_map/all_to_all | solution.py:265
  40.8 25.3 %collective-permute-start.6 = (bf16[5,1,8,768]{3,2,1,0:T(8,128)(2,1)}, bf16[5,1,8,768]{3,2,1,0:T(8,128)(2,1)S(1)}, u32[]{:S(2)}, u32[]{:S(2)}) collective-permute-start(bf16[5,1,8,768]{3,2,1,0:T(8,128)(2,1)} %get-tuple-element.28), channel_id=1, source_target_pairs={{0,64},{64,128},{128,192},{192,256},{256,320},{320,384},{384,448},... | collective-permute-start | bytes 184328 | tf_op jit(solution)/shard_map/ppermute | solution.py:277
  45.4 20.7 %collective-permute-start.7 = (bf16[5,1,8,768]{3,2,1,0:T(8,128)(2,1)}, bf16[5,1,8,768]{3,2,1,0:T(8,128)(2,1)S(1)}, u32[]{:S(2)}, u32[]{:S(2)}) collective-permute-start(bf16[5,1,8,768]{3,2,1,0:T(8,128)(2,1)} %get-tuple-element.29), channel_id=1, source_target_pairs={{64,0},{128,64},{192,128},{256,192},{320,256},{384,320},{448,384},... | collective-permute-start | bytes 184328 | tf_op jit(solution)/shard_map/ppermute | solution.py:278
  46.7 19.4 %collective-permute-start.8 = (bf16[5,4,1,768]{3,2,1,0:T(2,128)(2,1)}, bf16[5,4,1,768]{3,2,1,0:T(2,128)(2,1)S(1)}, u32[]{:S(2)}, u32[]{:S(2)}) collective-permute-start(bf16[5,4,1,768]{3,2,1,0:T(2,128)(2,1)} %get-tuple-element.30), channel_id=1, source_target_pairs={{0,8},{8,16},{16,24},{24,32},{32,40},{40,48},{48,56},{1,9},{9,17},... | collective-permute-start | bytes 92168 | tf_op jit(solution)/shard_map/ppermute | solution.py:277
  50.0 16.1 %collective-permute-start.9 = (bf16[5,4,1,768]{3,2,1,0:T(2,128)(2,1)}, bf16[5,4,1,768]{3,2,1,0:T(2,128)(2,1)S(1)}, u32[]{:S(2)}, u32[]{:S(2)}) collective-permute-start(bf16[5,4,1,768]{3,2,1,0:T(2,128)(2,1)} %get-tuple-element.31), channel_id=1, source_target_pairs={{8,0},{16,8},{24,16},{32,24},{40,32},{48,40},{56,48},{9,1},{17,9},... | collective-permute-start | bytes 92168 | tf_op jit(solution)/shard_map/ppermute | solution.py:278
  52.1 8.1 %collective-permute-start.10 = (bf16[5,4,8,1]{3,2,1,0:T(8,128)(2,1)}, bf16[5,4,8,1]{3,2,1,0:T(8,128)(2,1)S(1)}, u32[]{:S(2)}, u32[]{:S(2)}) collective-permute-start(bf16[5,4,8,1]{3,2,1,0:T(8,128)(2,1)} %get-tuple-element.32), channel_id=1, source_target_pairs={{0,1},{1,2},{2,3},{3,4},{4,5},{5,6},{6,7},{8,9},{9,10},{10,11},{11... | collective-permute-start | bytes 968 | tf_op jit(solution)/shard_map/ppermute | solution.py:277
  60.2 5.1 %copy-start.11 = (bf16[5,4,8,1]{3,2,1,0:T(8,128)(2,1)}, bf16[5,4,8,1]{3,2,1,0:T(8,128)(2,1)S(1)}, u32[]{:S(2)}) copy-start(bf16[5,4,8,1]{3,2,1,0:T(8,128)(2,1)S(1)} %collective-permute-done.10.zlo) | copy-start | bytes 964
  60.8 5.3 %collective-permute-start.11 = (bf16[5,4,8,1]{3,2,1,0:T(8,128)(2,1)S(1)}, bf16[5,4,8,1]{3,2,1,0:T(8,128)(2,1)S(1)}, u32[]{:S(2)}, u32[]{:S(2)}) collective-permute-start(bf16[5,4,8,1]{3,2,1,0:T(8,128)(2,1)S(1)} %copy-done.15), channel_id=1, source_target_pairs={{1,0},{2,1},{3,2},{4,3},{5,4},{6,5},{7,6},{9,8},{10,9},{11,10},{12... | collective-permute-start | bytes 968 | tf_op jit(solution)/shard_map/ppermute | solution.py:278
  91.3 18.9 %all-to-all-start.2 = ((f32[8,1,64]{2,1,0:T(1,128)}), f32[8,1,64]{2,1,0:T(1,128)S(1)}, u32[]{:S(2)}, u32[]{:S(2)}) async-start(f32[8,1,64]{2,1,0:T(1,128)} %broadcast_in_dim.27), calls=%async_computation.2 | async-start | bytes 8192 | tf_op jit(solution)/shard_map/all_to_all | solution.py:311
  (7 other events, 5.2 us)

commit v7 on v6

--- a/solution.py
+++ b/solution.py
@@ -195,8 +195,8 @@
         eff_ref[x] = (d * (1.0 + 0.5 * jnp.tanh(s1[0]))).astype(jnp.bfloat16)
 
 
-def adjoint_kernel(c_ref, s1_ref, s_ref, d_ref, xlo, xhi, ylo, yhi, zlo, zhi, eff_ref, goal_ref, react_ref,
-                   w_ref, enr_ref, part_ref, spread_ref):
+def adjoint_kernel(c_ref, slot_ref, s1_ref, s_ref, d_ref, xlo, xhi, ylo, yhi, zlo, zhi, eff_ref, arr_ref,
+                   w_ref, enr_ref, part_ref, spread_ref, goal_ref, react_ref):
     nf, nx, ny, nz = s_ref.shape
     geo = _masks(ny, nz)
     f32 = jnp.float32
@@ -211,9 +211,21 @@
             lap = _lap_halo(s1[f][x], xm, xp, ylo[f, x].astype(f32), yhi[f, x].astype(f32),
                             zlo[f, x].astype(f32), zhi[f, x].astype(f32), geo)
             residual[f][x] = d * lap + cs[f] - (s1[f][x] - s_ref[f, x].astype(f32)) / primal_step
+    for b in range(NBX * NBY * NBZ):
+        bx, by, bz = b // (NBY * NBZ), (b // NBZ) % NBY, b % NBZ
+        rows = arr_ref[slot_ref[b]].astype(f32)
+        lanes = pl.ds(bz * BZ, BZ)
+        for f in range(nf):
+            rate = jnp.broadcast_to(rows[nf * BX * BY:nf * BX * BY + 1, f:f + 1], (1, BZ))
+            for i in range(BX):
+                for j in range(BY):
+                    r = (f * BX + i) * BY + j
+                    y = pl.ds(by * BY + j, 1)
+                    goal_ref[f, bx * BX + i, y, lanes] = rows[r:r + 1, :]
+                    react_ref[f, bx * BX + i, y, lanes] = rate
     eff = [eff_ref[x].astype(f32) for x in range(nx)]
-    goal = [[goal_ref[f, x].astype(f32) for x in range(nx)] for f in range(nf)]
-    react = [[react_ref[f, x].astype(f32) for x in range(nx)] for f in range(nf)]
+    goal = [[goal_ref[f, x] for x in range(nx)] for f in range(nf)]
+    react = [[react_ref[f, x] for x in range(nx)] for f in range(nf)]
     dual = [list(row) for row in goal]
     for _ in range(SECTIONS):
         new = [[None] * nx for _ in range(nf)]
@@ -246,11 +258,10 @@
     dims = (1, 2, 3)
 
     slots = goal_weight.shape[0]
-    cells = FIELDS * BX * BY * BZ
     packed = jnp.concatenate(
         [
-            goal_weight.reshape(slots, cells),
-            jnp.pad(reaction, ((0, 0), (0, BZ - FIELDS))),
+            goal_weight.reshape(slots, FIELDS * BX * BY, BZ),
+            jnp.pad(reaction, ((0, 0), (0, BZ - FIELDS)))[:, None, :],
         ],
         axis=1,
     )
@@ -285,9 +296,6 @@
     capacity = goal_weight.shape[0] // (lax.axis_size("gy") * lax.axis_size("gz"))
     slot_of = targets * capacity + rank
 
-    mine = arrived[slot_of]
-    goal = to_cells(mine[:, :cells].reshape(-1, FIELDS, BX, BY, BZ))
-    react = per_block_cells(mine[:, cells : cells + FIELDS])
     weights = jnp.exp2(2.0 * levels.astype(jnp.float32))
     weight_cells = jnp.broadcast_to(
         weights.reshape(NBX, NBY, 1, NBZ, 1), (NBX, NBY, BY, NBZ, BZ)
@@ -300,9 +308,10 @@
             jax.ShapeDtypeStruct((nx // BX, ny, nz), f32),
             jax.ShapeDtypeStruct((plane, 1), f32),
         ],
-        in_specs=[smem] + [vmem] * 13,
+        in_specs=[smem, smem] + [vmem] * 12,
         out_specs=[vmem] * 3,
-    )(coupling, section_one, state, diffusivity, *section_halo, effective, goal, react, weight_cells)
+        scratch_shapes=[pltpu.VMEM(state.shape, f32), pltpu.VMEM(state.shape, f32)],
+    )(coupling, slot_of, section_one, state, diffusivity, *section_halo, effective, arrived, weight_cells)
     sums = jnp.sum(part.reshape(nx // BX, ny // BY, BY, nz // BZ, BZ), axis=(2, 4)).reshape(-1)
     indicator = weights * sums
 

time: 113 us -> 110 us (0.973)
  waiting for transfers between devices: 12 us -> 8.44 us
  local copies, waits for them, and re-layouts: 11.5 us -> 8.29 us
  blocking collectives: 18.4 us -> 21.4 us
  other arithmetic: 2.76 us -> 4.21 us
    ppermute x3, starting transfers between devices: 4.5 us -> 11.4 us  [faces(): above = lax.ppermute(head, axis, [(i + 1, i) for i in range(ends)])]
    ppermute x3, waiting for transfers between devices: 3.33 us -> 0.01 us  [faces(): above = lax.ppermute(head, axis, [(i + 1, i) for i in range(ends)])]
    all_to_all x1, waiting for transfers between devices: 3 us -> 0.01 us  [shards(): arrived = lax.all_to_all(packed, ('gy', 'gz'), 0, 0, tiled=True)]
    all_to_all x1, blocking collectives: 18.4 us -> 21.4 us  [shards(): level_one = lax.all_to_all(spread, ('gy', 'gz'), 0, 0, tiled=True)]
    ppermute x3, waiting for transfers between devices: 0.79 us -> 3.46 us  [shards(): lax.ppermute(low, axis, [(i + 1, i) for i in range(ends)])]
    all_to_all x1, starting transfers between devices: 11.9 us -> 9.48 us  [shards(): arrived = lax.all_to_all(packed, ('gy', 'gz'), 0, 0, tiled=True)]
    ppermute x3, starting transfers between devices: 12.3 us -> 9.9 us  [faces(): below = lax.ppermute(tail, axis, [(i, i + 1) for i in range(ends)])]
    reshape x4 -> x1, local copies, waits for them, and re-layouts: 2.32 us -> 0.44 us  [shards(): goal_weight.reshape(slots, FIELDS * BX * BY, BZ)]
  transfers between devices with their start and end apart: 14 -> 14, of which waited for: 4 -> 3; matrix products, arithmetic and copies ran while one was open for 7% -> 7% of each run, Pallas kernels for 3% -> 3%
where the time goes in v7:
time: 110 us; the launch traced here: 109 us
  starting transfers between devices  56.8 us (52%)
  blocking collectives  21.4 us (19%)
  Pallas kernels  8.7 us (8%)
  waiting for transfers between devices  8.44 us (8%)
  local copies, waits for them, and re-layouts  8.29 us (8%)
  other arithmetic  4.21 us (4%)
  between operations  1.61 us (1%)
    all_to_all x1, blocking collectives, shards(): level_one = lax.all_to_all(spread, ('gy', 'gz'), 0, 0, tiled=True)  21.4 us
    ppermute x3, starting transfers between devices, faces(): above = lax.ppermute(head, axis, [(i + 1, i) for i in range(ends)])  11.4 us
    all_to_all x1, starting transfers between devices, shards(): lax.all_to_all(jnp.broadcast_to(level_one.reshape(1, plane), (across, pla...  10.9 us
    ppermute x3, starting transfers between devices, shards(): lax.ppermute(high, axis, [(i, i + 1) for i in range(ends)])  10.6 us
    ppermute x3, starting transfers between devices, faces(): below = lax.ppermute(tail, axis, [(i, i + 1) for i in range(ends)])  9.9 us
    all_to_all x1, starting transfers between devices, shards(): arrived = lax.all_to_all(packed, ('gy', 'gz'), 0, 0, tiled=True)  9.48 us
    pallas_call x1, Pallas kernels, shards(): pl.pallas_call(adjoint_kernel, out_shape=[jax.ShapeDtypeStruct(state.shap...  5.62 us
    all_to_all x1, waiting for transfers between devices, shards(): lax.all_to_all(jnp.broadcast_to(level_one.reshape(1, plane), (across, pla...  4.88 us
  transfers between devices with their start and end apart: 14, of which 3 were waited for; matrix products, arithmetic and copies ran while one was open for 7% of the time, Pallas kernels for 3%

profile of v7, /device:TPU:1, one launch (start us, length us, event | category | flops | bytes accessed | tf_op | source)
XLA Modules:
  0.0 109.4 jit_solution(4955261680613721232)
XLA Ops:
  0.6 0.9 fusion.1
  1.6 8.8 %collective-permute-start.5 = (bf16[5,4,8,1]{3,2,1,0:T(8,128)(2,1)S(1)}, bf16[5,4,8,1]{3,2,1,0:T(8,128)(2,1)S(1)}, u32[]{:S(2)}, u32[]{:S(2)}) collective-permute-start(bf16[5,4,8,1]{3,2,1,0:T(8,128)(2,1)S(1)} %get-tuple-element.39), channel_id=1, source_target_pairs={{1,0},{2,1},{3,2},{4,3},{5,4},{6,5},{7,6},{9,8},{10,9},{11,10},{12... | collective-permute-start | bytes 968 | tf_op jit(solution)/shard_map/ppermute | solution.py:32
  10.4 1.9 %collective-permute-start.4 = (bf16[5,4,8,1]{3,2,1,0:T(8,128)(2,1)S(1)}, bf16[5,4,8,1]{3,2,1,0:T(8,128)(2,1)S(1)}, u32[]{:S(2)}, u32[]{:S(2)}) collective-permute-start(bf16[5,4,8,1]{3,2,1,0:T(8,128)(2,1)S(1)} %get-tuple-element.40), channel_id=1, source_target_pairs={{0,1},{1,2},{2,3},{3,4},{4,5},{5,6},{6,7},{8,9},{9,10},{10,11},{11... | collective-permute-start | bytes 968 | tf_op jit(solution)/shard_map/ppermute | solution.py:31
  12.3 0.9 fusion.3
  13.2 1.3 %collective-permute-start.1 = (bf16[5,1,8,768]{3,2,1,0:T(8,128)(2,1)S(1)}, bf16[5,1,8,768]{3,2,1,0:T(8,128)(2,1)S(1)}, u32[]{:S(2)}, u32[]{:S(2)}) collective-permute-start(bf16[5,1,8,768]{3,2,1,0:T(8,128)(2,1)S(1)} %get-tuple-element.43), channel_id=1, source_target_pairs={{64,0},{128,64},{192,128},{256,192},{320,256},{384,320},{448,384},... | collective-permute-start | bytes 184328 | tf_op jit(solution)/shard_map/ppermute | solution.py:32
  14.5 4.0 %collective-permute-start = (bf16[5,1,8,768]{3,2,1,0:T(8,128)(2,1)S(1)}, bf16[5,1,8,768]{3,2,1,0:T(8,128)(2,1)S(1)}, u32[]{:S(2)}, u32[]{:S(2)}) collective-permute-start(bf16[5,1,8,768]{3,2,1,0:T(8,128)(2,1)S(1)} %get-tuple-element.44), channel_id=1, source_target_pairs={{0,64},{64,128},{128,192},{192,256},{256,320},{320,384},{384,448},... | collective-permute-start | bytes 184328 | tf_op jit(solution)/shard_map/ppermute | solution.py:31
  18.5 1.2 %fusion.2 = (bf16[5,4,1,768]{3,2,1,0:T(2,128)(2,1)S(1)}, bf16[5,4,1,768]{3,2,1,0:T(2,128)(2,1)S(1)}) fusion(bf16[5,4,8,768]{3,2,1,0:T(8,128)(2,1)} %s_ref.3), kind=kLoop, calls=%fused_computation.10 | loop fusion | bytes 122880 | tf_op jit(solution)/shard_map/slice | solution.py:29
  19.6 1.3 %collective-permute-start.3 = (bf16[5,4,1,768]{3,2,1,0:T(2,128)(2,1)S(1)}, bf16[5,4,1,768]{3,2,1,0:T(2,128)(2,1)S(1)}, u32[]{:S(2)}, u32[]{:S(2)}) collective-permute-start(bf16[5,4,1,768]{3,2,1,0:T(2,128)(2,1)S(1)} %get-tuple-element.41), channel_id=1, source_target_pairs={{8,0},{16,8},{24,16},{32,24},{40,32},{48,40},{56,48},{9,1},{17,9},... | collective-permute-start | bytes 92168 | tf_op jit(solution)/shard_map/ppermute | solution.py:32
  22.4 4.0 %collective-permute-start.2 = (bf16[5,4,1,768]{3,2,1,0:T(2,128)(2,1)S(1)}, bf16[5,4,1,768]{3,2,1,0:T(2,128)(2,1)S(1)}, u32[]{:S(2)}, u32[]{:S(2)}) collective-permute-start(bf16[5,4,1,768]{3,2,1,0:T(2,128)(2,1)S(1)} %get-tuple-element.42), channel_id=1, source_target_pairs={{0,8},{8,16},{16,24},{24,32},{32,40},{40,48},{48,56},{1,9},{9,17},... | collective-permute-start | bytes 92168 | tf_op jit(solution)/shard_map/ppermute | solution.py:31
  26.4 1.1 %pad_maximum_fusion = bf16[128,21,128]{2,1,0:T(8,128)(2,1)} fusion(bf16[128,1,128]{2,1,0:T(2,128)(2,1)S(1)} %copy.34, bf16[128,20,128]{2,1,0:T(8,128)(2,1)S(1)} %copy.33), kind=kLoop, calls=%fused_computation | loop fusion | flops 1376256 | bytes 1376256 | tf_op jit(solution)/shard_map/concatenate | solution.py:261
  28.4 9.5 %all-to-all-start = ((bf16[128,21,128]{2,1,0:T(8,128)(2,1)}), bf16[128,21,128]{2,1,0:T(8,128)(2,1)S(1)}, u32[]{:S(2)}, u32[]{:S(2)}) async-start(bf16[128,21,128]{2,1,0:T(8,128)(2,1)} %pad_maximum_fusion), calls=%async_computation | async-start | bytes 1572864 | tf_op jit(solution)/shard_map/all_to_all | solution.py:276
  38.6 3.1 %shard_map.103 = (f32[5,4,8,768]{3,2,1,0:T(8,128)}, bf16[4,8,768]{2,1,0:T(8,128)(2,1)}, bf16[5,1,8,768]{3,2,1,0:T(8,128)(2,1)}, bf16[5,1,8,768]{3,2,1,0:T(8,128)...) custom-call(f32[5,5]{1,0:T(8,128)} %c_ref.3, ...), custom_call_target="tpu_custom_call" | custom-call | tf_op jit(solution)/shard_map/pallas_call | solution.py:277
  41.7 3.5 %collective-permute-start.10 = (bf16[5,4,8,1]{3,2,1,0:T(8,128)(2,1)}, bf16[5,4,8,1]{3,2,1,0:T(8,128)(2,1)S(1)}, u32[]{:S(2)}, u32[]{:S(2)}) collective-permute-start(bf16[5,4,8,1]{3,2,1,0:T(8,128)(2,1)} %get-tuple-element.32), channel_id=1, source_target_pairs={{0,1},{1,2},{2,3},{3,4},{4,5},{5,6},{6,7},{8,9},{9,10},{10,11},{11... | collective-permute-start | bytes 968 | tf_op jit(solution)/shard_map/ppermute | solution.py:288
  45.2 1.9 %collective-permute-start.11 = (bf16[5,4,8,1]{3,2,1,0:T(8,128)(2,1)}, bf16[5,4,8,1]{3,2,1,0:T(8,128)(2,1)S(1)}, u32[]{:S(2)}, u32[]{:S(2)}) collective-permute-start(bf16[5,4,8,1]{3,2,1,0:T(8,128)(2,1)} %get-tuple-element.33), channel_id=1, source_target_pairs={{1,0},{2,1},{3,2},{4,3},{5,4},{6,5},{7,6},{9,8},{10,9},{11,10},{12... | collective-permute-start | bytes 968 | tf_op jit(solution)/shard_map/ppermute | solution.py:289
  47.1 4.0 %collective-permute-start.6 = (bf16[5,1,8,768]{3,2,1,0:T(8,128)(2,1)}, bf16[5,1,8,768]{3,2,1,0:T(8,128)(2,1)S(1)}, u32[]{:S(2)}, u32[]{:S(2)}) collective-permute-start(bf16[5,1,8,768]{3,2,1,0:T(8,128)(2,1)} %get-tuple-element.28), channel_id=1, source_target_pairs={{0,64},{64,128},{128,192},{192,256},{256,320},{320,384},{384,448},... | collective-permute-start | bytes 184328 | tf_op jit(solution)/shard_map/ppermute | solution.py:288
  51.1 1.3 %collective-permute-start.7 = (bf16[5,1,8,768]{3,2,1,0:T(8,128)(2,1)}, bf16[5,1,8,768]{3,2,1,0:T(8,128)(2,1)S(1)}, u32[]{:S(2)}, u32[]{:S(2)}) collective-permute-start(bf16[5,1,8,768]{3,2,1,0:T(8,128)(2,1)} %get-tuple-element.29), channel_id=1, source_target_pairs={{64,0},{128,64},{192,128},{256,192},{320,256},{384,320},{448,384},... | collective-permute-start | bytes 184328 | tf_op jit(solution)/shard_map/ppermute | solution.py:289
  52.4 3.1 %collective-permute-start.8 = (bf16[5,4,1,768]{3,2,1,0:T(2,128)(2,1)}, bf16[5,4,1,768]{3,2,1,0:T(2,128)(2,1)S(1)}, u32[]{:S(2)}, u32[]{:S(2)}) collective-permute-start(bf16[5,4,1,768]{3,2,1,0:T(2,128)(2,1)} %get-tuple-element.30), channel_id=1, source_target_pairs={{0,8},{8,16},{16,24},{24,32},{32,40},{40,48},{48,56},{1,9},{9,17},... | collective-permute-start | bytes 92168 | tf_op jit(solution)/shard_map/ppermute | solution.py:288
  55.5 1.3 %collective-permute-start.9 = (bf16[5,4,1,768]{3,2,1,0:T(2,128)(2,1)}, bf16[5,4,1,768]{3,2,1,0:T(2,128)(2,1)S(1)}, u32[]{:S(2)}, u32[]{:S(2)}) collective-permute-start(bf16[5,4,1,768]{3,2,1,0:T(2,128)(2,1)} %get-tuple-element.31), channel_id=1, source_target_pairs={{8,0},{16,8},{24,16},{32,24},{40,32},{48,40},{56,48},{9,1},{17,9},... | collective-permute-start | bytes 92168 | tf_op jit(solution)/shard_map/ppermute | solution.py:289
  57.7 3.5 %collective-permute-done.9.yhi = bf16[5,4,1,768]{3,2,1,0:T(2,128)(2,1)S(1)} collective-permute-done((bf16[5,4,1,768]{3,2,1,0:T(2,128)(2,1)}, bf16[5,4,1,768]{3,2,1,0:T(2,128)(2,1)S(1)}, u32[]{:S(2)}, u32[]{:S(2)}) %collective-permute-start.9) | collective-permute-done | bytes 30752 | tf_op jit(solution)/shard_map/ppermute | solution.py:289
  62.1 5.6 %shard_map.104 = (bf16[5,4,8,768]{3,2,1,0:T(8,128)(2,1)}, f32[2,8,768]{2,1,0:T(8,128)}, f32[64,1]{1,0:T(8,128)}) custom-call(f32[5,5]{1,0:T(8,128)} %c_ref.3, s32[48]{0:T(128)} %multiply_add_fusion.slot_ref, f32[5,4,8,768]{3,2,1,0:T(8,128)} %get-tuple-element.27.s1_ref, bf16[5,4,8,768]{3,2,1,0:T(8,128)(2,1)} %s_ref.3, bf16[4,8,768]{2,1,0:T(8,128)(2,1)} %d_ref.3, ...), custom_call_target="tpu_custom_call" | custom-call | tf_op jit(solution)/shard_map/pallas_call | solution.py:304
  67.7 21.4 %all_to_all.20 = f32[64,1,1]{2,1,0:T(1,128)S(1)} all-to-all(f32[64,1,1]{2,1,0:T(1,128)} %bitcast.9), channel_id=1, replica_groups=mesh['gx'=8,'gy'=8,'gz'=8] {'gy','gz'}, dimensions={0} | all-to-all | bytes 512 | tf_op jit(solution)/shard_map/all_to_all | solution.py:319
  90.3 10.9 %all-to-all-start.2 = ((f32[8,1,64]{2,1,0:T(1,128)}), f32[8,1,64]{2,1,0:T(1,128)S(1)}, u32[]{:S(2)}, u32[]{:S(2)}) async-start(f32[8,1,64]{2,1,0:T(1,128)} %broadcast_in_dim.23), calls=%async_computation.2 | async-start | bytes 8192 | tf_op jit(solution)/shard_map/all_to_all | solution.py:320
  102.8 4.9 %all-to-all-done.2 = f32[8,1,64]{2,1,0:T(1,128)S(1)} async-done(((f32[8,1,64]{2,1,0:T(1,128)}), f32[8,1,64]{2,1,0:T(1,128)S(1)}, u32[]{:S(2)}, u32[]{:S(2)}) %all-to-all-start.2) | async-done | bytes 2080 | tf_op jit(solution)/shard_map/all_to_all | solution.py:320
  108.3 1.1 %divide_minimum_fusion = (f32[48]{0:T(128)}, f32[48]{0:T(128)}) fusion(f32[]{:T(128)} %bitcast.5, f32[]{:T(128)} %reduce_sum.29, f32[48]{0:T(128)S(1)} %reshape.37, s32[48]{0:T(128)S(1)} %copy-done.14), kind=kLoop, calls=%fused_computation.5 | loop fusion | flops 384 | bytes 776 | tf_op jit(solution)/shard_map/min | solution.py:326
  (61 shorter events, 7.4 us)
Async XLA Ops:
  0.6 21.2 %copy-start.1 = (bf16[128,5,2,2,128]{4,3,2,1,0:T(2,128)(2,1)S(1)}, bf16[128,5,2,2,128]{4,3,2,1,0:T(2,128)(2,1)}, u32[]{:S(2)}) copy-start(bf16[128,5,2,2,128]{4,3,2,1,0:T(2,128)(2,1)} %param.14) | copy-start | bytes 1966084
  1.6 20.8 %collective-permute-start.5 = (bf16[5,4,8,1]{3,2,1,0:T(8,128)(2,1)S(1)}, bf16[5,4,8,1]{3,2,1,0:T(8,128)(2,1)S(1)}, u32[]{:S(2)}, u32[]{:S(2)}) collective-permute-start(bf16[5,4,8,1]{3,2,1,0:T(8,128)(2,1)S(1)} %get-tuple-element.39), channel_id=1, source_target_pairs={{1,0},{2,1},{3,2},{4,3},{5,4},{6,5},{7,6},{9,8},{10,9},{11,10},{12... | collective-permute-start | bytes 968 | tf_op jit(solution)/shard_map/ppermute | solution.py:32
  10.4 17.2 %collective-permute-start.4 = (bf16[5,4,8,1]{3,2,1,0:T(8,128)(2,1)S(1)}, bf16[5,4,8,1]{3,2,1,0:T(8,128)(2,1)S(1)}, u32[]{:S(2)}, u32[]{:S(2)}) collective-permute-start(bf16[5,4,8,1]{3,2,1,0:T(8,128)(2,1)S(1)} %get-tuple-element.40), channel_id=1, source_target_pairs={{0,1},{1,2},{2,3},{3,4},{4,5},{5,6},{6,7},{8,9},{9,10},{10,11},{11... | collective-permute-start | bytes 968 | tf_op jit(solution)/shard_map/ppermute | solution.py:31
  13.2 14.5 %collective-permute-start.1 = (bf16[5,1,8,768]{3,2,1,0:T(8,128)(2,1)S(1)}, bf16[5,1,8,768]{3,2,1,0:T(8,128)(2,1)S(1)}, u32[]{:S(2)}, u32[]{:S(2)}) collective-permute-start(bf16[5,1,8,768]{3,2,1,0:T(8,128)(2,1)S(1)} %get-tuple-element.43), channel_id=1, source_target_pairs={{64,0},{128,64},{192,128},{256,192},{320,256},{384,320},{448,384},... | collective-permute-start | bytes 184328 | tf_op jit(solution)/shard_map/ppermute | solution.py:32
  14.5 13.2 %collective-permute-start = (bf16[5,1,8,768]{3,2,1,0:T(8,128)(2,1)S(1)}, bf16[5,1,8,768]{3,2,1,0:T(8,128)(2,1)S(1)}, u32[]{:S(2)}, u32[]{:S(2)}) collective-permute-start(bf16[5,1,8,768]{3,2,1,0:T(8,128)(2,1)S(1)} %get-tuple-element.44), channel_id=1, source_target_pairs={{0,64},{64,128},{128,192},{192,256},{256,320},{320,384},{384,448},... | collective-permute-start | bytes 184328 | tf_op jit(solution)/shard_map/ppermute | solution.py:31
  19.6 8.0 %collective-permute-start.3 = (bf16[5,4,1,768]{3,2,1,0:T(2,128)(2,1)S(1)}, bf16[5,4,1,768]{3,2,1,0:T(2,128)(2,1)S(1)}, u32[]{:S(2)}, u32[]{:S(2)}) collective-permute-start(bf16[5,4,1,768]{3,2,1,0:T(2,128)(2,1)S(1)} %get-tuple-element.41), channel_id=1, source_target_pairs={{8,0},{16,8},{24,16},{32,24},{40,32},{48,40},{56,48},{9,1},{17,9},... | collective-permute-start | bytes 92168 | tf_op jit(solution)/shard_map/ppermute | solution.py:32
  22.4 5.2 %copy-start.10 = (bf16[5,4,8,1]{3,2,1,0:T(8,128)(2,1)}, bf16[5,4,8,1]{3,2,1,0:T(8,128)(2,1)S(1)}, u32[]{:S(2)}) copy-start(bf16[5,4,8,1]{3,2,1,0:T(8,128)(2,1)S(1)} %collective-permute-done.5.zhi) | copy-start | bytes 964
  22.4 5.3 %collective-permute-start.2 = (bf16[5,4,1,768]{3,2,1,0:T(2,128)(2,1)S(1)}, bf16[5,4,1,768]{3,2,1,0:T(2,128)(2,1)S(1)}, u32[]{:S(2)}, u32[]{:S(2)}) collective-permute-start(bf16[5,4,1,768]{3,2,1,0:T(2,128)(2,1)S(1)} %get-tuple-element.42), channel_id=1, source_target_pairs={{0,8},{8,16},{16,24},{24,32},{32,40},{40,48},{48,56},{1,9},{9,17},... | collective-permute-start | bytes 92168 | tf_op jit(solution)/shard_map/ppermute | solution.py:31
  27.6 10.3 %copy-start.15 = (s32[48,1]{0,1:T(1,128)S(1)}, s32[48,1]{0,1:T(1,128)}, u32[]{:S(2)}) copy-start(s32[48,1]{0,1:T(1,128)} %param.11) | copy-start | bytes 580
  27.6 29.3 %copy-start.14 = (s32[48]{0:T(128)S(1)}, s32[48]{0:T(128)}, u32[]{:S(2)}) copy-start(s32[48]{0:T(128)} %param.12) | copy-start | bytes 580
  27.7 0.7 copy-start.3
  28.4 32.8 %all-to-all-start = ((bf16[128,21,128]{2,1,0:T(8,128)(2,1)}), bf16[128,21,128]{2,1,0:T(8,128)(2,1)S(1)}, u32[]{:S(2)}, u32[]{:S(2)}) async-start(bf16[128,21,128]{2,1,0:T(8,128)(2,1)} %pad_maximum_fusion), calls=%async_computation | async-start | bytes 1572864 | tf_op jit(solution)/shard_map/all_to_all | solution.py:276
  41.7 13.9 %collective-permute-start.10 = (bf16[5,4,8,1]{3,2,1,0:T(8,128)(2,1)}, bf16[5,4,8,1]{3,2,1,0:T(8,128)(2,1)S(1)}, u32[]{:S(2)}, u32[]{:S(2)}) collective-permute-start(bf16[5,4,8,1]{3,2,1,0:T(8,128)(2,1)} %get-tuple-element.32), channel_id=1, source_target_pairs={{0,1},{1,2},{2,3},{3,4},{4,5},{5,6},{6,7},{8,9},{9,10},{10,11},{11... | collective-permute-start | bytes 968 | tf_op jit(solution)/shard_map/ppermute | solution.py:288
  45.2 12.5 %collective-permute-start.11 = (bf16[5,4,8,1]{3,2,1,0:T(8,128)(2,1)}, bf16[5,4,8,1]{3,2,1,0:T(8,128)(2,1)S(1)}, u32[]{:S(2)}, u32[]{:S(2)}) collective-permute-start(bf16[5,4,8,1]{3,2,1,0:T(8,128)(2,1)} %get-tuple-element.33), channel_id=1, source_target_pairs={{1,0},{2,1},{3,2},{4,3},{5,4},{6,5},{7,6},{9,8},{10,9},{11,10},{12... | collective-permute-start | bytes 968 | tf_op jit(solution)/shard_map/ppermute | solution.py:289
  47.1 14.0 %collective-permute-start.6 = (bf16[5,1,8,768]{3,2,1,0:T(8,128)(2,1)}, bf16[5,1,8,768]{3,2,1,0:T(8,128)(2,1)S(1)}, u32[]{:S(2)}, u32[]{:S(2)}) collective-permute-start(bf16[5,1,8,768]{3,2,1,0:T(8,128)(2,1)} %get-tuple-element.28), channel_id=1, source_target_pairs={{0,64},{64,128},{128,192},{192,256},{256,320},{320,384},{384,448},... | collective-permute-start | bytes 184328 | tf_op jit(solution)/shard_map/ppermute | solution.py:288
  51.1 10.0 %collective-permute-start.7 = (bf16[5,1,8,768]{3,2,1,0:T(8,128)(2,1)}, bf16[5,1,8,768]{3,2,1,0:T(8,128)(2,1)S(1)}, u32[]{:S(2)}, u32[]{:S(2)}) collective-permute-start(bf16[5,1,8,768]{3,2,1,0:T(8,128)(2,1)} %get-tuple-element.29), channel_id=1, source_target_pairs={{64,0},{128,64},{192,128},{256,192},{320,256},{384,320},{448,384},... | collective-permute-start | bytes 184328 | tf_op jit(solution)/shard_map/ppermute | solution.py:289
  52.4 5.3 %collective-permute-start.8 = (bf16[5,4,1,768]{3,2,1,0:T(2,128)(2,1)}, bf16[5,4,1,768]{3,2,1,0:T(2,128)(2,1)S(1)}, u32[]{:S(2)}, u32[]{:S(2)}) collective-permute-start(bf16[5,4,1,768]{3,2,1,0:T(2,128)(2,1)} %get-tuple-element.30), channel_id=1, source_target_pairs={{0,8},{8,16},{16,24},{24,32},{32,40},{40,48},{48,56},{1,9},{9,17},... | collective-permute-start | bytes 92168 | tf_op jit(solution)/shard_map/ppermute | solution.py:288
  55.5 5.7 %copy-start.12 = (bf16[5,4,8,1]{3,2,1,0:T(8,128)(2,1)}, bf16[5,4,8,1]{3,2,1,0:T(8,128)(2,1)S(1)}, u32[]{:S(2)}) copy-start(bf16[5,4,8,1]{3,2,1,0:T(8,128)(2,1)S(1)} %collective-permute-done.10.zlo) | copy-start | bytes 964
  55.5 5.6 %collective-permute-start.9 = (bf16[5,4,1,768]{3,2,1,0:T(2,128)(2,1)}, bf16[5,4,1,768]{3,2,1,0:T(2,128)(2,1)S(1)}, u32[]{:S(2)}, u32[]{:S(2)}) collective-permute-start(bf16[5,4,1,768]{3,2,1,0:T(2,128)(2,1)} %get-tuple-element.31), channel_id=1, source_target_pairs={{8,0},{16,8},{24,16},{32,24},{40,32},{48,40},{56,48},{9,1},{17,9},... | collective-permute-start | bytes 92168 | tf_op jit(solution)/shard_map/ppermute | solution.py:289
  57.7 3.5 %copy-start.13 = (bf16[5,4,8,1]{3,2,1,0:T(8,128)(2,1)}, bf16[5,4,8,1]{3,2,1,0:T(8,128)(2,1)S(1)}, u32[]{:S(2)}) copy-start(bf16[5,4,8,1]{3,2,1,0:T(8,128)(2,1)S(1)} %collective-permute-done.11.zhi) | copy-start | bytes 964
  57.7 3.5 %copy-start.7 = (bf16[5,4,1,768]{3,2,1,0:T(2,128)(2,1)}, bf16[5,4,1,768]{3,2,1,0:T(2,128)(2,1)S(1)}, u32[]{:S(2)}) copy-start(bf16[5,4,1,768]{3,2,1,0:T(2,128)(2,1)S(1)} %collective-permute-done.8.ylo) | copy-start | bytes 92164
  61.2 0.7 copy-start.6
  61.2 0.9 copy-start
  90.3 17.4 %all-to-all-start.2 = ((f32[8,1,64]{2,1,0:T(1,128)}), f32[8,1,64]{2,1,0:T(1,128)S(1)}, u32[]{:S(2)}, u32[]{:S(2)}) async-start(f32[8,1,64]{2,1,0:T(1,128)} %broadcast_in_dim.23), calls=%async_computation.2 | async-start | bytes 8192 | tf_op jit(solution)/shard_map/all_to_all | solution.py:320
  (6 other events, 3.8 us)

commit v8 on v7

--- a/solution.py
+++ b/solution.py
@@ -272,7 +272,6 @@
     smem = pl.BlockSpec(memory_space=pltpu.SMEM)
     face_shapes = [(nf, 1, ny, nz)] * 2 + [(nf, nx, 1, nz)] * 2 + [(nf, nx, ny, 1)] * 2
     state_halo = [h for pair in faces(state, sides) for h in pair]
-    packed, *state_halo = lax.optimization_barrier((packed, *state_halo))
     arrived = lax.all_to_all(packed, ("gy", "gz"), 0, 0, tiled=True)
     primal = pl.pallas_call(
         primal_kernel,

time: 110 us -> 112 us (1.018)
  waiting for transfers between devices: 8.44 us -> 12.1 us
  starting transfers between devices: 56.8 us -> 55.1 us
  local copies, waits for them, and re-layouts: 8.29 us -> 6.71 us
    ppermute x3, starting transfers between devices: 11.4 us -> 4.49 us  [faces(): above = lax.ppermute(head, axis, [(i + 1, i) for i in range(ends)])]
    ppermute x3, waiting for transfers between devices: 0.01 us -> 4.12 us  [faces(): above = lax.ppermute(head, axis, [(i + 1, i) for i in range(ends)])]
    slice x3, local copies, waits for them, and re-layouts: 2.98 us -> 0.18 us  [faces(): head = lax.slice_in_dim(cells, 0, 1, axis=dim)]
    all_to_all x1, starting transfers between devices: 9.48 us -> 11.8 us  [shards(): arrived = lax.all_to_all(packed, ('gy', 'gz'), 0, 0, tiled=True)]
    ppermute x3, starting transfers between devices: 9.9 us -> 11.2 us  [faces(): below = lax.ppermute(tail, axis, [(i, i + 1) for i in range(ends)])]
    ppermute x3, waiting for transfers between devices: 3.46 us -> 2.21 us  [shards(): lax.ppermute(low, axis, [(i + 1, i) for i in range(ends)])]
    unnamed x34 -> x36, local copies, waits for them, and re-layouts: 2.51 us -> 3.75 us
  transfers between devices with their start and end apart: 14 -> 14, of which waited for: 3 -> 4; matrix products, arithmetic and copies ran while one was open for 7% -> 2% of each run, Pallas kernels for 3% -> 3%
where the time goes in v8:
time: 112 us; the launch traced here: 111 us
  starting transfers between devices  55.1 us (49%)
  blocking collectives  22.1 us (20%)
  waiting for transfers between devices  12.1 us (11%)
  Pallas kernels  8.69 us (8%)
  local copies, waits for them, and re-layouts  6.71 us (6%)
  other arithmetic  4.36 us (4%)
  between operations  1.62 us (1%)
    all_to_all x1, blocking collectives, shards(): level_one = lax.all_to_all(spread, ('gy', 'gz'), 0, 0, tiled=True)  22.1 us
    all_to_all x1, starting transfers between devices, shards(): lax.all_to_all(jnp.broadcast_to(level_one.reshape(1, plane), (across, pla...  12 us
    all_to_all x1, starting transfers between devices, shards(): arrived = lax.all_to_all(packed, ('gy', 'gz'), 0, 0, tiled=True)  11.8 us
    ppermute x3, starting transfers between devices, faces(): below = lax.ppermute(tail, axis, [(i, i + 1) for i in range(ends)])  11.2 us
    ppermute x3, starting transfers between devices, shards(): lax.ppermute(high, axis, [(i, i + 1) for i in range(ends)])  10.6 us
    pallas_call x1, Pallas kernels, shards(): pl.pallas_call(adjoint_kernel, out_shape=[jax.ShapeDtypeStruct(state.shap...  5.64 us
    ppermute x3, starting transfers between devices, shards(): lax.ppermute(low, axis, [(i + 1, i) for i in range(ends)])  5.08 us
    all_to_all x1, waiting for transfers between devices, shards(): lax.all_to_all(jnp.broadcast_to(level_one.reshape(1, plane), (across, pla...  4.88 us
  transfers between devices with their start and end apart: 14, of which 4 were waited for; matrix products, arithmetic and copies ran while one was open for 2% of the time, Pallas kernels for 3%

profile of v8, /device:TPU:1, one launch (start us, length us, event | category | flops | bytes accessed | tf_op | source)
XLA Modules:
  0.0 110.7 jit_solution(12843395717826438971)
XLA Ops:
  0.6 1.2 %copy.31 = bf16[128,5,2,2,128]{4,0,3,2,1:T(8,128)(2,1)S(1)} copy(bf16[128,5,2,2,128]{4,3,2,1,0:T(2,128)(2,1)} %param.14) | data formatting | bytes 1310720 | tf_op args[6]
  2.7 1.1 %pad_maximum_fusion = bf16[128,21,128]{2,1,0:T(8,128)(2,1)} fusion(bf16[128,1,128]{2,1,0:T(2,128)(2,1)S(1)} %copy.34, bf16[128,20,128]{2,1,0:T(8,128)(2,1)S(1)} %copy.33), kind=kLoop, calls=%fused_computation | loop fusion | flops 1376256 | bytes 1376256 | tf_op jit(solution)/shard_map/concatenate | solution.py:261
  3.9 11.8 %all-to-all-start = ((bf16[128,21,128]{2,1,0:T(8,128)(2,1)}), bf16[128,21,128]{2,1,0:T(8,128)(2,1)S(1)}, u32[]{:S(2)}, u32[]{:S(2)}) async-start(bf16[128,21,128]{2,1,0:T(8,128)(2,1)} %pad_maximum_fusion), calls=%async_computation | async-start | bytes 1572864 | tf_op jit(solution)/shard_map/all_to_all | solution.py:275
  15.7 4.0 %collective-permute-start = (bf16[5,1,8,768]{3,2,1,0:T(8,128)(2,1)S(1)}, bf16[5,1,8,768]{3,2,1,0:T(8,128)(2,1)S(1)}, u32[]{:S(2)}, u32[]{:S(2)}) collective-permute-start(bf16[5,1,8,768]{3,2,1,0:T(8,128)(2,1)S(1)} %get-tuple-element.30), channel_id=1, source_target_pairs={{0,64},{64,128},{128,192},{192,256},{256,320},{320,384},{384,448},... | collective-permute-start | bytes 184328 | tf_op jit(solution)/shard_map/ppermute | solution.py:31
  19.7 1.3 %collective-permute-start.1 = (bf16[5,1,8,768]{3,2,1,0:T(8,128)(2,1)S(1)}, bf16[5,1,8,768]{3,2,1,0:T(8,128)(2,1)S(1)}, u32[]{:S(2)}, u32[]{:S(2)}) collective-permute-start(bf16[5,1,8,768]{3,2,1,0:T(8,128)(2,1)S(1)} %get-tuple-element.29), channel_id=1, source_target_pairs={{64,0},{128,64},{192,128},{256,192},{320,256},{384,320},{448,384},... | collective-permute-start | bytes 184328 | tf_op jit(solution)/shard_map/ppermute | solution.py:32
  21.1 3.3 %collective-permute-start.2 = (bf16[5,4,1,768]{3,2,1,0:T(2,128)(2,1)S(1)}, bf16[5,4,1,768]{3,2,1,0:T(2,128)(2,1)S(1)}, u32[]{:S(2)}, u32[]{:S(2)}) collective-permute-start(bf16[5,4,1,768]{3,2,1,0:T(2,128)(2,1)S(1)} %get-tuple-element.28), channel_id=1, source_target_pairs={{0,8},{8,16},{16,24},{24,32},{32,40},{40,48},{48,56},{1,9},{9,17},... | collective-permute-start | bytes 92168 | tf_op jit(solution)/shard_map/ppermute | solution.py:31
  24.4 1.3 %collective-permute-start.3 = (bf16[5,4,1,768]{3,2,1,0:T(2,128)(2,1)S(1)}, bf16[5,4,1,768]{3,2,1,0:T(2,128)(2,1)S(1)}, u32[]{:S(2)}, u32[]{:S(2)}) collective-permute-start(bf16[5,4,1,768]{3,2,1,0:T(2,128)(2,1)S(1)} %get-tuple-element.27), channel_id=1, source_target_pairs={{8,0},{16,8},{24,16},{32,24},{40,32},{48,40},{56,48},{9,1},{17,9},... | collective-permute-start | bytes 92168 | tf_op jit(solution)/shard_map/ppermute | solution.py:32
  25.8 3.9 %collective-permute-start.4 = (bf16[5,4,8,1]{3,2,1,0:T(8,128)(2,1)S(1)}, bf16[5,4,8,1]{3,2,1,0:T(8,128)(2,1)S(1)}, u32[]{:S(2)}, u32[]{:S(2)}) collective-permute-start(bf16[5,4,8,1]{3,2,1,0:T(8,128)(2,1)S(1)} %get-tuple-element.26), channel_id=1, source_target_pairs={{0,1},{1,2},{2,3},{3,4},{4,5},{5,6},{6,7},{8,9},{9,10},{10,11},{11... | collective-permute-start | bytes 968 | tf_op jit(solution)/shard_map/ppermute | solution.py:31
  29.9 0.9 collective-permute-done.4.zlo
  30.8 1.9 %collective-permute-start.5 = (bf16[5,4,8,1]{3,2,1,0:T(8,128)(2,1)S(1)}, bf16[5,4,8,1]{3,2,1,0:T(8,128)(2,1)S(1)}, u32[]{:S(2)}, u32[]{:S(2)}) collective-permute-start(bf16[5,4,8,1]{3,2,1,0:T(8,128)(2,1)S(1)} %get-tuple-element.25), channel_id=1, source_target_pairs={{1,0},{2,1},{3,2},{4,3},{5,4},{6,5},{7,6},{9,8},{10,9},{11,10},{12... | collective-permute-start | bytes 968 | tf_op jit(solution)/shard_map/ppermute | solution.py:32
  33.2 4.1 %collective-permute-done.5.zhi = bf16[5,4,8,1]{3,2,1,0:T(8,128)(2,1)S(1)} collective-permute-done((bf16[5,4,8,1]{3,2,1,0:T(8,128)(2,1)S(1)}, bf16[5,4,8,1]{3,2,1,0:T(8,128)(2,1)S(1)}, u32[]{:S(2)}, u32[]{:S(2)}) %collective-permute-start.5) | collective-permute-done | bytes 352 | tf_op jit(solution)/shard_map/ppermute | solution.py:32
  38.6 3.1 %shard_map.103 = (f32[5,4,8,768]{3,2,1,0:T(8,128)}, bf16[4,8,768]{2,1,0:T(8,128)(2,1)}, bf16[5,1,8,768]{3,2,1,0:T(8,128)(2,1)}, bf16[5,1,8,768]{3,2,1,0:T(8,128)...) custom-call(f32[5,5]{1,0:T(8,128)} %c_ref.3, ...), custom_call_target="tpu_custom_call" | custom-call | tf_op jit(solution)/shard_map/pallas_call | solution.py:276
  41.7 4.8 %collective-permute-start.6 = (bf16[5,1,8,768]{3,2,1,0:T(8,128)(2,1)}, bf16[5,1,8,768]{3,2,1,0:T(8,128)(2,1)S(1)}, u32[]{:S(2)}, u32[]{:S(2)}) collective-permute-start(bf16[5,1,8,768]{3,2,1,0:T(8,128)(2,1)} %get-tuple-element.15), channel_id=1, source_target_pairs={{0,64},{64,128},{128,192},{192,256},{256,320},{320,384},{384,448},... | collective-permute-start | bytes 184328 | tf_op jit(solution)/shard_map/ppermute | solution.py:287
  46.4 1.9 %collective-permute-start.10 = (bf16[5,4,8,1]{3,2,1,0:T(8,128)(2,1)}, bf16[5,4,8,1]{3,2,1,0:T(8,128)(2,1)S(1)}, u32[]{:S(2)}, u32[]{:S(2)}) collective-permute-start(bf16[5,4,8,1]{3,2,1,0:T(8,128)(2,1)} %get-tuple-element.19), channel_id=1, source_target_pairs={{0,1},{1,2},{2,3},{3,4},{4,5},{5,6},{6,7},{8,9},{9,10},{10,11},{11... | collective-permute-start | bytes 968 | tf_op jit(solution)/shard_map/ppermute | solution.py:287
  48.4 1.3 %collective-permute-start.7 = (bf16[5,1,8,768]{3,2,1,0:T(8,128)(2,1)}, bf16[5,1,8,768]{3,2,1,0:T(8,128)(2,1)S(1)}, u32[]{:S(2)}, u32[]{:S(2)}) collective-permute-start(bf16[5,1,8,768]{3,2,1,0:T(8,128)(2,1)} %get-tuple-element.16), channel_id=1, source_target_pairs={{64,0},{128,64},{192,128},{256,192},{320,256},{384,320},{448,384},... | collective-permute-start | bytes 184328 | tf_op jit(solution)/shard_map/ppermute | solution.py:288
  49.7 3.9 %collective-permute-start.8 = (bf16[5,4,1,768]{3,2,1,0:T(2,128)(2,1)}, bf16[5,4,1,768]{3,2,1,0:T(2,128)(2,1)S(1)}, u32[]{:S(2)}, u32[]{:S(2)}) collective-permute-start(bf16[5,4,1,768]{3,2,1,0:T(2,128)(2,1)} %get-tuple-element.17), channel_id=1, source_target_pairs={{0,8},{8,16},{16,24},{24,32},{32,40},{40,48},{48,56},{1,9},{9,17},... | collective-permute-start | bytes 92168 | tf_op jit(solution)/shard_map/ppermute | solution.py:287
  53.6 1.3 %collective-permute-start.9 = (bf16[5,4,1,768]{3,2,1,0:T(2,128)(2,1)}, bf16[5,4,1,768]{3,2,1,0:T(2,128)(2,1)S(1)}, u32[]{:S(2)}, u32[]{:S(2)}) collective-permute-start(bf16[5,4,1,768]{3,2,1,0:T(2,128)(2,1)} %get-tuple-element.18), channel_id=1, source_target_pairs={{8,0},{16,8},{24,16},{32,24},{40,32},{48,40},{56,48},{9,1},{17,9},... | collective-permute-start | bytes 92168 | tf_op jit(solution)/shard_map/ppermute | solution.py:288
  54.9 2.5 %collective-permute-start.11 = (bf16[5,4,8,1]{3,2,1,0:T(8,128)(2,1)}, bf16[5,4,8,1]{3,2,1,0:T(8,128)(2,1)S(1)}, u32[]{:S(2)}, u32[]{:S(2)}) collective-permute-start(bf16[5,4,8,1]{3,2,1,0:T(8,128)(2,1)} %get-tuple-element.20), channel_id=1, source_target_pairs={{1,0},{2,1},{3,2},{4,3},{5,4},{6,5},{7,6},{9,8},{10,9},{11,10},{12... | collective-permute-start | bytes 968 | tf_op jit(solution)/shard_map/ppermute | solution.py:288
  58.2 2.2 %collective-permute-done.11.zhi = bf16[5,4,8,1]{3,2,1,0:T(8,128)(2,1)S(1)} collective-permute-done((bf16[5,4,8,1]{3,2,1,0:T(8,128)(2,1)}, bf16[5,4,8,1]{3,2,1,0:T(8,128)(2,1)S(1)}, u32[]{:S(2)}, u32[]{:S(2)}) %collective-permute-start.11) | collective-permute-done | bytes 352 | tf_op jit(solution)/shard_map/ppermute | solution.py:288
  61.4 5.6 %shard_map.104 = (bf16[5,4,8,768]{3,2,1,0:T(8,128)(2,1)}, f32[2,8,768]{2,1,0:T(8,128)}, f32[64,1]{1,0:T(8,128)}) custom-call(f32[5,5]{1,0:T(8,128)} %c_ref.3, s32[48]{0:T(128)} %multiply_add_fusion.slot_ref, f32[5,4,8,768]{3,2,1,0:T(8,128)} %get-tuple-element.14.s1_ref, bf16[5,4,8,768]{3,2,1,0:T(8,128)(2,1)} %s_ref.3, bf16[4,8,768]{2,1,0:T(8,128)(2,1)} %d_ref.3, ...), custom_call_target="tpu_custom_call" | custom-call | tf_op jit(solution)/shard_map/pallas_call | solution.py:303
  67.1 22.1 %all_to_all.20 = f32[64,1,1]{2,1,0:T(1,128)S(1)} all-to-all(f32[64,1,1]{2,1,0:T(1,128)} %bitcast.9), channel_id=1, replica_groups=mesh['gx'=8,'gy'=8,'gz'=8] {'gy','gz'}, dimensions={0} | all-to-all | bytes 512 | tf_op jit(solution)/shard_map/all_to_all | solution.py:318
  90.4 12.0 %all-to-all-start.2 = ((f32[8,1,64]{2,1,0:T(1,128)}), f32[8,1,64]{2,1,0:T(1,128)S(1)}, u32[]{:S(2)}, u32[]{:S(2)}) async-start(f32[8,1,64]{2,1,0:T(1,128)} %broadcast_in_dim.23), calls=%async_computation.2 | async-start | bytes 8192 | tf_op jit(solution)/shard_map/all_to_all | solution.py:319
  104.0 4.9 %all-to-all-done.2 = f32[8,1,64]{2,1,0:T(1,128)S(1)} async-done(((f32[8,1,64]{2,1,0:T(1,128)}), f32[8,1,64]{2,1,0:T(1,128)S(1)}, u32[]{:S(2)}, u32[]{:S(2)}) %all-to-all-start.2) | async-done | bytes 2080 | tf_op jit(solution)/shard_map/all_to_all | solution.py:319
  109.5 1.2 %divide_minimum_fusion = (f32[48]{0:T(128)}, f32[48]{0:T(128)}) fusion(f32[]{:T(128)} %bitcast.5, f32[]{:T(128)} %reduce_sum.29, f32[48]{0:T(128)S(1)} %reshape.37, s32[48]{0:T(128)S(1)} %copy-done.15), kind=kLoop, calls=%fused_computation.5 | loop fusion | flops 384 | bytes 776 | tf_op jit(solution)/shard_map/min | solution.py:325
  (63 shorter events, 7.5 us)
Async XLA Ops:
  1.8 0.7 copy-start.14
  3.9 11.8 %copy-start.1 = (bf16[5,4,8,768]{3,2,1,0:T(8,128)(2,1)S(1)}, bf16[5,4,8,768]{3,2,1,0:T(8,128)(2,1)}, u32[]{:S(2)}) copy-start(bf16[5,4,8,768]{3,2,1,0:T(8,128)(2,1)} %s_ref.3) | copy-start | bytes 737284
  3.9 25.8 %copy-start.16 = (s32[48,1]{0,1:T(1,128)S(1)}, s32[48,1]{0,1:T(1,128)}, u32[]{:S(2)}) copy-start(s32[48,1]{0,1:T(1,128)} %param.11) | copy-start | bytes 580
  3.9 56.6 %all-to-all-start = ((bf16[128,21,128]{2,1,0:T(8,128)(2,1)}), bf16[128,21,128]{2,1,0:T(8,128)(2,1)S(1)}, u32[]{:S(2)}, u32[]{:S(2)}) async-start(bf16[128,21,128]{2,1,0:T(8,128)(2,1)} %pad_maximum_fusion), calls=%async_computation | async-start | bytes 1572864 | tf_op jit(solution)/shard_map/all_to_all | solution.py:275
  15.7 41.8 %copy-start.15 = (s32[48]{0:T(128)S(1)}, s32[48]{0:T(128)}, u32[]{:S(2)}) copy-start(s32[48]{0:T(128)} %param.12) | copy-start | bytes 580
  15.7 21.6 %collective-permute-start = (bf16[5,1,8,768]{3,2,1,0:T(8,128)(2,1)S(1)}, bf16[5,1,8,768]{3,2,1,0:T(8,128)(2,1)S(1)}, u32[]{:S(2)}, u32[]{:S(2)}) collective-permute-start(bf16[5,1,8,768]{3,2,1,0:T(8,128)(2,1)S(1)} %get-tuple-element.30), channel_id=1, source_target_pairs={{0,64},{64,128},{128,192},{192,256},{256,320},{320,384},{384,448},... | collective-permute-start | bytes 184328 | tf_op jit(solution)/shard_map/ppermute | solution.py:31
  19.7 17.7 %collective-permute-start.1 = (bf16[5,1,8,768]{3,2,1,0:T(8,128)(2,1)S(1)}, bf16[5,1,8,768]{3,2,1,0:T(8,128)(2,1)S(1)}, u32[]{:S(2)}, u32[]{:S(2)}) collective-permute-start(bf16[5,1,8,768]{3,2,1,0:T(8,128)(2,1)S(1)} %get-tuple-element.29), channel_id=1, source_target_pairs={{64,0},{128,64},{192,128},{256,192},{320,256},{384,320},{448,384},... | collective-permute-start | bytes 184328 | tf_op jit(solution)/shard_map/ppermute | solution.py:32
  21.1 16.2 %collective-permute-start.2 = (bf16[5,4,1,768]{3,2,1,0:T(2,128)(2,1)S(1)}, bf16[5,4,1,768]{3,2,1,0:T(2,128)(2,1)S(1)}, u32[]{:S(2)}, u32[]{:S(2)}) collective-permute-start(bf16[5,4,1,768]{3,2,1,0:T(2,128)(2,1)S(1)} %get-tuple-element.28), channel_id=1, source_target_pairs={{0,8},{8,16},{16,24},{24,32},{32,40},{40,48},{48,56},{1,9},{9,17},... | collective-permute-start | bytes 92168 | tf_op jit(solution)/shard_map/ppermute | solution.py:31
  24.4 12.9 %collective-permute-start.3 = (bf16[5,4,1,768]{3,2,1,0:T(2,128)(2,1)S(1)}, bf16[5,4,1,768]{3,2,1,0:T(2,128)(2,1)S(1)}, u32[]{:S(2)}, u32[]{:S(2)}) collective-permute-start(bf16[5,4,1,768]{3,2,1,0:T(2,128)(2,1)S(1)} %get-tuple-element.27), channel_id=1, source_target_pairs={{8,0},{16,8},{24,16},{32,24},{40,32},{48,40},{56,48},{9,1},{17,9},... | collective-permute-start | bytes 92168 | tf_op jit(solution)/shard_map/ppermute | solution.py:32
  25.8 5.0 %collective-permute-start.4 = (bf16[5,4,8,1]{3,2,1,0:T(8,128)(2,1)S(1)}, bf16[5,4,8,1]{3,2,1,0:T(8,128)(2,1)S(1)}, u32[]{:S(2)}, u32[]{:S(2)}) collective-permute-start(bf16[5,4,8,1]{3,2,1,0:T(8,128)(2,1)S(1)} %get-tuple-element.26), channel_id=1, source_target_pairs={{0,1},{1,2},{2,3},{3,4},{4,5},{5,6},{6,7},{8,9},{9,10},{10,11},{11... | collective-permute-start | bytes 968 | tf_op jit(solution)/shard_map/ppermute | solution.py:31
  30.8 6.6 %copy-start.10 = (bf16[5,4,8,1]{3,2,1,0:T(8,128)(2,1)}, bf16[5,4,8,1]{3,2,1,0:T(8,128)(2,1)S(1)}, u32[]{:S(2)}) copy-start(bf16[5,4,8,1]{3,2,1,0:T(8,128)(2,1)S(1)} %collective-permute-done.4.zlo) | copy-start | bytes 964
  30.8 6.5 %collective-permute-start.5 = (bf16[5,4,8,1]{3,2,1,0:T(8,128)(2,1)S(1)}, bf16[5,4,8,1]{3,2,1,0:T(8,128)(2,1)S(1)}, u32[]{:S(2)}, u32[]{:S(2)}) collective-permute-start(bf16[5,4,8,1]{3,2,1,0:T(8,128)(2,1)S(1)} %get-tuple-element.25), channel_id=1, source_target_pairs={{1,0},{2,1},{3,2},{4,3},{5,4},{6,5},{7,6},{9,8},{10,9},{11,10},{12... | collective-permute-start | bytes 968 | tf_op jit(solution)/shard_map/ppermute | solution.py:32
  37.3 0.7 copy-start.9
  41.7 18.8 %collective-permute-start.6 = (bf16[5,1,8,768]{3,2,1,0:T(8,128)(2,1)}, bf16[5,1,8,768]{3,2,1,0:T(8,128)(2,1)S(1)}, u32[]{:S(2)}, u32[]{:S(2)}) collective-permute-start(bf16[5,1,8,768]{3,2,1,0:T(8,128)(2,1)} %get-tuple-element.15), channel_id=1, source_target_pairs={{0,64},{64,128},{128,192},{192,256},{256,320},{320,384},{384,448},... | collective-permute-start | bytes 184328 | tf_op jit(solution)/shard_map/ppermute | solution.py:287
  46.4 8.5 %collective-permute-start.10 = (bf16[5,4,8,1]{3,2,1,0:T(8,128)(2,1)}, bf16[5,4,8,1]{3,2,1,0:T(8,128)(2,1)S(1)}, u32[]{:S(2)}, u32[]{:S(2)}) collective-permute-start(bf16[5,4,8,1]{3,2,1,0:T(8,128)(2,1)} %get-tuple-element.19), channel_id=1, source_target_pairs={{0,1},{1,2},{2,3},{3,4},{4,5},{5,6},{6,7},{8,9},{9,10},{10,11},{11... | collective-permute-start | bytes 968 | tf_op jit(solution)/shard_map/ppermute | solution.py:287
  48.4 12.1 %collective-permute-start.7 = (bf16[5,1,8,768]{3,2,1,0:T(8,128)(2,1)}, bf16[5,1,8,768]{3,2,1,0:T(8,128)(2,1)S(1)}, u32[]{:S(2)}, u32[]{:S(2)}) collective-permute-start(bf16[5,1,8,768]{3,2,1,0:T(8,128)(2,1)} %get-tuple-element.16), channel_id=1, source_target_pairs={{64,0},{128,64},{192,128},{256,192},{320,256},{384,320},{448,384},... | collective-permute-start | bytes 184328 | tf_op jit(solution)/shard_map/ppermute | solution.py:288
  49.7 10.8 %collective-permute-start.8 = (bf16[5,4,1,768]{3,2,1,0:T(2,128)(2,1)}, bf16[5,4,1,768]{3,2,1,0:T(2,128)(2,1)S(1)}, u32[]{:S(2)}, u32[]{:S(2)}) collective-permute-start(bf16[5,4,1,768]{3,2,1,0:T(2,128)(2,1)} %get-tuple-element.17), channel_id=1, source_target_pairs={{0,8},{8,16},{16,24},{24,32},{32,40},{40,48},{48,56},{1,9},{9,17},... | collective-permute-start | bytes 92168 | tf_op jit(solution)/shard_map/ppermute | solution.py:287
  53.6 6.9 %collective-permute-start.9 = (bf16[5,4,1,768]{3,2,1,0:T(2,128)(2,1)}, bf16[5,4,1,768]{3,2,1,0:T(2,128)(2,1)S(1)}, u32[]{:S(2)}, u32[]{:S(2)}) collective-permute-start(bf16[5,4,1,768]{3,2,1,0:T(2,128)(2,1)} %get-tuple-element.18), channel_id=1, source_target_pairs={{8,0},{16,8},{24,16},{32,24},{40,32},{48,40},{56,48},{9,1},{17,9},... | collective-permute-start | bytes 92168 | tf_op jit(solution)/shard_map/ppermute | solution.py:288
  54.9 5.6 %copy-start.12 = (bf16[5,4,8,1]{3,2,1,0:T(8,128)(2,1)}, bf16[5,4,8,1]{3,2,1,0:T(8,128)(2,1)S(1)}, u32[]{:S(2)}) copy-start(bf16[5,4,8,1]{3,2,1,0:T(8,128)(2,1)S(1)} %collective-permute-done.10.zlo) | copy-start | bytes 964
  54.9 5.5 %collective-permute-start.11 = (bf16[5,4,8,1]{3,2,1,0:T(8,128)(2,1)}, bf16[5,4,8,1]{3,2,1,0:T(8,128)(2,1)S(1)}, u32[]{:S(2)}, u32[]{:S(2)}) collective-permute-start(bf16[5,4,8,1]{3,2,1,0:T(8,128)(2,1)} %get-tuple-element.20), channel_id=1, source_target_pairs={{1,0},{2,1},{3,2},{4,3},{5,4},{6,5},{7,6},{9,8},{10,9},{11,10},{12... | collective-permute-start | bytes 968 | tf_op jit(solution)/shard_map/ppermute | solution.py:288
  60.5 0.6 copy-start.8
  60.5 0.7 copy-start.5
  60.5 0.9 copy-start
  90.4 18.5 %all-to-all-start.2 = ((f32[8,1,64]{2,1,0:T(1,128)}), f32[8,1,64]{2,1,0:T(1,128)S(1)}, u32[]{:S(2)}, u32[]{:S(2)}) async-start(f32[8,1,64]{2,1,0:T(1,128)} %broadcast_in_dim.23), calls=%async_computation.2 | async-start | bytes 8192 | tf_op jit(solution)/shard_map/all_to_all | solution.py:319
  (7 other events, 4.4 us)

commit v9 on v7

--- a/solution.py
+++ b/solution.py
@@ -193,6 +193,21 @@
             ozlo[f, x] = low[:, 0:1]
             ozhi[f, x] = low[:, nz - 1:nz]
         eff_ref[x] = (d * (1.0 + 0.5 * jnp.tanh(s1[0]))).astype(jnp.bfloat16)
+
+
+def faces_kernel(s_ref, oxlo, oxhi, oylo, oyhi, ozlo, ozhi):
+    nf, nx, ny, nz = s_ref.shape
+    for f in range(nf):
+        for x in range(nx):
+            v = s_ref[f, x]
+            if x == 0:
+                oxlo[f, 0] = v
+            if x == nx - 1:
+                oxhi[f, 0] = v
+            oylo[f, x] = v[0:1, :]
+            oyhi[f, x] = v[ny - 1:ny, :]
+            ozlo[f, x] = v[:, 0:1]
+            ozhi[f, x] = v[:, nz - 1:nz]
 
 
 def adjoint_kernel(c_ref, slot_ref, s1_ref, s_ref, d_ref, xlo, xhi, ylo, yhi, zlo, zhi, eff_ref, arr_ref,
@@ -271,7 +286,17 @@
     vmem = pl.BlockSpec(memory_space=pltpu.VMEM)
     smem = pl.BlockSpec(memory_space=pltpu.SMEM)
     face_shapes = [(nf, 1, ny, nz)] * 2 + [(nf, nx, 1, nz)] * 2 + [(nf, nx, ny, 1)] * 2
-    state_halo = [h for pair in faces(state, sides) for h in pair]
+    state_faces = pl.pallas_call(
+        faces_kernel,
+        out_shape=[jax.ShapeDtypeStruct(shape, state.dtype) for shape in face_shapes],
+        in_specs=[vmem],
+        out_specs=[vmem] * 6,
+    )(state)
+    state_halo = []
+    for (axis, _), low, high in zip(sides, state_faces[0::2], state_faces[1::2]):
+        ends = lax.axis_size(axis) - 1
+        state_halo.append(lax.ppermute(high, axis, [(i, i + 1) for i in range(ends)]))
+        state_halo.append(lax.ppermute(low, axis, [(i + 1, i) for i in range(ends)]))
     packed, *state_halo = lax.optimization_barrier((packed, *state_halo))
     arrived = lax.all_to_all(packed, ("gy", "gz"), 0, 0, tiled=True)
     primal = pl.pallas_call(

time: 110 us -> 113 us (1.027)
  waiting for transfers between devices: 8.44 us -> 10.5 us
  Pallas kernels: 8.7 us -> 10.4 us
  local copies, waits for them, and re-layouts: 8.29 us -> 6.71 us
    ppermute x6 -> x0, starting transfers between devices: 21.3 us -> none  [the longest x3 11.4 us: faces(): above = lax.ppermute(head, axis, [(i + 1, i) for i in range(ends)])]
    ppermute x3 -> x6, starting transfers between devices: 10.6 us -> 19.3 us  [shards(): lax.ppermute(high, axis, [(i, i + 1) for i in range(ends)])]
    ppermute x3 -> x6, starting transfers between devices: 4.5 us -> 12.6 us  [shards(): lax.ppermute(low, axis, [(i + 1, i) for i in range(ends)])]
    all_to_all x1, starting transfers between devices: 9.48 us -> 12.7 us  [shards(): arrived = lax.all_to_all(packed, ('gy', 'gz'), 0, 0, tiled=True)]
    slice x3 -> x0, local copies, waits for them, and re-layouts: 2.98 us -> none  [faces(): head = lax.slice_in_dim(cells, 0, 1, axis=dim)]
    ppermute x3 -> x6, waiting for transfers between devices: 3.46 us -> 5.65 us  [shards(): lax.ppermute(low, axis, [(i + 1, i) for i in range(ends)])]
    pallas_call x0 -> x1, Pallas kernels: none -> 1.68 us  [shards(): pl.pallas_call(faces_kernel, out_shape=[jax.ShapeDtypeStruct(shape, state...]
    unnamed x34, local copies, waits for them, and re-layouts: 2.51 us -> 3.93 us
  transfers between devices with their start and end apart: 14 -> 14, of which waited for: 3 -> 3; matrix products, arithmetic and copies ran while one was open for 7% -> 5% of each run, Pallas kernels for 3% -> 3%
where the time goes in v9:
time: 113 us; the launch traced here: 112 us
  starting transfers between devices  56.9 us (50%)
  blocking collectives  21.7 us (19%)
  waiting for transfers between devices  10.5 us (9%)
  Pallas kernels  10.4 us (9%)
  local copies, waits for them, and re-layouts  6.71 us (6%)
  other arithmetic  4.26 us (4%)
  between operations  1.61 us (1%)
    all_to_all x1, blocking collectives, shards(): level_one = lax.all_to_all(spread, ('gy', 'gz'), 0, 0, tiled=True)  21.7 us
    ppermute x6, starting transfers between devices, shards(): lax.ppermute(high, axis, [(i, i + 1) for i in range(ends)])  19.3 us
    all_to_all x1, starting transfers between devices, shards(): arrived = lax.all_to_all(packed, ('gy', 'gz'), 0, 0, tiled=True)  12.7 us
    ppermute x6, starting transfers between devices, shards(): lax.ppermute(low, axis, [(i + 1, i) for i in range(ends)])  12.6 us
    all_to_all x1, starting transfers between devices, shards(): lax.all_to_all(jnp.broadcast_to(level_one.reshape(1, plane), (across, pla...  12.3 us
    ppermute x6, waiting for transfers between devices, shards(): lax.ppermute(low, axis, [(i + 1, i) for i in range(ends)])  5.65 us
    pallas_call x1, Pallas kernels, shards(): pl.pallas_call(adjoint_kernel, out_shape=[jax.ShapeDtypeStruct(state.shap...  5.62 us
    all_to_all x1, waiting for transfers between devices, shards(): lax.all_to_all(jnp.broadcast_to(level_one.reshape(1, plane), (across, pla...  4.88 us
  transfers between devices with their start and end apart: 14, of which 3 were waited for; matrix products, arithmetic and copies ran while one was open for 5% of the time, Pallas kernels for 3%

profile of v9, /device:TPU:1, one launch (start us, length us, event | category | flops | bytes accessed | tf_op | source)
XLA Modules:
  0.0 112.1 jit_solution(13262168626811947250)
XLA Ops:
  0.6 1.7 %shard_map.103 = (bf16[5,1,8,768]{3,2,1,0:T(8,128)(2,1)}, bf16[5,1,8,768]{3,2,1,0:T(8,128)(2,1)}, bf16[5,4,1,768]{3,2,1,0:T(2,128)(2,1)}, bf16[5,4,1,768]{3,2,1,...) custom-call(bf16[5,4,8,768]{3,2,1,0:T(8,128)(2,1)} %s_ref.5), custom_call_target="tpu_custom_call" | custom-call | tf_op jit(solution)/shard_map/pallas_call | solution.py:289
  2.3 4.5 %collective-permute-start.4 = (bf16[5,4,8,1]{3,2,1,0:T(8,128)(2,1)}, bf16[5,4,8,1]{3,2,1,0:T(8,128)(2,1)S(1)}, u32[]{:S(2)}, u32[]{:S(2)}) collective-permute-start(bf16[5,4,8,1]{3,2,1,0:T(8,128)(2,1)} %get-tuple-element.31), channel_id=1, source_target_pairs={{0,1},{1,2},{2,3},{3,4},{4,5},{5,6},{6,7},{8,9},{9,10},{10,11},{11... | collective-permute-start | bytes 968 | tf_op jit(solution)/shard_map/ppermute | solution.py:298
  6.8 5.6 %collective-permute-start.5 = (bf16[5,4,8,1]{3,2,1,0:T(8,128)(2,1)}, bf16[5,4,8,1]{3,2,1,0:T(8,128)(2,1)S(1)}, u32[]{:S(2)}, u32[]{:S(2)}) collective-permute-start(bf16[5,4,8,1]{3,2,1,0:T(8,128)(2,1)} %get-tuple-element.32), channel_id=1, source_target_pairs={{1,0},{2,1},{3,2},{4,3},{5,4},{6,5},{7,6},{9,8},{10,9},{11,10},{12... | collective-permute-start | bytes 968 | tf_op jit(solution)/shard_map/ppermute | solution.py:299
  12.4 1.3 %collective-permute-start = (bf16[5,1,8,768]{3,2,1,0:T(8,128)(2,1)}, bf16[5,1,8,768]{3,2,1,0:T(8,128)(2,1)S(1)}, u32[]{:S(2)}, u32[]{:S(2)}) collective-permute-start(bf16[5,1,8,768]{3,2,1,0:T(8,128)(2,1)} %get-tuple-element.27), channel_id=1, source_target_pairs={{0,64},{64,128},{128,192},{192,256},{256,320},{320,384},{384,448},... | collective-permute-start | bytes 184328 | tf_op jit(solution)/shard_map/ppermute | solution.py:298
  13.7 1.3 %collective-permute-start.1 = (bf16[5,1,8,768]{3,2,1,0:T(8,128)(2,1)}, bf16[5,1,8,768]{3,2,1,0:T(8,128)(2,1)S(1)}, u32[]{:S(2)}, u32[]{:S(2)}) collective-permute-start(bf16[5,1,8,768]{3,2,1,0:T(8,128)(2,1)} %get-tuple-element.28), channel_id=1, source_target_pairs={{64,0},{128,64},{192,128},{256,192},{320,256},{384,320},{448,384},... | collective-permute-start | bytes 184328 | tf_op jit(solution)/shard_map/ppermute | solution.py:299
  15.0 2.3 %collective-permute-start.2 = (bf16[5,4,1,768]{3,2,1,0:T(2,128)(2,1)}, bf16[5,4,1,768]{3,2,1,0:T(2,128)(2,1)S(1)}, u32[]{:S(2)}, u32[]{:S(2)}) collective-permute-start(bf16[5,4,1,768]{3,2,1,0:T(2,128)(2,1)} %get-tuple-element.29), channel_id=1, source_target_pairs={{0,8},{8,16},{16,24},{24,32},{32,40},{40,48},{48,56},{1,9},{9,17},... | collective-permute-start | bytes 92168 | tf_op jit(solution)/shard_map/ppermute | solution.py:298
  18.1 1.2 %copy.31 = bf16[128,5,2,2,128]{4,0,3,2,1:T(8,128)(2,1)S(1)} copy(bf16[128,5,2,2,128]{4,3,2,1,0:T(2,128)(2,1)} %param.14) | data formatting | bytes 1310720 | tf_op args[6]
  20.2 1.3 %collective-permute-start.3 = (bf16[5,4,1,768]{3,2,1,0:T(2,128)(2,1)S(1)}, bf16[5,4,1,768]{3,2,1,0:T(2,128)(2,1)S(1)}, u32[]{:S(2)}, u32[]{:S(2)}) collective-permute-start(bf16[5,4,1,768]{3,2,1,0:T(2,128)(2,1)S(1)} %copy-done.14), channel_id=1, source_target_pairs={{8,0},{16,8},{24,16},{32,24},{40,32},{48,40},{56,48},{9,1},{17,9},... | collective-permute-start | bytes 92168 | tf_op jit(solution)/shard_map/ppermute | solution.py:299
  21.5 1.1 %pad_maximum_fusion = bf16[128,21,128]{2,1,0:T(8,128)(2,1)} fusion(bf16[128,1,128]{2,1,0:T(2,128)(2,1)S(1)} %copy.34, bf16[128,20,128]{2,1,0:T(8,128)(2,1)S(1)} %copy.33), kind=kLoop, calls=%fused_computation | loop fusion | flops 1376256 | bytes 1376256 | tf_op jit(solution)/shard_map/concatenate | solution.py:276
  22.7 2.5 %collective-permute-done.3.yhi = bf16[5,4,1,768]{3,2,1,0:T(2,128)(2,1)S(1)} collective-permute-done((bf16[5,4,1,768]{3,2,1,0:T(2,128)(2,1)S(1)}, bf16[5,4,1,768]{3,2,1,0:T(2,128)(2,1)S(1)}, u32[]{:S(2)}, u32[]{:S(2)}) %collective-permute-start.3) | collective-permute-done | bytes 30752 | tf_op jit(solution)/shard_map/ppermute | solution.py:299
  25.8 12.7 %all-to-all-start = ((bf16[128,21,128]{2,1,0:T(8,128)(2,1)}), bf16[128,21,128]{2,1,0:T(8,128)(2,1)S(1)}, u32[]{:S(2)}, u32[]{:S(2)}) async-start(bf16[128,21,128]{2,1,0:T(8,128)(2,1)} %pad_maximum_fusion), calls=%async_computation | async-start | bytes 1572864 | tf_op jit(solution)/shard_map/all_to_all | solution.py:301
  39.2 3.1 %shard_map.104 = (f32[5,4,8,768]{3,2,1,0:T(8,128)}, bf16[4,8,768]{2,1,0:T(8,128)(2,1)}, bf16[5,1,8,768]{3,2,1,0:T(8,128)(2,1)}, bf16[5,1,8,768]{3,2,1,0:T(8,128)...) custom-call(f32[5,5]{1,0:T(8,128)} %c_ref.3, ...), custom_call_target="tpu_custom_call" | custom-call | tf_op jit(solution)/shard_map/pallas_call | solution.py:302
  42.3 3.5 %collective-permute-start.10 = (bf16[5,4,8,1]{3,2,1,0:T(8,128)(2,1)}, bf16[5,4,8,1]{3,2,1,0:T(8,128)(2,1)S(1)}, u32[]{:S(2)}, u32[]{:S(2)}) collective-permute-start(bf16[5,4,8,1]{3,2,1,0:T(8,128)(2,1)} %get-tuple-element.44), channel_id=1, source_target_pairs={{0,1},{1,2},{2,3},{3,4},{4,5},{5,6},{6,7},{8,9},{9,10},{10,11},{11... | collective-permute-start | bytes 968 | tf_op jit(solution)/shard_map/ppermute | solution.py:313
  45.8 1.9 %collective-permute-start.11 = (bf16[5,4,8,1]{3,2,1,0:T(8,128)(2,1)}, bf16[5,4,8,1]{3,2,1,0:T(8,128)(2,1)S(1)}, u32[]{:S(2)}, u32[]{:S(2)}) collective-permute-start(bf16[5,4,8,1]{3,2,1,0:T(8,128)(2,1)} %get-tuple-element.45), channel_id=1, source_target_pairs={{1,0},{2,1},{3,2},{4,3},{5,4},{6,5},{7,6},{9,8},{10,9},{11,10},{12... | collective-permute-start | bytes 968 | tf_op jit(solution)/shard_map/ppermute | solution.py:314
  47.7 4.6 %collective-permute-start.6 = (bf16[5,1,8,768]{3,2,1,0:T(8,128)(2,1)}, bf16[5,1,8,768]{3,2,1,0:T(8,128)(2,1)S(1)}, u32[]{:S(2)}, u32[]{:S(2)}) collective-permute-start(bf16[5,1,8,768]{3,2,1,0:T(8,128)(2,1)} %get-tuple-element.40), channel_id=1, source_target_pairs={{0,64},{64,128},{128,192},{192,256},{256,320},{320,384},{384,448},... | collective-permute-start | bytes 184328 | tf_op jit(solution)/shard_map/ppermute | solution.py:313
  52.4 1.3 %collective-permute-start.7 = (bf16[5,1,8,768]{3,2,1,0:T(8,128)(2,1)}, bf16[5,1,8,768]{3,2,1,0:T(8,128)(2,1)S(1)}, u32[]{:S(2)}, u32[]{:S(2)}) collective-permute-start(bf16[5,1,8,768]{3,2,1,0:T(8,128)(2,1)} %get-tuple-element.41), channel_id=1, source_target_pairs={{64,0},{128,64},{192,128},{256,192},{320,256},{384,320},{448,384},... | collective-permute-start | bytes 184328 | tf_op jit(solution)/shard_map/ppermute | solution.py:314
  53.7 3.1 %collective-permute-start.8 = (bf16[5,4,1,768]{3,2,1,0:T(2,128)(2,1)}, bf16[5,4,1,768]{3,2,1,0:T(2,128)(2,1)S(1)}, u32[]{:S(2)}, u32[]{:S(2)}) collective-permute-start(bf16[5,4,1,768]{3,2,1,0:T(2,128)(2,1)} %get-tuple-element.42), channel_id=1, source_target_pairs={{0,8},{8,16},{16,24},{24,32},{32,40},{40,48},{48,56},{1,9},{9,17},... | collective-permute-start | bytes 92168 | tf_op jit(solution)/shard_map/ppermute | solution.py:313
  56.8 1.3 %collective-permute-start.9 = (bf16[5,4,1,768]{3,2,1,0:T(2,128)(2,1)}, bf16[5,4,1,768]{3,2,1,0:T(2,128)(2,1)S(1)}, u32[]{:S(2)}, u32[]{:S(2)}) collective-permute-start(bf16[5,4,1,768]{3,2,1,0:T(2,128)(2,1)} %get-tuple-element.43), channel_id=1, source_target_pairs={{8,0},{16,8},{24,16},{32,24},{40,32},{48,40},{56,48},{9,1},{17,9},... | collective-permute-start | bytes 92168 | tf_op jit(solution)/shard_map/ppermute | solution.py:314
  58.9 3.2 %collective-permute-done.9.yhi = bf16[5,4,1,768]{3,2,1,0:T(2,128)(2,1)S(1)} collective-permute-done((bf16[5,4,1,768]{3,2,1,0:T(2,128)(2,1)}, bf16[5,4,1,768]{3,2,1,0:T(2,128)(2,1)S(1)}, u32[]{:S(2)}, u32[]{:S(2)}) %collective-permute-start.9) | collective-permute-done | bytes 30752 | tf_op jit(solution)/shard_map/ppermute | solution.py:314
  63.1 5.6 %shard_map.105 = (bf16[5,4,8,768]{3,2,1,0:T(8,128)(2,1)}, f32[2,8,768]{2,1,0:T(8,128)}, f32[64,1]{1,0:T(8,128)}) custom-call(f32[5,5]{1,0:T(8,128)} %c_ref.3, s32[48]{0:T(128)} %multiply_add_fusion.slot_ref, f32[5,4,8,768]{3,2,1,0:T(8,128)} %get-tuple-element.39.s1_ref, bf16[5,4,8,768]{3,2,1,0:T(8,128)(2,1)} %s_ref.5, bf16[4,8,768]{2,1,0:T(8,128)(2,1)} %d_ref.3, ...), custom_call_target="tpu_custom_call" | custom-call | tf_op jit(solution)/shard_map/pallas_call | solution.py:329
  68.7 21.7 %all_to_all.20 = f32[64,1,1]{2,1,0:T(1,128)S(1)} all-to-all(f32[64,1,1]{2,1,0:T(1,128)} %bitcast.9), channel_id=1, replica_groups=mesh['gx'=8,'gy'=8,'gz'=8] {'gy','gz'}, dimensions={0} | all-to-all | bytes 512 | tf_op jit(solution)/shard_map/all_to_all | solution.py:344
  91.5 12.3 %all-to-all-start.2 = ((f32[8,1,64]{2,1,0:T(1,128)}), f32[8,1,64]{2,1,0:T(1,128)S(1)}, u32[]{:S(2)}, u32[]{:S(2)}) async-start(f32[8,1,64]{2,1,0:T(1,128)} %broadcast_in_dim.23), calls=%async_computation.2 | async-start | bytes 8192 | tf_op jit(solution)/shard_map/all_to_all | solution.py:345
  105.5 4.9 %all-to-all-done.2 = f32[8,1,64]{2,1,0:T(1,128)S(1)} async-done(((f32[8,1,64]{2,1,0:T(1,128)}), f32[8,1,64]{2,1,0:T(1,128)S(1)}, u32[]{:S(2)}, u32[]{:S(2)}) %all-to-all-start.2) | async-done | bytes 2080 | tf_op jit(solution)/shard_map/all_to_all | solution.py:345
  111.0 1.2 %divide_minimum_fusion = (f32[48]{0:T(128)}, f32[48]{0:T(128)}) fusion(f32[]{:T(128)} %bitcast.5, f32[]{:T(128)} %reduce_sum.29, f32[48]{0:T(128)S(1)} %reshape.37, s32[48]{0:T(128)S(1)} %copy-done.13), kind=kLoop, calls=%fused_computation.5 | loop fusion | flops 384 | bytes 776 | tf_op jit(solution)/shard_map/min | solution.py:351
  (59 shorter events, 7.5 us)
Async XLA Ops:
  2.3 17.5 %collective-permute-start.4 = (bf16[5,4,8,1]{3,2,1,0:T(8,128)(2,1)}, bf16[5,4,8,1]{3,2,1,0:T(8,128)(2,1)S(1)}, u32[]{:S(2)}, u32[]{:S(2)}) collective-permute-start(bf16[5,4,8,1]{3,2,1,0:T(8,128)(2,1)} %get-tuple-element.31), channel_id=1, source_target_pairs={{0,1},{1,2},{2,3},{3,4},{4,5},{5,6},{6,7},{8,9},{9,10},{10,11},{11... | collective-permute-start | bytes 968 | tf_op jit(solution)/shard_map/ppermute | solution.py:298
  6.8 15.8 %collective-permute-start.5 = (bf16[5,4,8,1]{3,2,1,0:T(8,128)(2,1)}, bf16[5,4,8,1]{3,2,1,0:T(8,128)(2,1)S(1)}, u32[]{:S(2)}, u32[]{:S(2)}) collective-permute-start(bf16[5,4,8,1]{3,2,1,0:T(8,128)(2,1)} %get-tuple-element.32), channel_id=1, source_target_pairs={{1,0},{2,1},{3,2},{4,3},{5,4},{6,5},{7,6},{9,8},{10,9},{11,10},{12... | collective-permute-start | bytes 968 | tf_op jit(solution)/shard_map/ppermute | solution.py:299
  12.4 12.8 %collective-permute-start = (bf16[5,1,8,768]{3,2,1,0:T(8,128)(2,1)}, bf16[5,1,8,768]{3,2,1,0:T(8,128)(2,1)S(1)}, u32[]{:S(2)}, u32[]{:S(2)}) collective-permute-start(bf16[5,1,8,768]{3,2,1,0:T(8,128)(2,1)} %get-tuple-element.27), channel_id=1, source_target_pairs={{0,64},{64,128},{128,192},{192,256},{256,320},{320,384},{384,448},... | collective-permute-start | bytes 184328 | tf_op jit(solution)/shard_map/ppermute | solution.py:298
  13.7 11.5 %collective-permute-start.1 = (bf16[5,1,8,768]{3,2,1,0:T(8,128)(2,1)}, bf16[5,1,8,768]{3,2,1,0:T(8,128)(2,1)S(1)}, u32[]{:S(2)}, u32[]{:S(2)}) collective-permute-start(bf16[5,1,8,768]{3,2,1,0:T(8,128)(2,1)} %get-tuple-element.28), channel_id=1, source_target_pairs={{64,0},{128,64},{192,128},{256,192},{320,256},{384,320},{448,384},... | collective-permute-start | bytes 184328 | tf_op jit(solution)/shard_map/ppermute | solution.py:299
  15.0 7.7 %collective-permute-start.2 = (bf16[5,4,1,768]{3,2,1,0:T(2,128)(2,1)}, bf16[5,4,1,768]{3,2,1,0:T(2,128)(2,1)S(1)}, u32[]{:S(2)}, u32[]{:S(2)}) collective-permute-start(bf16[5,4,1,768]{3,2,1,0:T(2,128)(2,1)} %get-tuple-element.29), channel_id=1, source_target_pairs={{0,8},{8,16},{16,24},{24,32},{32,40},{40,48},{48,56},{1,9},{9,17},... | collective-permute-start | bytes 92168 | tf_op jit(solution)/shard_map/ppermute | solution.py:298
  19.4 0.8 copy-start.14
  19.8 2.8 %copy-start.9 = (bf16[5,4,8,1]{3,2,1,0:T(8,128)(2,1)}, bf16[5,4,8,1]{3,2,1,0:T(8,128)(2,1)S(1)}, u32[]{:S(2)}) copy-start(bf16[5,4,8,1]{3,2,1,0:T(8,128)(2,1)S(1)} %collective-permute-done.4.zlo) | copy-start | bytes 964
  20.2 5.0 %collective-permute-start.3 = (bf16[5,4,1,768]{3,2,1,0:T(2,128)(2,1)S(1)}, bf16[5,4,1,768]{3,2,1,0:T(2,128)(2,1)S(1)}, u32[]{:S(2)}, u32[]{:S(2)}) collective-permute-start(bf16[5,4,1,768]{3,2,1,0:T(2,128)(2,1)S(1)} %copy-done.14), channel_id=1, source_target_pairs={{8,0},{16,8},{24,16},{32,24},{40,32},{48,40},{56,48},{9,1},{17,9},... | collective-permute-start | bytes 92168 | tf_op jit(solution)/shard_map/ppermute | solution.py:299
  22.6 15.9 %copy-start.15 = (s32[48,1]{0,1:T(1,128)S(1)}, s32[48,1]{0,1:T(1,128)}, u32[]{:S(2)}) copy-start(s32[48,1]{0,1:T(1,128)} %param.11) | copy-start | bytes 580
  22.6 35.5 %copy-start.13 = (s32[48]{0:T(128)S(1)}, s32[48]{0:T(128)}, u32[]{:S(2)}) copy-start(s32[48]{0:T(128)} %param.12) | copy-start | bytes 580
  22.6 2.5 %copy-start.10 = (bf16[5,4,8,1]{3,2,1,0:T(8,128)(2,1)}, bf16[5,4,8,1]{3,2,1,0:T(8,128)(2,1)S(1)}, u32[]{:S(2)}) copy-start(bf16[5,4,8,1]{3,2,1,0:T(8,128)(2,1)S(1)} %collective-permute-done.5.zhi) | copy-start | bytes 964
  22.7 2.5 %copy-start.3 = (bf16[5,4,1,768]{3,2,1,0:T(2,128)(2,1)}, bf16[5,4,1,768]{3,2,1,0:T(2,128)(2,1)S(1)}, u32[]{:S(2)}) copy-start(bf16[5,4,1,768]{3,2,1,0:T(2,128)(2,1)S(1)} %collective-permute-done.2.ylo) | copy-start | bytes 92164
  25.8 36.3 %all-to-all-start = ((bf16[128,21,128]{2,1,0:T(8,128)(2,1)}), bf16[128,21,128]{2,1,0:T(8,128)(2,1)S(1)}, u32[]{:S(2)}, u32[]{:S(2)}) async-start(bf16[128,21,128]{2,1,0:T(8,128)(2,1)} %pad_maximum_fusion), calls=%async_computation | async-start | bytes 1572864 | tf_op jit(solution)/shard_map/all_to_all | solution.py:301
  42.3 14.5 %collective-permute-start.10 = (bf16[5,4,8,1]{3,2,1,0:T(8,128)(2,1)}, bf16[5,4,8,1]{3,2,1,0:T(8,128)(2,1)S(1)}, u32[]{:S(2)}, u32[]{:S(2)}) collective-permute-start(bf16[5,4,8,1]{3,2,1,0:T(8,128)(2,1)} %get-tuple-element.44), channel_id=1, source_target_pairs={{0,1},{1,2},{2,3},{3,4},{4,5},{5,6},{6,7},{8,9},{9,10},{10,11},{11... | collective-permute-start | bytes 968 | tf_op jit(solution)/shard_map/ppermute | solution.py:313
  45.8 13.1 %collective-permute-start.11 = (bf16[5,4,8,1]{3,2,1,0:T(8,128)(2,1)}, bf16[5,4,8,1]{3,2,1,0:T(8,128)(2,1)S(1)}, u32[]{:S(2)}, u32[]{:S(2)}) collective-permute-start(bf16[5,4,8,1]{3,2,1,0:T(8,128)(2,1)} %get-tuple-element.45), channel_id=1, source_target_pairs={{1,0},{2,1},{3,2},{4,3},{5,4},{6,5},{7,6},{9,8},{10,9},{11,10},{12... | collective-permute-start | bytes 968 | tf_op jit(solution)/shard_map/ppermute | solution.py:314
  47.7 14.4 %collective-permute-start.6 = (bf16[5,1,8,768]{3,2,1,0:T(8,128)(2,1)}, bf16[5,1,8,768]{3,2,1,0:T(8,128)(2,1)S(1)}, u32[]{:S(2)}, u32[]{:S(2)}) collective-permute-start(bf16[5,1,8,768]{3,2,1,0:T(8,128)(2,1)} %get-tuple-element.40), channel_id=1, source_target_pairs={{0,64},{64,128},{128,192},{192,256},{256,320},{320,384},{384,448},... | collective-permute-start | bytes 184328 | tf_op jit(solution)/shard_map/ppermute | solution.py:313
  52.4 9.7 %collective-permute-start.7 = (bf16[5,1,8,768]{3,2,1,0:T(8,128)(2,1)}, bf16[5,1,8,768]{3,2,1,0:T(8,128)(2,1)S(1)}, u32[]{:S(2)}, u32[]{:S(2)}) collective-permute-start(bf16[5,1,8,768]{3,2,1,0:T(8,128)(2,1)} %get-tuple-element.41), channel_id=1, source_target_pairs={{64,0},{128,64},{192,128},{256,192},{320,256},{384,320},{448,384},... | collective-permute-start | bytes 184328 | tf_op jit(solution)/shard_map/ppermute | solution.py:314
  53.7 5.3 %collective-permute-start.8 = (bf16[5,4,1,768]{3,2,1,0:T(2,128)(2,1)}, bf16[5,4,1,768]{3,2,1,0:T(2,128)(2,1)S(1)}, u32[]{:S(2)}, u32[]{:S(2)}) collective-permute-start(bf16[5,4,1,768]{3,2,1,0:T(2,128)(2,1)} %get-tuple-element.42), channel_id=1, source_target_pairs={{0,8},{8,16},{16,24},{24,32},{32,40},{40,48},{48,56},{1,9},{9,17},... | collective-permute-start | bytes 92168 | tf_op jit(solution)/shard_map/ppermute | solution.py:313
  56.8 5.4 %copy-start.11 = (bf16[5,4,8,1]{3,2,1,0:T(8,128)(2,1)}, bf16[5,4,8,1]{3,2,1,0:T(8,128)(2,1)S(1)}, u32[]{:S(2)}) copy-start(bf16[5,4,8,1]{3,2,1,0:T(8,128)(2,1)S(1)} %collective-permute-done.10.zlo) | copy-start | bytes 964
  56.8 5.3 %collective-permute-start.9 = (bf16[5,4,1,768]{3,2,1,0:T(2,128)(2,1)}, bf16[5,4,1,768]{3,2,1,0:T(2,128)(2,1)S(1)}, u32[]{:S(2)}, u32[]{:S(2)}) collective-permute-start(bf16[5,4,1,768]{3,2,1,0:T(2,128)(2,1)} %get-tuple-element.43), channel_id=1, source_target_pairs={{8,0},{16,8},{24,16},{32,24},{40,32},{48,40},{56,48},{9,1},{17,9},... | collective-permute-start | bytes 92168 | tf_op jit(solution)/shard_map/ppermute | solution.py:314
  58.9 3.2 %copy-start.12 = (bf16[5,4,8,1]{3,2,1,0:T(8,128)(2,1)}, bf16[5,4,8,1]{3,2,1,0:T(8,128)(2,1)S(1)}, u32[]{:S(2)}) copy-start(bf16[5,4,8,1]{3,2,1,0:T(8,128)(2,1)S(1)} %collective-permute-done.11.zhi) | copy-start | bytes 964
  58.9 3.2 %copy-start.6 = (bf16[5,4,1,768]{3,2,1,0:T(2,128)(2,1)}, bf16[5,4,1,768]{3,2,1,0:T(2,128)(2,1)S(1)}, u32[]{:S(2)}) copy-start(bf16[5,4,1,768]{3,2,1,0:T(2,128)(2,1)S(1)} %collective-permute-done.8.ylo) | copy-start | bytes 92164
  62.1 0.9 copy-start
  91.5 18.9 %all-to-all-start.2 = ((f32[8,1,64]{2,1,0:T(1,128)}), f32[8,1,64]{2,1,0:T(1,128)S(1)}, u32[]{:S(2)}, u32[]{:S(2)}) async-start(f32[8,1,64]{2,1,0:T(1,128)} %broadcast_in_dim.23), calls=%async_computation.2 | async-start | bytes 8192 | tf_op jit(solution)/shard_map/all_to_all | solution.py:345
  (6 other events, 3.9 us)

commit v10 on v9

--- a/solution.py
+++ b/solution.py
@@ -297,7 +297,6 @@
         ends = lax.axis_size(axis) - 1
         state_halo.append(lax.ppermute(high, axis, [(i, i + 1) for i in range(ends)]))
         state_halo.append(lax.ppermute(low, axis, [(i + 1, i) for i in range(ends)]))
-    packed, *state_halo = lax.optimization_barrier((packed, *state_halo))
     arrived = lax.all_to_all(packed, ("gy", "gz"), 0, 0, tiled=True)
     primal = pl.pallas_call(
         primal_kernel,

time: 113 us -> 113 us (level)
  waiting for transfers between devices: 10.5 us -> 12.9 us
  starting transfers between devices: 56.9 us -> 55.2 us
    ppermute x6, starting transfers between devices: 12.6 us -> 9.41 us  [shards(): lax.ppermute(low, axis, [(i + 1, i) for i in range(ends)])]
    ppermute x6, starting transfers between devices: 19.3 us -> 21.9 us  [shards(): lax.ppermute(high, axis, [(i, i + 1) for i in range(ends)])]
    ppermute x6, waiting for transfers between devices: 0.02 us -> 1.36 us  [shards(): lax.ppermute(high, axis, [(i, i + 1) for i in range(ends)])]
  transfers between devices with their start and end apart: 14 -> 14, of which waited for: 3 -> 4; matrix products, arithmetic and copies ran while one was open for 5% -> 2% of each run, Pallas kernels for 3% -> 4%
where the time goes in v10:
time: 113 us
  starting transfers between devices  55.2 us (49%)
  blocking collectives  21.9 us (19%)
  waiting for transfers between devices  12.9 us (11%)
  Pallas kernels  10.4 us (9%)
  local copies, waits for them, and re-layouts  6.54 us (6%)
  other arithmetic  4.25 us (4%)
  between operations  1.6 us (1%)
    ppermute x6, starting transfers between devices, shards(): lax.ppermute(high, axis, [(i, i + 1) for i in range(ends)])  21.9 us
    all_to_all x1, blocking collectives, shards(): level_one = lax.all_to_all(spread, ('gy', 'gz'), 0, 0, tiled=True)  21.9 us
    all_to_all x1, starting transfers between devices, shards(): lax.all_to_all(jnp.broadcast_to(level_one.reshape(1, plane), (across, pla...  12.1 us
    all_to_all x1, starting transfers between devices, shards(): arrived = lax.all_to_all(packed, ('gy', 'gz'), 0, 0, tiled=True)  11.8 us
    ppermute x6, starting transfers between devices, shards(): lax.ppermute(low, axis, [(i + 1, i) for i in range(ends)])  9.41 us
    ppermute x6, waiting for transfers between devices, shards(): lax.ppermute(low, axis, [(i + 1, i) for i in range(ends)])  6.61 us
    pallas_call x1, Pallas kernels, shards(): pl.pallas_call(adjoint_kernel, out_shape=[jax.ShapeDtypeStruct(state.shap...  5.62 us
    all_to_all x1, waiting for transfers between devices, shards(): lax.all_to_all(jnp.broadcast_to(level_one.reshape(1, plane), (across, pla...  4.88 us
  transfers between devices with their start and end apart: 14, of which 4 were waited for; matrix products, arithmetic and copies ran while one was open for 2% of the time, Pallas kernels for 4%

profile of v10, /device:TPU:1, one launch (start us, length us, event | category | flops | bytes accessed | tf_op | source)
XLA Modules:
  0.0 112.7 jit_solution(3122844923945290581)
XLA Ops:
  0.6 1.2 %copy.31 = bf16[128,5,2,2,128]{4,0,3,2,1:T(8,128)(2,1)S(1)} copy(bf16[128,5,2,2,128]{4,3,2,1,0:T(2,128)(2,1)} %param.14) | data formatting | bytes 1310720 | tf_op args[6]
  3.9 11.8 %all-to-all-start = ((bf16[128,21,128]{2,1,0:T(8,128)(2,1)}), bf16[128,21,128]{2,1,0:T(8,128)(2,1)S(1)}, u32[]{:S(2)}, u32[]{:S(2)}) async-start(bf16[128,21,128]{2,1,0:T(8,128)(2,1)} %pad_maximum_fusion), calls=%async_computation | async-start | bytes 1572864 | tf_op jit(solution)/shard_map/all_to_all | solution.py:300
  15.7 1.7 %shard_map.103 = (bf16[5,1,8,768]{3,2,1,0:T(8,128)(2,1)}, bf16[5,1,8,768]{3,2,1,0:T(8,128)(2,1)}, bf16[5,4,1,768]{3,2,1,0:T(2,128)(2,1)}, bf16[5,4,1,768]{3,2,1,...) custom-call(bf16[5,4,8,768]{3,2,1,0:T(8,128)(2,1)} %s_ref.5), custom_call_target="tpu_custom_call" | custom-call | tf_op jit(solution)/shard_map/pallas_call | solution.py:289
  17.3 4.0 %collective-permute-start = (bf16[5,1,8,768]{3,2,1,0:T(8,128)(2,1)}, bf16[5,1,8,768]{3,2,1,0:T(8,128)(2,1)S(1)}, u32[]{:S(2)}, u32[]{:S(2)}) collective-permute-start(bf16[5,1,8,768]{3,2,1,0:T(8,128)(2,1)} %get-tuple-element.20), channel_id=1, source_target_pairs={{0,64},{64,128},{128,192},{192,256},{256,320},{320,384},{384,448},... | collective-permute-start | bytes 184328 | tf_op jit(solution)/shard_map/ppermute | solution.py:298
  21.3 1.3 %collective-permute-start.1 = (bf16[5,1,8,768]{3,2,1,0:T(8,128)(2,1)}, bf16[5,1,8,768]{3,2,1,0:T(8,128)(2,1)S(1)}, u32[]{:S(2)}, u32[]{:S(2)}) collective-permute-start(bf16[5,1,8,768]{3,2,1,0:T(8,128)(2,1)} %get-tuple-element.21), channel_id=1, source_target_pairs={{64,0},{128,64},{192,128},{256,192},{320,256},{384,320},{448,384},... | collective-permute-start | bytes 184328 | tf_op jit(solution)/shard_map/ppermute | solution.py:299
  22.6 3.3 %collective-permute-start.2 = (bf16[5,4,1,768]{3,2,1,0:T(2,128)(2,1)}, bf16[5,4,1,768]{3,2,1,0:T(2,128)(2,1)S(1)}, u32[]{:S(2)}, u32[]{:S(2)}) collective-permute-start(bf16[5,4,1,768]{3,2,1,0:T(2,128)(2,1)} %get-tuple-element.22), channel_id=1, source_target_pairs={{0,8},{8,16},{16,24},{24,32},{32,40},{40,48},{48,56},{1,9},{9,17},... | collective-permute-start | bytes 92168 | tf_op jit(solution)/shard_map/ppermute | solution.py:298
  25.9 1.3 %collective-permute-start.3 = (bf16[5,4,1,768]{3,2,1,0:T(2,128)(2,1)}, bf16[5,4,1,768]{3,2,1,0:T(2,128)(2,1)S(1)}, u32[]{:S(2)}, u32[]{:S(2)}) collective-permute-start(bf16[5,4,1,768]{3,2,1,0:T(2,128)(2,1)} %get-tuple-element.23), channel_id=1, source_target_pairs={{8,0},{16,8},{24,16},{32,24},{40,32},{48,40},{56,48},{9,1},{17,9},... | collective-permute-start | bytes 92168 | tf_op jit(solution)/shard_map/ppermute | solution.py:299
  27.2 3.9 %collective-permute-start.4 = (bf16[5,4,8,1]{3,2,1,0:T(8,128)(2,1)}, bf16[5,4,8,1]{3,2,1,0:T(8,128)(2,1)S(1)}, u32[]{:S(2)}, u32[]{:S(2)}) collective-permute-start(bf16[5,4,8,1]{3,2,1,0:T(8,128)(2,1)} %get-tuple-element.24), channel_id=1, source_target_pairs={{0,1},{1,2},{2,3},{3,4},{4,5},{5,6},{6,7},{8,9},{9,10},{10,11},{11... | collective-permute-start | bytes 968 | tf_op jit(solution)/shard_map/ppermute | solution.py:298
  31.3 1.3 %collective-permute-done.4.zlo = bf16[5,4,8,1]{3,2,1,0:T(8,128)(2,1)S(1)} collective-permute-done((bf16[5,4,8,1]{3,2,1,0:T(8,128)(2,1)}, bf16[5,4,8,1]{3,2,1,0:T(8,128)(2,1)S(1)}, u32[]{:S(2)}, u32[]{:S(2)}) %collective-permute-start.4) | collective-permute-done | bytes 352 | tf_op jit(solution)/shard_map/ppermute | solution.py:298
  32.7 1.9 %collective-permute-start.5 = (bf16[5,4,8,1]{3,2,1,0:T(8,128)(2,1)}, bf16[5,4,8,1]{3,2,1,0:T(8,128)(2,1)S(1)}, u32[]{:S(2)}, u32[]{:S(2)}) collective-permute-start(bf16[5,4,8,1]{3,2,1,0:T(8,128)(2,1)} %get-tuple-element.25), channel_id=1, source_target_pairs={{1,0},{2,1},{3,2},{4,3},{5,4},{6,5},{7,6},{9,8},{10,9},{11,10},{12... | collective-permute-start | bytes 968 | tf_op jit(solution)/shard_map/ppermute | solution.py:299
  35.1 4.2 %collective-permute-done.5.zhi = bf16[5,4,8,1]{3,2,1,0:T(8,128)(2,1)S(1)} collective-permute-done((bf16[5,4,8,1]{3,2,1,0:T(8,128)(2,1)}, bf16[5,4,8,1]{3,2,1,0:T(8,128)(2,1)S(1)}, u32[]{:S(2)}, u32[]{:S(2)}) %collective-permute-start.5) | collective-permute-done | bytes 352 | tf_op jit(solution)/shard_map/ppermute | solution.py:299
  40.7 3.1 %shard_map.104 = (f32[5,4,8,768]{3,2,1,0:T(8,128)}, bf16[4,8,768]{2,1,0:T(8,128)(2,1)}, bf16[5,1,8,768]{3,2,1,0:T(8,128)(2,1)}, bf16[5,1,8,768]{3,2,1,0:T(8,128)...) custom-call(f32[5,5]{1,0:T(8,128)} %c_ref.3, ...), custom_call_target="tpu_custom_call" | custom-call | tf_op jit(solution)/shard_map/pallas_call | solution.py:301
  43.7 4.1 %collective-permute-start.6 = (bf16[5,1,8,768]{3,2,1,0:T(8,128)(2,1)}, bf16[5,1,8,768]{3,2,1,0:T(8,128)(2,1)S(1)}, u32[]{:S(2)}, u32[]{:S(2)}) collective-permute-start(bf16[5,1,8,768]{3,2,1,0:T(8,128)(2,1)} %get-tuple-element.27), channel_id=1, source_target_pairs={{0,64},{64,128},{128,192},{192,256},{256,320},{320,384},{384,448},... | collective-permute-start | bytes 184328 | tf_op jit(solution)/shard_map/ppermute | solution.py:312
  47.9 2.3 %collective-permute-start.10 = (bf16[5,4,8,1]{3,2,1,0:T(8,128)(2,1)}, bf16[5,4,8,1]{3,2,1,0:T(8,128)(2,1)S(1)}, u32[]{:S(2)}, u32[]{:S(2)}) collective-permute-start(bf16[5,4,8,1]{3,2,1,0:T(8,128)(2,1)} %get-tuple-element.31), channel_id=1, source_target_pairs={{0,1},{1,2},{2,3},{3,4},{4,5},{5,6},{6,7},{8,9},{9,10},{10,11},{11... | collective-permute-start | bytes 968 | tf_op jit(solution)/shard_map/ppermute | solution.py:312
  50.2 1.3 %collective-permute-start.7 = (bf16[5,1,8,768]{3,2,1,0:T(8,128)(2,1)}, bf16[5,1,8,768]{3,2,1,0:T(8,128)(2,1)S(1)}, u32[]{:S(2)}, u32[]{:S(2)}) collective-permute-start(bf16[5,1,8,768]{3,2,1,0:T(8,128)(2,1)} %get-tuple-element.28), channel_id=1, source_target_pairs={{64,0},{128,64},{192,128},{256,192},{320,256},{384,320},{448,384},... | collective-permute-start | bytes 184328 | tf_op jit(solution)/shard_map/ppermute | solution.py:313
  51.5 4.3 %collective-permute-start.8 = (bf16[5,4,1,768]{3,2,1,0:T(2,128)(2,1)}, bf16[5,4,1,768]{3,2,1,0:T(2,128)(2,1)S(1)}, u32[]{:S(2)}, u32[]{:S(2)}) collective-permute-start(bf16[5,4,1,768]{3,2,1,0:T(2,128)(2,1)} %get-tuple-element.29), channel_id=1, source_target_pairs={{0,8},{8,16},{16,24},{24,32},{32,40},{40,48},{48,56},{1,9},{9,17},... | collective-permute-start | bytes 92168 | tf_op jit(solution)/shard_map/ppermute | solution.py:312
  55.8 1.3 %collective-permute-start.9 = (bf16[5,4,1,768]{3,2,1,0:T(2,128)(2,1)}, bf16[5,4,1,768]{3,2,1,0:T(2,128)(2,1)S(1)}, u32[]{:S(2)}, u32[]{:S(2)}) collective-permute-start(bf16[5,4,1,768]{3,2,1,0:T(2,128)(2,1)} %get-tuple-element.30), channel_id=1, source_target_pairs={{8,0},{16,8},{24,16},{32,24},{40,32},{48,40},{56,48},{9,1},{17,9},... | collective-permute-start | bytes 92168 | tf_op jit(solution)/shard_map/ppermute | solution.py:313
  57.1 2.3 %collective-permute-start.11 = (bf16[5,4,8,1]{3,2,1,0:T(8,128)(2,1)}, bf16[5,4,8,1]{3,2,1,0:T(8,128)(2,1)S(1)}, u32[]{:S(2)}, u32[]{:S(2)}) collective-permute-start(bf16[5,4,8,1]{3,2,1,0:T(8,128)(2,1)} %get-tuple-element.32), channel_id=1, source_target_pairs={{1,0},{2,1},{3,2},{4,3},{5,4},{6,5},{7,6},{9,8},{10,9},{11,10},{12... | collective-permute-start | bytes 968 | tf_op jit(solution)/shard_map/ppermute | solution.py:313
  60.3 2.4 %collective-permute-done.11.zhi = bf16[5,4,8,1]{3,2,1,0:T(8,128)(2,1)S(1)} collective-permute-done((bf16[5,4,8,1]{3,2,1,0:T(8,128)(2,1)}, bf16[5,4,8,1]{3,2,1,0:T(8,128)(2,1)S(1)}, u32[]{:S(2)}, u32[]{:S(2)}) %collective-permute-start.11) | collective-permute-done | bytes 352 | tf_op jit(solution)/shard_map/ppermute | solution.py:313
  63.7 5.6 %shard_map.105 = (bf16[5,4,8,768]{3,2,1,0:T(8,128)(2,1)}, f32[2,8,768]{2,1,0:T(8,128)}, f32[64,1]{1,0:T(8,128)}) custom-call(f32[5,5]{1,0:T(8,128)} %c_ref.3, s32[48]{0:T(128)} %multiply_add_fusion.slot_ref, f32[5,4,8,768]{3,2,1,0:T(8,128)} %get-tuple-element.26.s1_ref, bf16[5,4,8,768]{3,2,1,0:T(8,128)(2,1)} %s_ref.5, bf16[4,8,768]{2,1,0:T(8,128)(2,1)} %d_ref.3, ...), custom_call_target="tpu_custom_call" | custom-call | tf_op jit(solution)/shard_map/pallas_call | solution.py:328
  69.3 21.9 %all_to_all.20 = f32[64,1,1]{2,1,0:T(1,128)S(1)} all-to-all(f32[64,1,1]{2,1,0:T(1,128)} %bitcast.9), channel_id=1, replica_groups=mesh['gx'=8,'gy'=8,'gz'=8] {'gy','gz'}, dimensions={0} | all-to-all | bytes 512 | tf_op jit(solution)/shard_map/all_to_all | solution.py:343
  92.3 12.1 %all-to-all-start.2 = ((f32[8,1,64]{2,1,0:T(1,128)}), f32[8,1,64]{2,1,0:T(1,128)S(1)}, u32[]{:S(2)}, u32[]{:S(2)}) async-start(f32[8,1,64]{2,1,0:T(1,128)} %broadcast_in_dim.23), calls=%async_computation.2 | async-start | bytes 8192 | tf_op jit(solution)/shard_map/all_to_all | solution.py:344
  106.0 4.9 %all-to-all-done.2 = f32[8,1,64]{2,1,0:T(1,128)S(1)} async-done(((f32[8,1,64]{2,1,0:T(1,128)}), f32[8,1,64]{2,1,0:T(1,128)S(1)}, u32[]{:S(2)}, u32[]{:S(2)}) %all-to-all-start.2) | async-done | bytes 2080 | tf_op jit(solution)/shard_map/all_to_all | solution.py:344
  111.5 1.2 %divide_minimum_fusion = (f32[48]{0:T(128)}, f32[48]{0:T(128)}) fusion(f32[]{:T(128)} %bitcast.5, f32[]{:T(128)} %reduce_sum.29, f32[48]{0:T(128)S(1)} %reshape.37, s32[48]{0:T(128)S(1)} %copy-done.14), kind=kLoop, calls=%fused_computation.5 | loop fusion | flops 384 | bytes 776 | tf_op jit(solution)/shard_map/min | solution.py:350
  (59 shorter events, 8.5 us)
Async XLA Ops:
  1.8 0.7 copy-start.13
  3.9 27.3 %copy-start.15 = (s32[48,1]{0,1:T(1,128)S(1)}, s32[48,1]{0,1:T(1,128)}, u32[]{:S(2)}) copy-start(s32[48,1]{0,1:T(1,128)} %param.11) | copy-start | bytes 580
  3.9 58.9 %all-to-all-start = ((bf16[128,21,128]{2,1,0:T(8,128)(2,1)}), bf16[128,21,128]{2,1,0:T(8,128)(2,1)S(1)}, u32[]{:S(2)}, u32[]{:S(2)}) async-start(bf16[128,21,128]{2,1,0:T(8,128)(2,1)} %pad_maximum_fusion), calls=%async_computation | async-start | bytes 1572864 | tf_op jit(solution)/shard_map/all_to_all | solution.py:300
  15.6 43.8 %copy-start.14 = (s32[48]{0:T(128)S(1)}, s32[48]{0:T(128)}, u32[]{:S(2)}) copy-start(s32[48]{0:T(128)} %param.12) | copy-start | bytes 580
  17.3 22.0 %collective-permute-start = (bf16[5,1,8,768]{3,2,1,0:T(8,128)(2,1)}, bf16[5,1,8,768]{3,2,1,0:T(8,128)(2,1)S(1)}, u32[]{:S(2)}, u32[]{:S(2)}) collective-permute-start(bf16[5,1,8,768]{3,2,1,0:T(8,128)(2,1)} %get-tuple-element.20), channel_id=1, source_target_pairs={{0,64},{64,128},{128,192},{192,256},{256,320},{320,384},{384,448},... | collective-permute-start | bytes 184328 | tf_op jit(solution)/shard_map/ppermute | solution.py:298
  21.3 18.1 %collective-permute-start.1 = (bf16[5,1,8,768]{3,2,1,0:T(8,128)(2,1)}, bf16[5,1,8,768]{3,2,1,0:T(8,128)(2,1)S(1)}, u32[]{:S(2)}, u32[]{:S(2)}) collective-permute-start(bf16[5,1,8,768]{3,2,1,0:T(8,128)(2,1)} %get-tuple-element.21), channel_id=1, source_target_pairs={{64,0},{128,64},{192,128},{256,192},{320,256},{384,320},{448,384},... | collective-permute-start | bytes 184328 | tf_op jit(solution)/shard_map/ppermute | solution.py:299
  22.6 16.7 %collective-permute-start.2 = (bf16[5,4,1,768]{3,2,1,0:T(2,128)(2,1)}, bf16[5,4,1,768]{3,2,1,0:T(2,128)(2,1)S(1)}, u32[]{:S(2)}, u32[]{:S(2)}) collective-permute-start(bf16[5,4,1,768]{3,2,1,0:T(2,128)(2,1)} %get-tuple-element.22), channel_id=1, source_target_pairs={{0,8},{8,16},{16,24},{24,32},{32,40},{40,48},{48,56},{1,9},{9,17},... | collective-permute-start | bytes 92168 | tf_op jit(solution)/shard_map/ppermute | solution.py:298
  25.9 13.4 %collective-permute-start.3 = (bf16[5,4,1,768]{3,2,1,0:T(2,128)(2,1)}, bf16[5,4,1,768]{3,2,1,0:T(2,128)(2,1)S(1)}, u32[]{:S(2)}, u32[]{:S(2)}) collective-permute-start(bf16[5,4,1,768]{3,2,1,0:T(2,128)(2,1)} %get-tuple-element.23), channel_id=1, source_target_pairs={{8,0},{16,8},{24,16},{32,24},{40,32},{48,40},{56,48},{9,1},{17,9},... | collective-permute-start | bytes 92168 | tf_op jit(solution)/shard_map/ppermute | solution.py:299
  27.2 5.4 %collective-permute-start.4 = (bf16[5,4,8,1]{3,2,1,0:T(8,128)(2,1)}, bf16[5,4,8,1]{3,2,1,0:T(8,128)(2,1)S(1)}, u32[]{:S(2)}, u32[]{:S(2)}) collective-permute-start(bf16[5,4,8,1]{3,2,1,0:T(8,128)(2,1)} %get-tuple-element.24), channel_id=1, source_target_pairs={{0,1},{1,2},{2,3},{3,4},{4,5},{5,6},{6,7},{8,9},{9,10},{10,11},{11... | collective-permute-start | bytes 968 | tf_op jit(solution)/shard_map/ppermute | solution.py:298
  32.7 6.7 %copy-start.9 = (bf16[5,4,8,1]{3,2,1,0:T(8,128)(2,1)}, bf16[5,4,8,1]{3,2,1,0:T(8,128)(2,1)S(1)}, u32[]{:S(2)}) copy-start(bf16[5,4,8,1]{3,2,1,0:T(8,128)(2,1)S(1)} %collective-permute-done.4.zlo) | copy-start | bytes 964
  32.7 6.7 %collective-permute-start.5 = (bf16[5,4,8,1]{3,2,1,0:T(8,128)(2,1)}, bf16[5,4,8,1]{3,2,1,0:T(8,128)(2,1)S(1)}, u32[]{:S(2)}, u32[]{:S(2)}) collective-permute-start(bf16[5,4,8,1]{3,2,1,0:T(8,128)(2,1)} %get-tuple-element.25), channel_id=1, source_target_pairs={{1,0},{2,1},{3,2},{4,3},{5,4},{6,5},{7,6},{9,8},{10,9},{11,10},{12... | collective-permute-start | bytes 968 | tf_op jit(solution)/shard_map/ppermute | solution.py:299
  39.4 0.7 copy-start.7
  39.4 0.7 copy-start.8
  39.4 0.7 copy-start.3
  43.7 19.0 %collective-permute-start.6 = (bf16[5,1,8,768]{3,2,1,0:T(8,128)(2,1)}, bf16[5,1,8,768]{3,2,1,0:T(8,128)(2,1)S(1)}, u32[]{:S(2)}, u32[]{:S(2)}) collective-permute-start(bf16[5,1,8,768]{3,2,1,0:T(8,128)(2,1)} %get-tuple-element.27), channel_id=1, source_target_pairs={{0,64},{64,128},{128,192},{192,256},{256,320},{320,384},{384,448},... | collective-permute-start | bytes 184328 | tf_op jit(solution)/shard_map/ppermute | solution.py:312
  47.9 9.3 %collective-permute-start.10 = (bf16[5,4,8,1]{3,2,1,0:T(8,128)(2,1)}, bf16[5,4,8,1]{3,2,1,0:T(8,128)(2,1)S(1)}, u32[]{:S(2)}, u32[]{:S(2)}) collective-permute-start(bf16[5,4,8,1]{3,2,1,0:T(8,128)(2,1)} %get-tuple-element.31), channel_id=1, source_target_pairs={{0,1},{1,2},{2,3},{3,4},{4,5},{5,6},{6,7},{8,9},{9,10},{10,11},{11... | collective-permute-start | bytes 968 | tf_op jit(solution)/shard_map/ppermute | solution.py:312
  50.2 12.6 %collective-permute-start.7 = (bf16[5,1,8,768]{3,2,1,0:T(8,128)(2,1)}, bf16[5,1,8,768]{3,2,1,0:T(8,128)(2,1)S(1)}, u32[]{:S(2)}, u32[]{:S(2)}) collective-permute-start(bf16[5,1,8,768]{3,2,1,0:T(8,128)(2,1)} %get-tuple-element.28), channel_id=1, source_target_pairs={{64,0},{128,64},{192,128},{256,192},{320,256},{384,320},{448,384},... | collective-permute-start | bytes 184328 | tf_op jit(solution)/shard_map/ppermute | solution.py:313
  51.5 11.2 %collective-permute-start.8 = (bf16[5,4,1,768]{3,2,1,0:T(2,128)(2,1)}, bf16[5,4,1,768]{3,2,1,0:T(2,128)(2,1)S(1)}, u32[]{:S(2)}, u32[]{:S(2)}) collective-permute-start(bf16[5,4,1,768]{3,2,1,0:T(2,128)(2,1)} %get-tuple-element.29), channel_id=1, source_target_pairs={{0,8},{8,16},{16,24},{24,32},{32,40},{40,48},{48,56},{1,9},{9,17},... | collective-permute-start | bytes 92168 | tf_op jit(solution)/shard_map/ppermute | solution.py:312
  55.8 6.9 %collective-permute-start.9 = (bf16[5,4,1,768]{3,2,1,0:T(2,128)(2,1)}, bf16[5,4,1,768]{3,2,1,0:T(2,128)(2,1)S(1)}, u32[]{:S(2)}, u32[]{:S(2)}) collective-permute-start(bf16[5,4,1,768]{3,2,1,0:T(2,128)(2,1)} %get-tuple-element.30), channel_id=1, source_target_pairs={{8,0},{16,8},{24,16},{32,24},{40,32},{48,40},{56,48},{9,1},{17,9},... | collective-permute-start | bytes 92168 | tf_op jit(solution)/shard_map/ppermute | solution.py:313
  57.1 5.6 %copy-start.11 = (bf16[5,4,8,1]{3,2,1,0:T(8,128)(2,1)}, bf16[5,4,8,1]{3,2,1,0:T(8,128)(2,1)S(1)}, u32[]{:S(2)}) copy-start(bf16[5,4,8,1]{3,2,1,0:T(8,128)(2,1)S(1)} %collective-permute-done.10.zlo) | copy-start | bytes 964
  57.1 5.5 %collective-permute-start.11 = (bf16[5,4,8,1]{3,2,1,0:T(8,128)(2,1)}, bf16[5,4,8,1]{3,2,1,0:T(8,128)(2,1)S(1)}, u32[]{:S(2)}, u32[]{:S(2)}) collective-permute-start(bf16[5,4,8,1]{3,2,1,0:T(8,128)(2,1)} %get-tuple-element.32), channel_id=1, source_target_pairs={{1,0},{2,1},{3,2},{4,3},{5,4},{6,5},{7,6},{9,8},{10,9},{11,10},{12... | collective-permute-start | bytes 968 | tf_op jit(solution)/shard_map/ppermute | solution.py:313
  62.7 0.7 copy-start.2
  62.8 0.9 copy-start
  92.3 18.6 %all-to-all-start.2 = ((f32[8,1,64]{2,1,0:T(1,128)}), f32[8,1,64]{2,1,0:T(1,128)S(1)}, u32[]{:S(2)}, u32[]{:S(2)}) async-start(f32[8,1,64]{2,1,0:T(1,128)} %broadcast_in_dim.23), calls=%async_computation.2 | async-start | bytes 8192 | tf_op jit(solution)/shard_map/all_to_all | solution.py:344
  (6 other events, 3.8 us)
